TPU v7x, 256 devices: a whole 4x4x8 slice. The times are simulated.
256 devices in a mesh: dp: 64 (over z, y, core), mp: 4 (over x).
Axes of the slice: x: 4, y: 4, z: 8, core: 2. Of those that a mesh axis runs over, the one named last changes fastest.
Arguments:
- tree_query: bfloat16 [8192, 2048], P('dp', 'mp'), may hold values from -6 to 6
- new_kv: bfloat16 [8192, 2, 512], P('dp', None, 'mp'), may hold values from -6 to 6
- kv_cache: bfloat16 [2560, 2, 128, 512], P('dp', None, None, 'mp'), may hold values from -4 to 4
- page_table: int32 [128, 32], P('dp'), may hold values from 0 to 39, as said below
- cache_len: int32 [128], P('dp'), may hold values from 2 to 4096, as said below
- tree_mask: int32 [128, 64, 64], P('dp'), may hold values from 0 to 1, as said below
- out_weight: bfloat16 [2048, 2048], P('mp'), may hold values from -0.5 to 0.5
- residual_in: bfloat16 [8192, 2048], P('dp'), may hold values from -3 to 3
- norm_gain: float32 [2048], replicated, may hold values from 0.25 to 1.75
- route_ids: int32 [8192, 6], P('dp'), may hold values from 0 to 63, all different within a row; in each aligned block of 128 rows (0 to 127, 128 to 255, ...) at most 16 rows name the same one
- route_weight: float32 [8192, 6], P('dp'), may hold values from 0.05 to 0.5
- w_gate: bfloat16 [64, 2048, 1408], P('dp', None, 'mp'), may hold values from -0.125 to 0.125
- w_up: bfloat16 [64, 2048, 1408], P('dp', None, 'mp'), may hold values from -0.125 to 0.125
- w_down: bfloat16 [64, 1408, 2048], P('dp', None, 'mp'), may hold values from -0.15625 to 0.15625
- shared_gate: bfloat16 [2048, 2816], P('dp', 'mp'), may hold values from -0.125 to 0.125
- shared_up: bfloat16 [2048, 2816], P('dp', 'mp'), may hold values from -0.125 to 0.125
- shared_down: bfloat16 [2816, 2048], P('mp', 'dp'), may hold values from -0.109375 to 0.109375
Outputs:
- layer_out: bfloat16 [8192, 2048], P('dp', 'mp')
Inputs may be any that keep to these rules, and one draw needn't show every extreme that they name: `route_ids`: each row names 6 different experts. Within the rows of one index of dp (aligned blocks of 128 rows) no expert is named by more than 16 rows, and in some block one expert is named by exactly 16 rows. `cache_len`: the pages of the requests of one index of dp number at most 40 together; some request has exactly 4096 cached positions. `page_table`: entry [r, j] is the slot, in the pool of the index of dp that holds request r, of the page with cache positions j * 128 to j * 128 + 127. Entries with j * 128 < cache_len[r] are distinct over the requests of one index of dp; the other entries are valid slots whose contents are not read. tree_mask[r, i, u] is 1 where tree node u is node i or an ancestor of it, else 0; node 0 is the root and each other node's parent has a smaller index.
All inputs are finite; a program needn't handle non-finite values.
Results may differ from a plain program's by a relative error of at most 0.009.
Values may be sent and summed in bfloat16 or wider, within the bound.
No kernel may reach another device: no remote copies, remote signals or barrier semaphores. Data moves between devices by JAX's collectives and lax.ppermute only.
A program may use at most 128 MiB of HBM per device.

v0:
```python
import jax
import jax.numpy as jnp
from jax import lax
from jax.sharding import PartitionSpec as P

NEGATIVE_FILL = -1e30
EPSILON = 1e-05


def normalize(rows, gain):
    values = rows.astype(jnp.float32)
    mean_square = jnp.mean(values * values, axis=-1, keepdims=True)
    return (values * lax.rsqrt(mean_square + EPSILON) * gain).astype(jnp.bfloat16)


def attend_requests(
    queries, tree_keys, tree_values, tree_allow, kv_cache, page_table, cache_len, score_scale
):

    def per_request(request_item):
        q_rows, own_keys, own_values, allow_rows, table_row, length = request_item
        kv_pages = kv_cache[table_row]
        cache_keys = kv_pages[:, 0].reshape(-1, kv_pages.shape[-1])
        cache_values = kv_pages[:, 1].reshape(-1, kv_pages.shape[-1])
        live_mask = (jnp.arange(cache_keys.shape[0], dtype=jnp.int32) < length)[None, :]
        cache_scores = (
            jnp.einsum("qd,kd->qk", q_rows, cache_keys, preferred_element_type=jnp.float32)
            * score_scale
        )
        cache_scores = jnp.where(live_mask, cache_scores, NEGATIVE_FILL)
        tree_scores = (
            jnp.einsum("qd,ud->qu", q_rows, own_keys, preferred_element_type=jnp.float32)
            * score_scale
        )
        tree_scores = jnp.where(allow_rows, tree_scores, NEGATIVE_FILL)
        row_peak = jnp.maximum(jnp.max(cache_scores, axis=1), jnp.max(tree_scores, axis=1))[:, None]
        cache_probs = jnp.where(live_mask, jnp.exp(cache_scores - row_peak), 0.0)
        tree_probs = jnp.where(allow_rows, jnp.exp(tree_scores - row_peak), 0.0)
        denom_sum = jnp.sum(cache_probs, axis=1) + jnp.sum(tree_probs, axis=1)
        weighted = jnp.dot(
            cache_probs.astype(jnp.bfloat16), cache_values, preferred_element_type=jnp.float32
        )
        weighted = weighted + jnp.dot(
            tree_probs.astype(jnp.bfloat16), own_values, preferred_element_type=jnp.float32
        )
        return (weighted / denom_sum[:, None]).astype(jnp.bfloat16)

    return lax.map(
        per_request, (queries, tree_keys, tree_values, tree_allow, page_table, cache_len)
    )


def run_experts(rows, w_gate, w_up, w_down):
    source_count, slot_count, model_width = rows.shape
    flat_rows = rows.reshape(source_count * slot_count, model_width)
    gate_proj = jnp.dot(flat_rows, w_gate[0], preferred_element_type=jnp.float32)
    up_proj = jnp.dot(flat_rows, w_up[0], preferred_element_type=jnp.float32)
    hidden_act = (jax.nn.silu(gate_proj) * up_proj).astype(jnp.bfloat16)
    down_rows = w_down[0]
    summed = jnp.dot(
        lax.all_gather(hidden_act, "mp", axis=1, tiled=True),
        down_rows,
        preferred_element_type=jnp.float32,
    )
    outputs = summed.astype(jnp.bfloat16).reshape(source_count, slot_count, w_down.shape[2])
    return lax.all_to_all(outputs, "dp", split_axis=0, concat_axis=0, tiled=True)


def shared_experts(normed_rows, shared_gate, shared_up, shared_down):
    gate_total = jnp.dot(
        normed_rows,
        lax.all_gather(shared_gate, "dp", axis=0, tiled=True),
        preferred_element_type=jnp.float32,
    )
    up_total = jnp.dot(
        normed_rows,
        lax.all_gather(shared_up, "dp", axis=0, tiled=True),
        preferred_element_type=jnp.float32,
    )
    shared_hidden = (jax.nn.silu(gate_total) * up_total).astype(jnp.bfloat16)
    terms = jnp.dot(
        shared_hidden,
        lax.all_gather(shared_down, "dp", axis=1, tiled=True),
        preferred_element_type=jnp.float32,
    )
    return lax.psum_scatter(terms.astype(jnp.bfloat16), "mp", scatter_dimension=1, tiled=True)


def on_device(
    tree_query,
    new_kv,
    kv_cache,
    page_table,
    cache_len,
    tree_mask,
    out_weight,
    residual_in,
    norm_gain,
    route_ids,
    route_weight,
    w_gate,
    w_up,
    w_down,
    shared_gate,
    shared_up,
    shared_down,
):
    tok_rows = tree_query.shape[0]
    req_count = cache_len.shape[0]
    tree_len = tree_mask.shape[1]
    head_width = new_kv.shape[2]
    local_heads = tree_query.shape[1] // head_width
    score_scale = head_width ** (-0.5)
    queries = tree_query.reshape(req_count, tree_len, local_heads, head_width)
    queries = queries.transpose(0, 2, 1, 3).reshape(req_count, local_heads * tree_len, head_width)
    tree_keys = new_kv[:, 0, :].reshape(req_count, tree_len, head_width)
    tree_values = new_kv[:, 1, :].reshape(req_count, tree_len, head_width)
    tree_allow = jnp.tile(tree_mask, (1, local_heads, 1)) == 1
    attended = attend_requests(
        queries, tree_keys, tree_values, tree_allow, kv_cache, page_table, cache_len, score_scale
    )
    attended = attended.reshape(req_count, local_heads, tree_len, head_width).transpose(0, 2, 1, 3)
    attended = attended.reshape(tok_rows, local_heads * head_width)
    partial_value = jnp.dot(attended, out_weight, preferred_element_type=jnp.float32)
    model_width = residual_in.shape[1]
    quarter = model_width // lax.axis_size("mp")
    col_start = lax.axis_index("mp") * quarter
    experts = lax.axis_size("dp") * w_gate.shape[0]
    route_count = route_ids.shape[1]
    capacity = min(tok_rows, 4 * tok_rows * route_count // (3 * experts))
    expert_ids = route_ids.reshape(-1)
    onehot = (expert_ids[:, None] == jnp.arange(experts, dtype=jnp.int32)[None, :]).astype(
        jnp.int32
    )
    slot_index = jnp.sum((jnp.cumsum(onehot, axis=0) - onehot) * onehot, axis=1)
    sources = jnp.arange(expert_ids.shape[0], dtype=jnp.int32) // route_count
    summed_heads = lax.psum(partial_value, "mp")
    stream = (residual_in.astype(jnp.float32) + summed_heads).astype(jnp.bfloat16)
    own_stream = lax.dynamic_slice_in_dim(stream, col_start, quarter, 1)
    normed_rows = normalize(stream, norm_gain)
    buffer = jnp.zeros((experts, capacity, normed_rows.shape[1]), jnp.bfloat16)
    results = run_experts(
        lax.all_to_all(
            buffer.at[expert_ids, slot_index].set(normed_rows[sources]),
            "dp",
            split_axis=0,
            concat_axis=0,
            tiled=True,
        ),
        w_gate,
        w_up,
        w_down,
    )
    shared_out = shared_experts(normed_rows, shared_gate, shared_up, shared_down)
    result_rows = results.reshape(experts * capacity, quarter)
    picked = (
        result_rows[expert_ids * capacity + slot_index]
        .reshape(tok_rows, route_count, quarter)
        .astype(jnp.float32)
    )
    mixture = jnp.einsum("tk,tkc->tc", route_weight, picked, precision=lax.Precision.HIGHEST)
    return (own_stream.astype(jnp.float32) + shared_out.astype(jnp.float32) + mixture).astype(
        jnp.bfloat16
    )


def solution(mesh):
    return jax.shard_map(
        on_device,
        mesh=mesh,
        in_specs=(
            P("dp", "mp"),
            P("dp", None, "mp"),
            P("dp", None, None, "mp"),
            P("dp", None),
            P("dp"),
            P("dp", None, None),
            P("mp", None),
            P("dp", None),
            P(),
            P("dp", None),
            P("dp", None),
            P("dp", None, "mp"),
            P("dp", None, "mp"),
            P("dp", None, "mp"),
            P("dp", "mp"),
            P("dp", "mp"),
            P("mp", "dp"),
        ),
        out_specs=P("dp", "mp"),
        check_vma=False,
    )
```

profile of v0, /device:TPU:32, one launch (start us, length us, event | category | flops | bytes accessed | tf_op | source)
XLA Modules:
  0.0 658.8 jit_solution(10278691214841616985)
XLA Ops:
  6.5 1.1 fusion.66
  7.7 0.9 reshape.211
  8.7 0.9 broadcast_compare_fusion
  9.5 0.1 copy.21
  9.6 0.1 tile.2
  9.7 0.2 eq.37
  9.9 21.6 %while.10 = (s32[]{:T(128)}, bf16[2,256,128]{2,1,0:T(8,128)(2,1)S(1)}, s32[2]{0:T(128)}, bf16[2,256,128]{2,1,0:T(8,128)(2,1)S(1)}, s32[2,32]{1,0:T(2,128)}, /*in...) while((s32[]{:T(128)}, ...), condition=%wide.region_5.6_spmd, body=%wide.region_0.5_spmd.sunk | while | flops 554947200 | bytes 23845564 | solution.py:48
  9.9 0.7 fusion.100
  10.6 3.9 gather_fusion
  14.5 1.7 fusion.101
  16.2 0.7 dynamic_slice.79
  16.9 0.7 iota_compare_fusion.4
  17.6 0.8 fusion.102
  18.4 0.2 fusion.103
  18.6 0.9 fusion.105
  19.6 0.9 fusion.104
  20.5 0.2 fusion.107
  20.7 0.7 fusion.100
  21.4 3.9 gather_fusion
  25.3 1.7 fusion.101
  27.0 0.7 dynamic_slice.79
  27.7 0.7 iota_compare_fusion.4
  28.4 0.8 fusion.102
  29.2 0.2 fusion.103
  29.4 0.9 fusion.105
  30.4 0.9 fusion.104
  31.3 0.2 fusion.107
  31.5 0.1 copy.24
  31.7 1.5 fusion.55
  33.2 0.0 all-gather.11.cloned.1.call-start
  33.2 0.1 copy.25
  33.3 0.1 eq.42
  33.5 0.1 eq.38
  33.6 0.1 reshape.215
  33.8 1.8 reduce-window.6
  35.6 0.3 slice_reduce_fusion
  35.9 0.1 fusion.52
  36.1 50.8 %all-reduce.2.cloned.1.call-done = f32[128,2048]{1,0:T(8,128)} async-done(((f32[128,2048]{1,0:T(8,128)}), f32[128,2048]{1,0:T(8,128)}) %all-reduce.2.cloned.1.call-update) | async-done | bytes 1048592 | tf_op jit(solution)/shard_map/psum | solution.py:137
  86.9 1.5 fusion.41
  88.4 0.8 copy-done.1
  89.2 0.2 fusion.43
  89.3 4.3 gather_fusion.1
  93.6 2.4 broadcast_in_dim.47
  96.1 137.8 %scatter_fusion = bf16[64,16,2048]{2,1,0:T(8,128)(2,1)} fusion(bf16[64,16,2048]{2,1,0:T(8,128)(2,1)} %broadcast_in_dim.47, s32[768]{0:T(1024)S(1)} %get-tuple-element.54, bf16[768,2048]{1,0:T(8,128)(2,1)} %gather_fusion.1), kind=kCustom, calls=%fused_computation.3 | custom fusion | bytes 9443328 | tf_op jit(solution)/shard_map/scatter | solution.py:144
  233.9 105.9 %all_to_all.10 = bf16[64,16,2048]{2,1,0:T(8,128)(2,1)S(1)} all-to-all(bf16[64,16,2048]{2,1,0:T(8,128)(2,1)} %scatter_fusion), channel_id=1, replica_groups=mesh['dp'=64,'mp'=4] {'dp'}, dimensions={0} | all-to-all | bytes 8388608 | tf_op jit(solution)/shard_map/all_to_all | solution.py:143
  339.8 1.8 fusion.35
  341.6 2.7 fusion.37
  344.4 0.7 all-gather.5.cloned.1.call-update
  345.1 0.5 all-gather.7.cloned.1.call-update
  345.7 0.5 all-gather.9.cloned.1.call-update
  346.3 34.8 %all-gather.11.cloned.1.call-done = bf16[1024,1408]{0,1:T(8,128)(2,1)} async-done(((bf16[1024,352]{0,1:T(8,128)(2,1)}), bf16[1024,1408]{0,1:T(8,128)(2,1)}) %all-gather.11.cloned.1.call-update) | async-done | bytes 2883600 | tf_op jit(solution)/shard_map/all_gather | solution.py:61
  381.1 5.1 convolution_convert_fusion.1
  386.2 10.7 %all-to-all-start.1 = ((bf16[64,16,512]{2,1,0:T(8,128)(2,1)}), bf16[64,16,512]{2,1,0:T(8,128)(2,1)}, u32[]{:S(2)}, u32[]{:S(2)}) async-start(bf16[64,16,512]{2,1,0:T(8,128)(2,1)} %bitcast.139), calls=%async_computation.2 | async-start | bytes 2097152 | tf_op jit(solution)/shard_map/all_to_all | solution.py:66
  396.9 66.3 %all-gather.5.cloned.1.call-done = bf16[2048,704]{1,0:T(8,128)(2,1)} async-done(((bf16[32,704]{1,0:T(8,128)(2,1)}), bf16[2048,704]{1,0:T(8,128)(2,1)}) %all-gather.5.cloned.1.call-update) | async-done | bytes 2883600 | tf_op jit(solution)/shard_map/all_gather | solution.py:72
  463.2 3.2 fusion.67
  466.4 75.6 %all-gather.7.cloned.1.call-done = bf16[2048,704]{1,0:T(8,128)(2,1)} async-done(((bf16[32,704]{1,0:T(8,128)(2,1)}), bf16[2048,704]{1,0:T(8,128)(2,1)}) %all-gather.7.cloned.1.call-update) | async-done | bytes 2883600 | tf_op jit(solution)/shard_map/all_gather | solution.py:77
  542.0 78.8 %all-gather.9.cloned.1.call-done = bf16[704,2048]{0,1:T(8,128)(2,1)} async-done(((bf16[704,32]{0,1:T(8,128)(2,1)}), bf16[704,2048]{0,1:T(8,128)(2,1)}) %all-gather.9.cloned.1.call-update) | async-done | bytes 2883600 | tf_op jit(solution)/shard_map/all_gather | solution.py:83
  620.8 7.0 %convolution_convert_fusion = bf16[128,2048]{1,0:T(8,128)(2,1)} fusion(bf16[704,2048]{0,1:T(8,128)(2,1)} %all-gather.9.cloned.1.call-done, bf16[128,2048]{1,0:T(8,128)(2,1)S(1)} %fusion.43, bf16[2048,704]{1,0:T(8,128)(2,1)} %all-gather.7.cloned.1.call-done, f32[128,704]{0,1:T(8,128)S(1)} %fusion.67), kind=kOutput, calls=%fused_computation.44 | convolution fusion | flops 739000320 | bytes 7176192 | tf_op jit(solution)/shard_map/dot_general | solution.py:81
  627.9 0.1 copy.29
  628.0 4.7 gather_fusion.2
  632.7 1.3 reshape.220
  634.1 1.0 fusion.68
  635.1 15.2 %reduce-scatter.2.cloned.1.call-done = bf16[128,512]{1,0:T(8,128)(2,1)} async-done(((bf16[128,2048]{1,0:T(8,128)(2,1)}), bf16[128,512]{1,0:T(8,128)(2,1)}) %reduce-scatter.2.cloned.1.call-update) | async-done | bytes 131088 | tf_op jit(solution)/shard_map/reduce_scatter | solution.py:86
  650.3 1.7 fusion.49
  (47 shorter events, 0.5 us)
Async XLA Ops:
  6.5 25.1 %copy-start = (bf16[512,2048]{1,0:T(8,128)(2,1)S(1)}, bf16[512,2048]{1,0:T(8,128)(2,1)}, u32[]{:S(2)}) copy-start(bf16[512,2048]{1,0:T(8,128)(2,1)} %param.25) | copy-start | bytes 6291460
  6.5 80.3 %all-reduce.2.cloned.1.call-start = ((), (), s32[]{:S(2)}) async-start(), calls=%async_computation.3 | async-start | bytes 2097152 | tf_op jit(solution)/shard_map/psum | solution.py:137
  14.5 1.7 copy-start.8
  25.3 1.7 copy-start.8
  31.5 1.7 copy-start.4
  31.5 55.4 %copy-start.2 = (bf16[128,2048]{1,0:T(8,128)(2,1)S(1)}, bf16[128,2048]{1,0:T(8,128)(2,1)}, u32[]{:S(2)}) copy-start(bf16[128,2048]{1,0:T(8,128)(2,1)} %param.26) | copy-start | bytes 1572868
  31.6 57.5 %copy-start.3 = (f32[2048]{0:T(1024)S(1)}, f32[2048]{0:T(1024)}, u32[]{:S(2)}) copy-start(f32[2048]{0:T(1024)} %param.27) | copy-start | bytes 24580
  33.2 347.9 %all-gather.11.cloned.1.call-start = ((), (), s32[]{:S(2)}) async-start(), calls=%async_computation.8 | async-start | bytes 3604480 | tf_op jit(solution)/shard_map/all_gather | solution.py:61
  88.3 0.8 copy-start.1
  233.9 105.9 %copy-start.6 = (bf16[1,2048,352]{1,2,0:T(8,128)(2,1)S(1)}, bf16[1,2048,352]{1,2,0:T(8,128)(2,1)}, u32[]{:S(2)}) copy-start(bf16[1,2048,352]{1,2,0:T(8,128)(2,1)} %param.30) | copy-start | bytes 4325380
  339.8 1.8 copy-start.7
  344.4 118.9 %all-gather.5.cloned.1.call-start = ((), (), s32[]{:S(2)}) async-start(), calls=%async_computation.4 | async-start | bytes 3194880 | tf_op jit(solution)/shard_map/all_gather | solution.py:72
  345.1 196.9 %all-gather.7.cloned.1.call-start = ((), (), s32[]{:S(2)}) async-start(), calls=%async_computation.5 | async-start | bytes 3194880 | tf_op jit(solution)/shard_map/all_gather | solution.py:77
  345.7 275.2 %all-gather.9.cloned.1.call-start = ((), (), s32[]{:S(2)}) async-start(), calls=%async_computation.6 | async-start | bytes 3194880 | tf_op jit(solution)/shard_map/all_gather | solution.py:83
  386.2 241.8 %all-to-all-start.1 = ((bf16[64,16,512]{2,1,0:T(8,128)(2,1)}), bf16[64,16,512]{2,1,0:T(8,128)(2,1)}, u32[]{:S(2)}, u32[]{:S(2)}) async-start(bf16[64,16,512]{2,1,0:T(8,128)(2,1)} %bitcast.139), calls=%async_computation.2 | async-start | bytes 2097152 | tf_op jit(solution)/shard_map/all_to_all | solution.py:66
  396.9 253.4 %reduce-scatter.2.cloned.1.call-start = ((), (), s32[]{:S(2)}) async-start(), calls=%async_computation.7 | async-start | bytes 655360 | tf_op jit(solution)/shard_map/reduce_scatter | solution.py:86
  466.4 161.4 %copy-start.5 = (f32[128,6]{0,1:T(8,128)S(1)}, f32[128,6]{0,1:T(8,128)}, u32[]{:S(2)}) copy-start(f32[128,6]{0,1:T(8,128)} %param.29) | copy-start | bytes 9220
Sparse Core Ops, SparseCore 0:
  33.3 53.5 all-reduce.1
  344.5 36.5 all-gather.10
  384.2 78.9 all-gather.4
  466.2 75.7 all-gather.6
  545.0 75.7 all-gather.8
  628.0 22.2 reduce-scatter.1
where the time goes:
time: 663 us; the launch traced here: 659 us
  waiting for transfers between devices  323 us (49%)
  local copies, waits for them, and re-layouts  167 us (25%)
  blocking collectives  106 us (16%)
  matrix products  26.5 us (4%)
  between operations  13.7 us (2%)
  starting transfers between devices  10.9 us (2%)
  other arithmetic  10.9 us (2%)
    scatter x1, local copies, waits for them, and re-layouts, on_device(): buffer.at[expert_ids, slot_index].set(normed_rows[sources])  138 us
    all_to_all x1, blocking collectives, on_device(): lax.all_to_all(buffer.at[expert_ids, slot_index].set(normed_rows[sources]...  106 us
    all_gather x1, waiting for transfers between devices, shared_experts(): lax.all_gather(shared_down, 'dp', axis=1, tiled=True)  78.8 us
    all_gather x1, waiting for transfers between devices, shared_experts(): lax.all_gather(shared_up, 'dp', axis=0, tiled=True)  75.6 us
    all_gather x1, waiting for transfers between devices, shared_experts(): lax.all_gather(shared_gate, 'dp', axis=0, tiled=True)  66.3 us
    psum x1, waiting for transfers between devices, on_device(): summed_heads = lax.psum(partial_value, 'mp')  50.8 us
    all_gather x1, waiting for transfers between devices, run_experts(): lax.all_gather(hidden_act, 'mp', axis=1, tiled=True)  34.8 us
    reduce_scatter x1, waiting for transfers between devices, shared_experts(): lax.psum_scatter(terms.astype(jnp.bfloat16), 'mp', scatter_dimension=1, t...  15.2 us
  transfers between devices with their start and end apart: 7, of which 6 were waited for; matrix products, arithmetic and copies ran while one was open for 4% of the time, Pallas kernels for 0%

commit v1 on v0

--- a/solution.py
+++ b/solution.py
@@ -50,6 +50,24 @@
     )
 
 
+def gather_mp(block, axis):
+    parts = lax.axis_size("mp")
+    copies = jnp.broadcast_to(block[None], (parts,) + block.shape)
+    pieces = lax.all_to_all(copies, "mp", split_axis=0, concat_axis=0, tiled=True)
+    pieces = jnp.moveaxis(pieces, 0, axis)
+    shape = list(block.shape)
+    shape[axis] = shape[axis] * parts
+    return pieces.reshape(shape)
+
+
+def scatter_sum_mp(terms):
+    parts = lax.axis_size("mp")
+    rows, width = terms.shape
+    blocks = terms.reshape(rows, parts, width // parts).transpose(1, 0, 2)
+    pieces = lax.all_to_all(blocks, "mp", split_axis=0, concat_axis=0, tiled=True)
+    return jnp.sum(pieces.astype(jnp.float32), axis=0)
+
+
 def run_experts(rows, w_gate, w_up, w_down):
     source_count, slot_count, model_width = rows.shape
     flat_rows = rows.reshape(source_count * slot_count, model_width)
@@ -58,7 +76,7 @@
     hidden_act = (jax.nn.silu(gate_proj) * up_proj).astype(jnp.bfloat16)
     down_rows = w_down[0]
     summed = jnp.dot(
-        lax.all_gather(hidden_act, "mp", axis=1, tiled=True),
+        gather_mp(hidden_act, 1),
         down_rows,
         preferred_element_type=jnp.float32,
     )
@@ -83,7 +101,7 @@
         lax.all_gather(shared_down, "dp", axis=1, tiled=True),
         preferred_element_type=jnp.float32,
     )
-    return lax.psum_scatter(terms.astype(jnp.bfloat16), "mp", scatter_dimension=1, tiled=True)
+    return scatter_sum_mp(terms.astype(jnp.bfloat16))
 
 
 def on_device(
@@ -133,15 +151,18 @@
         jnp.int32
     )
     slot_index = jnp.sum((jnp.cumsum(onehot, axis=0) - onehot) * onehot, axis=1)
-    sources = jnp.arange(expert_ids.shape[0], dtype=jnp.int32) // route_count
-    summed_heads = lax.psum(partial_value, "mp")
-    stream = (residual_in.astype(jnp.float32) + summed_heads).astype(jnp.bfloat16)
-    own_stream = lax.dynamic_slice_in_dim(stream, col_start, quarter, 1)
+    own_residual = lax.dynamic_slice_in_dim(residual_in, col_start, quarter, 1)
+    own_stream = (own_residual.astype(jnp.float32) + scatter_sum_mp(partial_value)).astype(jnp.bfloat16)
+    stream = gather_mp(own_stream, 1)
     normed_rows = normalize(stream, norm_gain)
-    buffer = jnp.zeros((experts, capacity, normed_rows.shape[1]), jnp.bfloat16)
+    codes = (expert_ids * capacity + slot_index).reshape(tok_rows, route_count)
+    slots = jnp.arange(experts * capacity, dtype=jnp.int32)
+    placing = jnp.any(codes[None, :, :] == slots[:, None, None], axis=2).astype(jnp.bfloat16)
+    buffer = jnp.dot(placing, normed_rows, preferred_element_type=jnp.float32).astype(jnp.bfloat16)
+    buffer = buffer.reshape(experts, capacity, normed_rows.shape[1])
     results = run_experts(
         lax.all_to_all(
-            buffer.at[expert_ids, slot_index].set(normed_rows[sources]),
+            buffer,
             "dp",
             split_axis=0,
             concat_axis=0,

time: 663 us -> 336 us (0.51)
  local copies, waits for them, and re-layouts: 167 us -> 26.5 us
  waiting for transfers between devices: 323 us -> 211 us
  blocking collectives: 106 us -> 0 us
  starting transfers between devices: 10.9 us -> 36.3 us
  matrix products: 26.5 us -> 33.6 us
    scatter x1 -> x0, local copies, waits for them, and re-layouts: 138 us -> none  [on_device(): buffer.at[expert_ids, slot_index].set(normed_rows[sources])]
    all_to_all x0 -> x5, waiting for transfers between devices: none -> 128 us  [the longest x1 104 us: on_device(): lax.all_to_all(buffer, 'dp', split_axis=0, concat_axis=0, tiled=True)]
    all_to_all x1 -> x0, blocking collectives: 106 us -> none  [on_device(): lax.all_to_all(buffer.at[expert_ids, slot_index].set(normed_rows[sources]...]
    all_gather x1, waiting for transfers between devices: 75.6 us -> 0.02 us  [shared_experts(): lax.all_gather(shared_up, 'dp', axis=0, tiled=True)]
    all_gather x1, waiting for transfers between devices: 66.3 us -> 0.02 us  [shared_experts(): lax.all_gather(shared_gate, 'dp', axis=0, tiled=True)]
    psum x1 -> x0, waiting for transfers between devices: 50.8 us -> none  [on_device(): summed_heads = lax.psum(partial_value, 'mp')]
    all_gather x1 -> x0, waiting for transfers between devices: 34.8 us -> none  [run_experts(): lax.all_gather(hidden_act, 'mp', axis=1, tiled=True)]
    all_to_all x0 -> x5, starting transfers between devices: none -> 28.6 us  [the longest x1 12 us: on_device(): lax.all_to_all(buffer, 'dp', split_axis=0, concat_axis=0, tiled=True)]
  transfers between devices with their start and end apart: 7 -> 9, of which waited for: 6 -> 6; matrix products, arithmetic and copies ran while one was open for 4% -> 19% of each run, Pallas kernels for 0% -> 0%
where the time goes in v1:
time: 336 us; the launch traced here: 333 us
  waiting for transfers between devices  211 us (63%)
  starting transfers between devices  36.3 us (11%)
  matrix products  33.6 us (10%)
  local copies, waits for them, and re-layouts  26.5 us (8%)
  between operations  13.4 us (4%)
  other arithmetic  12 us (4%)
    all_to_all x1, waiting for transfers between devices, on_device(): lax.all_to_all(buffer, 'dp', split_axis=0, concat_axis=0, tiled=True)  104 us
    all_gather x1, waiting for transfers between devices, shared_experts(): lax.all_gather(shared_down, 'dp', axis=1, tiled=True)  54.1 us
    all_to_all x1, waiting for transfers between devices, run_experts(): lax.all_to_all(outputs, 'dp', split_axis=0, concat_axis=0, tiled=True)  26.9 us
    all_to_all x2, waiting for transfers between devices, scatter_sum_mp(): lax.all_to_all(blocks, 'mp', split_axis=0, concat_axis=0, tiled=True)  17.1 us
    all_to_all x1, starting transfers between devices, on_device(): lax.all_to_all(buffer, 'dp', split_axis=0, concat_axis=0, tiled=True)  12 us
    all_to_all x2, starting transfers between devices, scatter_sum_mp(): lax.all_to_all(blocks, 'mp', split_axis=0, concat_axis=0, tiled=True)  8.55 us
    all_to_all x2, starting transfers between devices, gather_mp(): lax.all_to_all(copies, 'mp', split_axis=0, concat_axis=0, tiled=True)  8.07 us
    all_to_all x2, waiting for transfers between devices, gather_mp(): lax.all_to_all(copies, 'mp', split_axis=0, concat_axis=0, tiled=True)  7.65 us
  transfers between devices with their start and end apart: 9, of which 6 were waited for; matrix products, arithmetic and copies ran while one was open for 19% of the time, Pallas kernels for 0%

profile of v1, /device:TPU:32, one launch (start us, length us, event | category | flops | bytes accessed | tf_op | source)
XLA Modules:
  0.0 333.5 jit_solution(15534831628222421942)
XLA Ops:
  6.5 0.7 all-gather.4.cloned.1.call-update
  7.3 1.0 fusion.61
  8.3 0.6 copy.63
  8.9 0.6 copy.64
  9.5 0.9 reshape.149
  10.5 0.7 copy.47
  11.2 0.8 broadcast_compare_fusion
  12.2 0.8 eq.50
  13.0 18.3 %while.10 = (s32[]{:T(128)}, bf16[2,256,128]{2,1,0:T(8,128)(2,1)}, s32[2]{0:T(128)}, bf16[2,256,128]{2,1,0:T(8,128)(2,1)}, s32[2,32]{1,0:T(2,128)}, /*index=5*/b...) while((s32[]{:T(128)}, bf16[2,256,128]{2,1,0:T(8,128)(2,1)}, ...), condition=%wide.region_5.6_spmd, body=%wide.region_0.5_spmd.sunk | while | flops 554947200 | bytes 25811812 | solution.py:48
  13.0 0.7 fusion.98
  13.7 2.7 gather_fusion
  16.6 0.4 copy-done.11
  17.0 0.6 dynamic_slice.79
  17.6 0.6 iota_compare_fusion.5
  18.3 0.8 fusion.100
  19.3 0.9 fusion.103
  20.3 0.9 fusion.102
  21.5 0.6 copy-done.5
  22.1 0.7 fusion.98
  22.8 2.7 gather_fusion
  25.7 0.4 copy-done.11
  26.2 0.6 dynamic_slice.79
  26.8 0.6 iota_compare_fusion.5
  27.4 0.8 fusion.100
  28.5 0.9 fusion.103
  29.4 0.9 fusion.102
  30.6 0.6 copy-done.5
  31.2 1.0 copy.51
  32.3 0.7 reshape.178
  33.0 2.9 copy.62
  35.8 2.7 convolution_bitcast_fusion
  38.5 4.3 %all-to-all-start = ((f32[4,128,512]{2,1,0:T(8,128)}), f32[4,128,512]{2,1,0:T(8,128)S(1)}, u32[]{:S(2)}, u32[]{:S(2)}) async-start(f32[4,128,512]{2,1,0:T(8,128)} %convolution_bitcast_fusion), calls=%async_computation | async-start | bytes 2097152 | tf_op jit(solution)/shard_map/all_to_all | solution.py:67
  42.8 0.7 all-gather.6.cloned.1.call-update
  44.0 1.8 reduce-window.6
  45.8 0.3 slice_reduce_fusion
  46.1 11.8 %all-to-all-done = f32[4,128,512]{2,1,0:T(8,128)S(1)} async-done(((f32[4,128,512]{2,1,0:T(8,128)}), f32[4,128,512]{2,1,0:T(8,128)S(1)}, u32[]{:S(2)}, u32[]{:S(2)}) %all-to-all-start) | async-done | bytes 1048608 | tf_op jit(solution)/shard_map/all_to_all | solution.py:67
  58.0 0.9 add_convert_fusion
  59.1 0.9 broadcast_in_dim.54
  59.9 3.5 %all-to-all-start.1 = ((bf16[4,128,512]{1,2,0:T(8,128)(2,1)}), bf16[4,128,512]{1,2,0:T(8,128)(2,1)S(1)}, u32[]{:S(2)}, u32[]{:S(2)}) async-start(bf16[4,128,512]{1,2,0:T(8,128)(2,1)} %broadcast_in_dim.54), calls=%async_computation.1 | async-start | bytes 1048576 | tf_op jit(solution)/shard_map/all_to_all | solution.py:56
  63.8 0.5 fusion.33
  64.3 7.6 %all-to-all-done.1 = bf16[4,128,512]{1,2,0:T(8,128)(2,1)S(1)} async-done(((bf16[4,128,512]{1,2,0:T(8,128)(2,1)}), bf16[4,128,512]{1,2,0:T(8,128)(2,1)S(1)}, u32[]{:S(2)}, u32[]{:S(2)}) %all-to-all-start.1) | async-done | bytes 524320 | tf_op jit(solution)/shard_map/all_to_all | solution.py:56
  72.0 0.3 multiply_reduce_fusion
  72.3 0.3 fusion.43
  72.6 3.2 convolution_convert_fusion
  75.8 12.0 %all-to-all-start.3 = ((bf16[64,16,2048]{2,1,0:T(8,128)(2,1)}), bf16[64,16,2048]{2,1,0:T(8,128)(2,1)}, u32[]{:S(2)}, u32[]{:S(2)}) async-start(bf16[64,16,2048]{2,1,0:T(8,128)(2,1)} %bitcast.159), calls=%async_computation.3 | async-start | bytes 8388608 | tf_op jit(solution)/shard_map/all_to_all | solution.py:164
  88.0 0.5 all-gather.8.cloned.1.call-update
  88.5 103.7 %all-to-all-done.3 = bf16[64,16,2048]{2,1,0:T(8,128)(2,1)} async-done(((bf16[64,16,2048]{2,1,0:T(8,128)(2,1)}), bf16[64,16,2048]{2,1,0:T(8,128)(2,1)}, u32[]{:S(2)}, u32[]{:S(2)}) %all-to-all-start.3) | async-done | bytes 4194336 | tf_op jit(solution)/shard_map/all_to_all | solution.py:164
  192.3 4.4 %fusion.36 = f32[1024,352]{0,1:T(8,128)S(1)} fusion(bf16[1024,2048]{1,0:T(8,128)(2,1)} %bitcast.24, bf16[1,2048,352]{1,2,0:T(8,128)(2,1)} %param.30), kind=kOutput, calls=%fused_computation.50 | convolution fusion | flops 1476395008 | bytes 7077888 | tf_op jit(solution)/shard_map/dot_general | solution.py:74
  196.7 4.0 %fusion.38 = bf16[1024,352]{0,1:T(8,128)(2,1)S(1)} fusion(bf16[1024,2048]{1,0:T(8,128)(2,1)} %bitcast.24, bf16[1,2048,352]{1,2,0:T(8,128)(2,1)S(1)} %copy-done.10, f32[1024,352]{0,1:T(8,128)S(1)} %fusion.36), kind=kOutput, calls=%fused_computation.52 | convolution fusion | flops 1478557696 | bytes 7798784 | tf_op jit(solution)/shard_map/dot_general | solution.py:75
  200.7 2.0 broadcast_in_dim.55
  202.7 4.6 %all-to-all-start.4 = ((bf16[4,1024,352]{1,2,0:T(8,128)(2,1)}), bf16[4,1024,352]{1,2,0:T(8,128)(2,1)}, u32[]{:S(2)}, u32[]{:S(2)}) async-start(bf16[4,1024,352]{1,2,0:T(8,128)(2,1)} %broadcast_in_dim.55), calls=%async_computation.4 | async-start | bytes 5767168 | tf_op jit(solution)/shard_map/all_to_all | solution.py:56
  207.4 3.2 fusion.62
  210.6 54.1 %all-gather.8.cloned.1.call-done = bf16[704,2048]{0,1:T(8,128)(2,1)} async-done(((bf16[704,32]{0,1:T(8,128)(2,1)}), bf16[704,2048]{0,1:T(8,128)(2,1)}) %all-gather.8.cloned.1.call-update) | async-done | bytes 2883600 | tf_op jit(solution)/shard_map/all_gather | solution.py:101
  264.7 6.2 %convolution_convert_fusion.1 = bf16[128,2048]{1,0:T(8,128)(2,1)S(1)} fusion(bf16[704,2048]{0,1:T(8,128)(2,1)} %all-gather.8.cloned.1.call-done, bf16[128,2048]{0,1:T(8,128)(2,1)S(1)} %fusion.43, bf16[2048,704]{1,0:T(8,128)(2,1)} %all-gather.6.cloned.1.call-done, f32[128,704]{0,1:T(8,128)S(1)} %fusion.62), kind=kOutput, calls=%fused_computation.45 | convolution fusion | flops 739000320 | bytes 7176192 | tf_op jit(solution)/shard_map/dot_general | solution.py:99
  270.9 0.9 copy.70
  271.8 4.3 %all-to-all-start.2 = ((bf16[4,128,512]{2,1,0:T(8,128)(2,1)}), bf16[4,128,512]{2,1,0:T(8,128)(2,1)S(1)}, u32[]{:S(2)}, u32[]{:S(2)}) async-start(bf16[4,128,512]{2,1,0:T(8,128)(2,1)} %bitcast.126), calls=%async_computation.2 | async-start | bytes 1048576 | tf_op jit(solution)/shard_map/all_to_all | solution.py:67
  276.0 4.6 %convolution_convert_fusion.2 = bf16[1024,512]{1,0:T(8,128)(2,1)} fusion(bf16[1024,1408]{0,1:T(8,128)(2,1)} %bitcast.28, bf16[1,1408,512]{2,1,0:T(8,128)(2,1)S(1)} %copy-done), kind=kOutput, calls=%fused_computation.46 | convolution fusion | flops 1476919296 | bytes 5373952 | tf_op jit(solution)/shard_map/dot_general | solution.py:78
  280.7 5.3 %all-to-all-done.2 = bf16[4,128,512]{2,1,0:T(8,128)(2,1)S(1)} async-done(((bf16[4,128,512]{2,1,0:T(8,128)(2,1)}), bf16[4,128,512]{2,1,0:T(8,128)(2,1)S(1)}, u32[]{:S(2)}, u32[]{:S(2)}) %all-to-all-start.2) | async-done | bytes 524320 | tf_op jit(solution)/shard_map/all_to_all | solution.py:67
  285.9 7.5 %all-to-all-start.5 = ((bf16[64,16,512]{2,1,0:T(8,128)(2,1)}), bf16[64,16,512]{2,1,0:T(8,128)(2,1)S(1)}, u32[]{:S(2)}, u32[]{:S(2)}) async-start(bf16[64,16,512]{2,1,0:T(8,128)(2,1)} %bitcast.163), calls=%async_computation.5 | async-start | bytes 2097152 | tf_op jit(solution)/shard_map/all_to_all | solution.py:84
  293.7 0.8 convert_reduce_fusion
  294.5 26.9 %all-to-all-done.5 = bf16[64,16,512]{2,1,0:T(8,128)(2,1)S(1)} async-done(((bf16[64,16,512]{2,1,0:T(8,128)(2,1)}), bf16[64,16,512]{2,1,0:T(8,128)(2,1)S(1)}, u32[]{:S(2)}, u32[]{:S(2)}) %all-to-all-start.5) | async-done | bytes 1048608 | tf_op jit(solution)/shard_map/all_to_all | solution.py:84
  321.4 2.7 gather_fusion.1
  324.3 1.0 fusion.63
  325.3 1.7 fusion.49
  (74 shorter events, 3.3 us)
Async XLA Ops:
  6.5 269.5 %copy-start = (bf16[1,1408,512]{2,1,0:T(8,128)(2,1)S(1)}, bf16[1,1408,512]{2,1,0:T(8,128)(2,1)}, u32[]{:S(2)}) copy-start(bf16[1,1408,512]{2,1,0:T(8,128)(2,1)} %param.32) | copy-start | bytes 4325380
  6.5 200.8 %all-gather.4.cloned.1.call-start = ((), (), s32[]{:S(2)}) async-start(), calls=%async_computation.6 | async-start | bytes 3194880 | tf_op jit(solution)/shard_map/all_gather | solution.py:90
  16.4 0.7 copy-start.11
  16.4 1.9 copy-start.1
  16.6 2.6 copy-start.2
  16.6 2.6 copy-start.3
  20.2 1.0 copy-start.4
  20.3 1.0 copy-start.6
  21.4 0.7 copy-start.5
  25.5 0.7 copy-start.11
  25.5 1.9 copy-start.1
  25.7 2.6 copy-start.2
  25.7 2.6 copy-start.3
  29.4 1.0 copy-start.4
  29.4 1.0 copy-start.6
  30.6 0.7 copy-start.5
  35.8 7.8 %copy-start.8 = (s32[128,6]{0,1:T(8,128)S(1)}, s32[128,6]{0,1:T(8,128)}, u32[]{:S(2)}) copy-start(s32[128,6]{0,1:T(8,128)} %param.28) | copy-start | bytes 9220
  38.5 19.4 %all-to-all-start = ((f32[4,128,512]{2,1,0:T(8,128)}), f32[4,128,512]{2,1,0:T(8,128)S(1)}, u32[]{:S(2)}, u32[]{:S(2)}) async-start(f32[4,128,512]{2,1,0:T(8,128)} %convolution_bitcast_fusion), calls=%async_computation | async-start | bytes 2097152 | tf_op jit(solution)/shard_map/all_to_all | solution.py:67
  42.8 29.4 %copy-start.7 = (f32[2048]{0:T(1024)S(1)}, f32[2048]{0:T(1024)}, u32[]{:S(2)}) copy-start(f32[2048]{0:T(1024)} %param.27) | copy-start | bytes 24580
  42.8 167.7 %all-gather.6.cloned.1.call-start = ((), (), s32[]{:S(2)}) async-start(), calls=%async_computation.7 | async-start | bytes 3194880 | tf_op jit(solution)/shard_map/all_gather | solution.py:95
  59.9 12.0 %all-to-all-start.1 = ((bf16[4,128,512]{1,2,0:T(8,128)(2,1)}), bf16[4,128,512]{1,2,0:T(8,128)(2,1)S(1)}, u32[]{:S(2)}, u32[]{:S(2)}) async-start(bf16[4,128,512]{1,2,0:T(8,128)(2,1)} %broadcast_in_dim.54), calls=%async_computation.1 | async-start | bytes 1048576 | tf_op jit(solution)/shard_map/all_to_all | solution.py:56
  75.8 116.5 %all-to-all-start.3 = ((bf16[64,16,2048]{2,1,0:T(8,128)(2,1)}), bf16[64,16,2048]{2,1,0:T(8,128)(2,1)}, u32[]{:S(2)}, u32[]{:S(2)}) async-start(bf16[64,16,2048]{2,1,0:T(8,128)(2,1)} %bitcast.159), calls=%async_computation.3 | async-start | bytes 8388608 | tf_op jit(solution)/shard_map/all_to_all | solution.py:164
  87.8 176.9 %all-gather.8.cloned.1.call-start = ((), (), s32[]{:S(2)}) async-start(), calls=%async_computation.8 | async-start | bytes 3194880 | tf_op jit(solution)/shard_map/all_gather | solution.py:101
  192.3 4.4 %copy-start.10 = (bf16[1,2048,352]{1,2,0:T(8,128)(2,1)S(1)}, bf16[1,2048,352]{1,2,0:T(8,128)(2,1)}, u32[]{:S(2)}) copy-start(bf16[1,2048,352]{1,2,0:T(8,128)(2,1)} %param.31) | copy-start | bytes 4325380
  202.7 69.1 %all-to-all-start.4 = ((bf16[4,1024,352]{1,2,0:T(8,128)(2,1)}), bf16[4,1024,352]{1,2,0:T(8,128)(2,1)}, u32[]{:S(2)}, u32[]{:S(2)}) async-start(bf16[4,1024,352]{1,2,0:T(8,128)(2,1)} %broadcast_in_dim.55), calls=%async_computation.4 | async-start | bytes 5767168 | tf_op jit(solution)/shard_map/all_to_all | solution.py:56
  271.8 14.2 %all-to-all-start.2 = ((bf16[4,128,512]{2,1,0:T(8,128)(2,1)}), bf16[4,128,512]{2,1,0:T(8,128)(2,1)S(1)}, u32[]{:S(2)}, u32[]{:S(2)}) async-start(bf16[4,128,512]{2,1,0:T(8,128)(2,1)} %bitcast.126), calls=%async_computation.2 | async-start | bytes 1048576 | tf_op jit(solution)/shard_map/all_to_all | solution.py:67
  276.0 17.5 %copy-start.9 = (f32[128,6]{0,1:T(8,128)S(1)}, f32[128,6]{0,1:T(8,128)}, u32[]{:S(2)}) copy-start(f32[128,6]{0,1:T(8,128)} %param.29) | copy-start | bytes 9220
  285.9 35.4 %all-to-all-start.5 = ((bf16[64,16,512]{2,1,0:T(8,128)(2,1)}), bf16[64,16,512]{2,1,0:T(8,128)(2,1)S(1)}, u32[]{:S(2)}, u32[]{:S(2)}) async-start(bf16[64,16,512]{2,1,0:T(8,128)(2,1)} %bitcast.163), calls=%async_computation.5 | async-start | bytes 2097152 | tf_op jit(solution)/shard_map/all_to_all | solution.py:84
Sparse Core Ops, SparseCore 0:
  10.1 80.1 all-gather.3
  93.0 89.9 all-gather.5
  185.8 78.8 all-gather.7

commit v2 on v1

--- a/solution.py
+++ b/solution.py
@@ -85,20 +85,20 @@
 
 
 def shared_experts(normed_rows, shared_gate, shared_up, shared_down):
+    hidden_width = shared_gate.shape[1]
+    packed = jnp.concatenate([shared_gate, shared_up, shared_down.T], axis=1)
+    gathered = lax.all_gather(packed, "dp", axis=0, tiled=True)
     gate_total = jnp.dot(
-        normed_rows,
-        lax.all_gather(shared_gate, "dp", axis=0, tiled=True),
-        preferred_element_type=jnp.float32,
+        normed_rows, gathered[:, :hidden_width], preferred_element_type=jnp.float32
     )
     up_total = jnp.dot(
-        normed_rows,
-        lax.all_gather(shared_up, "dp", axis=0, tiled=True),
-        preferred_element_type=jnp.float32,
+        normed_rows, gathered[:, hidden_width : 2 * hidden_width], preferred_element_type=jnp.float32
     )
     shared_hidden = (jax.nn.silu(gate_total) * up_total).astype(jnp.bfloat16)
-    terms = jnp.dot(
+    terms = jnp.einsum(
+        "th,dh->td",
         shared_hidden,
-        lax.all_gather(shared_down, "dp", axis=1, tiled=True),
+        gathered[:, 2 * hidden_width :],
         preferred_element_type=jnp.float32,
     )
     return scatter_sum_mp(terms.astype(jnp.bfloat16))

time: 336 us -> 288 us (0.86)
  waiting for transfers between devices: 211 us -> 40.1 us
  blocking collectives: 0 us -> 148 us
  starting transfers between devices: 36.3 us -> 18.5 us
  matrix products: 33.6 us -> 27.8 us
    all_to_all x0 -> x2, blocking collectives: none -> 148 us  [the longest x1 110 us: on_device(): lax.all_to_all(buffer, 'dp', split_axis=0, concat_axis=0, tiled=True)]
    all_to_all x1 -> x0, waiting for transfers between devices: 104 us -> none  [on_device(): lax.all_to_all(buffer, 'dp', split_axis=0, concat_axis=0, tiled=True)]
    all_gather x3 -> x1, waiting for transfers between devices: 54.2 us -> 0.02 us  [shared_experts(): gathered = lax.all_gather(packed, 'dp', axis=0, tiled=True)]
    all_to_all x1, waiting for transfers between devices: 26.9 us -> 13.8 us  [run_experts(): lax.all_to_all(outputs, 'dp', split_axis=0, concat_axis=0, tiled=True)]
    all_to_all x1 -> x0, starting transfers between devices: 12 us -> none  [on_device(): lax.all_to_all(buffer, 'dp', split_axis=0, concat_axis=0, tiled=True)]
    all_to_all x2 -> x1, starting transfers between devices: 8.07 us -> 3.48 us  [gather_mp(): lax.all_to_all(copies, 'mp', split_axis=0, concat_axis=0, tiled=True)]
    all_to_all x2 -> x1, waiting for transfers between devices: 7.65 us -> 7.61 us  [gather_mp(): lax.all_to_all(copies, 'mp', split_axis=0, concat_axis=0, tiled=True)]
  transfers between devices with their start and end apart: 9 -> 5, of which waited for: 6 -> 4; matrix products, arithmetic and copies ran while one was open for 19% -> 21% of each run, Pallas kernels for 0% -> 0%
where the time goes in v2:
time: 288 us; the launch traced here: 287 us
  blocking collectives  148 us (51%)
  waiting for transfers between devices  40.1 us (14%)
  matrix products  27.8 us (10%)
  local copies, waits for them, and re-layouts  27.5 us (10%)
  starting transfers between devices  18.5 us (6%)
  between operations  13.7 us (5%)
  other arithmetic  11.3 us (4%)
    all_to_all x1, blocking collectives, on_device(): lax.all_to_all(buffer, 'dp', split_axis=0, concat_axis=0, tiled=True)  110 us
    all_to_all x1, blocking collectives, gather_mp(): lax.all_to_all(copies, 'mp', split_axis=0, concat_axis=0, tiled=True)  37.8 us
    all_to_all x2, waiting for transfers between devices, scatter_sum_mp(): lax.all_to_all(blocks, 'mp', split_axis=0, concat_axis=0, tiled=True)  18.7 us
    all_to_all x1, waiting for transfers between devices, run_experts(): lax.all_to_all(outputs, 'dp', split_axis=0, concat_axis=0, tiled=True)  13.8 us
    all_to_all x2, starting transfers between devices, scatter_sum_mp(): lax.all_to_all(blocks, 'mp', split_axis=0, concat_axis=0, tiled=True)  8.43 us
    dot_general x1, matrix products, shared_experts(): jnp.einsum('th,dh->td', shared_hidden, gathered[:, 2 * hidden_width:], pr...  8.17 us
    all_to_all x1, waiting for transfers between devices, gather_mp(): lax.all_to_all(copies, 'mp', split_axis=0, concat_axis=0, tiled=True)  7.61 us
    all_to_all x1, starting transfers between devices, run_experts(): lax.all_to_all(outputs, 'dp', split_axis=0, concat_axis=0, tiled=True)  6.54 us
  transfers between devices with their start and end apart: 5, of which 4 were waited for; matrix products, arithmetic and copies ran while one was open for 21% of the time, Pallas kernels for 0%

profile of v2, /device:TPU:32, one launch (start us, length us, event | category | flops | bytes accessed | tf_op | source)
XLA Modules:
  0.0 286.7 jit_solution(7963905776582777550)
XLA Ops:
  6.5 1.7 concatenate.3
  8.3 1.0 fusion.77
  9.3 0.6 copy.63
  9.9 0.6 copy.64
  10.5 0.9 reshape.149
  11.5 0.7 copy.47
  12.1 0.8 broadcast_compare_fusion
  13.2 0.8 eq.50
  14.0 18.0 %while.10 = (s32[]{:T(128)}, bf16[2,256,128]{2,1,0:T(8,128)(2,1)}, s32[2]{0:T(128)}, bf16[2,256,128]{2,1,0:T(8,128)(2,1)}, s32[2,32]{1,0:T(2,128)}, /*index=5*/b...) while((s32[]{:T(128)}, bf16[2,256,128]{2,1,0:T(8,128)(2,1)}, ...), condition=%wide.region_5.6_spmd, body=%wide.region_0.5_spmd.sunk | while | flops 554947200 | bytes 25811812 | solution.py:48
  14.0 0.7 fusion.110
  14.6 2.7 gather_fusion
  17.6 0.4 copy-done.12
  18.0 0.5 dynamic_slice.79
  18.6 0.5 iota_compare_fusion.5
  19.1 0.8 fusion.112
  20.2 0.9 fusion.115
  21.1 0.9 fusion.114
  22.0 0.2 fusion.117
  22.3 0.6 copy-done.5
  22.9 0.7 fusion.110
  23.6 2.7 gather_fusion
  26.4 0.2 fusion.111
  26.6 0.4 copy-done.12
  27.0 0.5 dynamic_slice.79
  27.6 0.5 iota_compare_fusion.5
  28.2 0.8 fusion.112
  29.2 0.9 fusion.115
  30.2 0.9 fusion.114
  31.1 0.2 fusion.117
  31.3 0.6 copy-done.5
  32.0 1.0 copy.51
  33.0 0.7 reshape.178
  33.7 2.9 %copy.62 = bf16[2048,512]{1,0:T(8,128)(2,1)S(1)} copy(bf16[2048,512]{0,1:T(8,128)(2,1)} %bitcast.163) | data formatting | bytes 4194304 | tf_op jit(solution)/shard_map/dot_general | solution.py:142
  36.6 2.8 convolution_bitcast_fusion
  39.3 4.3 %all-to-all-start = ((f32[4,128,512]{2,1,0:T(8,128)}), f32[4,128,512]{2,1,0:T(8,128)S(1)}, u32[]{:S(2)}, u32[]{:S(2)}) async-start(f32[4,128,512]{2,1,0:T(8,128)} %convolution_bitcast_fusion), calls=%async_computation | async-start | bytes 2097152 | tf_op jit(solution)/shard_map/all_to_all | solution.py:67
  44.1 1.8 reduce-window.6
  45.9 0.3 slice_reduce_fusion
  46.2 12.5 %all-to-all-done = f32[4,128,512]{2,1,0:T(8,128)S(1)} async-done(((f32[4,128,512]{2,1,0:T(8,128)}), f32[4,128,512]{2,1,0:T(8,128)S(1)}, u32[]{:S(2)}, u32[]{:S(2)}) %all-to-all-start) | async-done | bytes 1048608 | tf_op jit(solution)/shard_map/all_to_all | solution.py:67
  58.8 0.9 add_convert_fusion
  59.9 0.9 broadcast_in_dim.54
  60.8 3.5 %all-to-all-start.1 = ((bf16[4,128,512]{1,2,0:T(8,128)(2,1)}), bf16[4,128,512]{1,2,0:T(8,128)(2,1)S(1)}, u32[]{:S(2)}, u32[]{:S(2)}) async-start(bf16[4,128,512]{1,2,0:T(8,128)(2,1)} %broadcast_in_dim.54), calls=%async_computation.1 | async-start | bytes 1048576 | tf_op jit(solution)/shard_map/all_to_all | solution.py:56
  64.6 0.5 fusion.39
  65.2 7.6 %all-to-all-done.1 = bf16[4,128,512]{1,2,0:T(8,128)(2,1)S(1)} async-done(((bf16[4,128,512]{1,2,0:T(8,128)(2,1)}), bf16[4,128,512]{1,2,0:T(8,128)(2,1)S(1)}, u32[]{:S(2)}, u32[]{:S(2)}) %all-to-all-start.1) | async-done | bytes 524320 | tf_op jit(solution)/shard_map/all_to_all | solution.py:56
  72.8 0.3 multiply_reduce_fusion
  73.1 0.3 fusion.59
  73.4 1.3 convolution_convert_fusion
  74.7 109.8 %all_to_all.30 = bf16[64,16,2048]{2,1,0:T(8,128)(2,1)S(1)} all-to-all(bf16[64,16,2048]{2,1,0:T(8,128)(2,1)S(1)} %bitcast.157), channel_id=1, replica_groups=mesh['dp'=64,'mp'=4] {'dp'}, dimensions={0} | all-to-all | bytes 8388608 | tf_op jit(solution)/shard_map/all_to_all | solution.py:164
  184.5 1.8 fusion.45
  186.2 1.8 fusion.47
  188.1 0.4 broadcast_in_dim.55
  188.5 37.8 %all_to_all.31 = bf16[4,1024,352]{1,2,0:T(8,128)(2,1)S(1)} all-to-all(bf16[4,1024,352]{1,2,0:T(8,128)(2,1)S(1)} %broadcast_in_dim.55), channel_id=1, replica_groups=mesh['dp'=64,'mp'=4] {'mp'}, dimensions={0} | all-to-all | bytes 5767168 | tf_op jit(solution)/shard_map/all_to_all | solution.py:56
  226.2 2.9 %convolution_convert_fusion.1 = bf16[1024,512]{1,0:T(8,128)(2,1)} fusion(bf16[1024,1408]{0,1:T(8,128)(2,1)S(1)} %bitcast.162, bf16[1,1408,512]{2,1,0:T(8,128)(2,1)S(1)} %copy-done), kind=kOutput, calls=%fused_computation.52 | convolution fusion | flops 1476919296 | bytes 5373952 | tf_op jit(solution)/shard_map/dot_general | solution.py:78
  229.1 6.5 %all-to-all-start.5 = ((bf16[64,16,512]{2,1,0:T(8,128)(2,1)}), bf16[64,16,512]{2,1,0:T(8,128)(2,1)S(1)}, u32[]{:S(2)}, u32[]{:S(2)}) async-start(bf16[64,16,512]{2,1,0:T(8,128)(2,1)} %bitcast.164), calls=%async_computation.5 | async-start | bytes 2097152 | tf_op jit(solution)/shard_map/all_to_all | solution.py:84
  235.8 3.9 %fusion.37 = f32[128,704]{0,1:T(8,128)} fusion(bf16[128,2048]{0,1:T(8,128)(2,1)S(1)} %fusion.59, bf16[2048,2112]{1,0:T(8,128)(2,1)} %all-gather.2.cloned.1.call-done), kind=kOutput, calls=%fused_computation.47 | convolution fusion | flops 369098752 | bytes 4030464 | tf_op jit(solution)/shard_map/dot_general | solution.py:91
  239.8 8.2 %fusion.40 = bf16[128,2048]{1,0:T(8,128)(2,1)} fusion(bf16[2048,2112]{1,0:T(8,128)(2,1)} %all-gather.2.cloned.1.call-done, bf16[128,2048]{0,1:T(8,128)(2,1)S(1)} %fusion.59, f32[128,704]{0,1:T(8,128)} %fusion.37), kind=kOutput, calls=%fused_computation.51 | convolution fusion | flops 739000320 | bytes 7700480 | tf_op jit(solution)/shard_map/th,dh->td/dot_general | solution.py:98
  247.9 1.9 copy.70
  249.8 13.8 %all-to-all-done.5 = bf16[64,16,512]{2,1,0:T(8,128)(2,1)S(1)} async-done(((bf16[64,16,512]{2,1,0:T(8,128)(2,1)}), bf16[64,16,512]{2,1,0:T(8,128)(2,1)S(1)}, u32[]{:S(2)}, u32[]{:S(2)}) %all-to-all-start.5) | async-done | bytes 1048608 | tf_op jit(solution)/shard_map/all_to_all | solution.py:84
  263.6 4.1 %all-to-all-start.2 = ((bf16[4,128,512]{2,1,0:T(8,128)(2,1)}), bf16[4,128,512]{2,1,0:T(8,128)(2,1)}, u32[]{:S(2)}, u32[]{:S(2)}) async-start(bf16[4,128,512]{2,1,0:T(8,128)(2,1)} %bitcast.124), calls=%async_computation.2 | async-start | bytes 1048576 | tf_op jit(solution)/shard_map/all_to_all | solution.py:67
  267.9 2.7 gather_fusion.1
  270.6 0.3 reshape.160
  270.8 1.0 fusion.78
  271.8 6.1 %all-to-all-done.2 = bf16[4,128,512]{2,1,0:T(8,128)(2,1)} async-done(((bf16[4,128,512]{2,1,0:T(8,128)(2,1)}), bf16[4,128,512]{2,1,0:T(8,128)(2,1)}, u32[]{:S(2)}, u32[]{:S(2)}) %all-to-all-start.2) | async-done | bytes 524320 | tf_op jit(solution)/shard_map/all_to_all | solution.py:67
  278.0 1.1 convert_reduce_fusion
  279.1 0.7 fusion.65
  (69 shorter events, 2.2 us)
Async XLA Ops:
  6.5 219.7 %copy-start = (bf16[1,1408,512]{2,1,0:T(8,128)(2,1)S(1)}, bf16[1,1408,512]{2,1,0:T(8,128)(2,1)}, u32[]{:S(2)}) copy-start(bf16[1,1408,512]{2,1,0:T(8,128)(2,1)} %param.32) | copy-start | bytes 4325380
  6.5 229.3 %all-gather.2.cloned.1.call-start = ((), (), s32[]{:S(2)}) async-start(), calls=%async_computation.6 | async-start | bytes 9052160 | tf_op jit(solution)/shard_map/all_gather | solution.py:90
  17.3 0.7 copy-start.12
  17.4 1.8 copy-start.1
  17.6 2.4 copy-start.2
  17.6 2.4 copy-start.3
  21.1 1.0 copy-start.4
  21.1 1.0 copy-start.6
  22.3 0.7 copy-start.5
  26.4 0.7 copy-start.12
  26.4 1.8 copy-start.1
  26.6 2.4 copy-start.2
  26.6 2.4 copy-start.3
  30.1 1.0 copy-start.4
  30.1 1.0 copy-start.6
  31.3 0.7 copy-start.5
  36.6 7.1 %copy-start.8 = (s32[128,6]{0,1:T(8,128)S(1)}, s32[128,6]{0,1:T(8,128)}, u32[]{:S(2)}) copy-start(s32[128,6]{0,1:T(8,128)} %param.28) | copy-start | bytes 9220
  39.3 19.4 %all-to-all-start = ((f32[4,128,512]{2,1,0:T(8,128)}), f32[4,128,512]{2,1,0:T(8,128)S(1)}, u32[]{:S(2)}, u32[]{:S(2)}) async-start(f32[4,128,512]{2,1,0:T(8,128)} %convolution_bitcast_fusion), calls=%async_computation | async-start | bytes 2097152 | tf_op jit(solution)/shard_map/all_to_all | solution.py:67
  43.6 29.4 %copy-start.7 = (f32[2048]{0:T(1024)S(1)}, f32[2048]{0:T(1024)}, u32[]{:S(2)}) copy-start(f32[2048]{0:T(1024)} %param.27) | copy-start | bytes 24580
  60.8 12.0 %all-to-all-start.1 = ((bf16[4,128,512]{1,2,0:T(8,128)(2,1)}), bf16[4,128,512]{1,2,0:T(8,128)(2,1)S(1)}, u32[]{:S(2)}, u32[]{:S(2)}) async-start(bf16[4,128,512]{1,2,0:T(8,128)(2,1)} %broadcast_in_dim.54), calls=%async_computation.1 | async-start | bytes 1048576 | tf_op jit(solution)/shard_map/all_to_all | solution.py:56
  74.7 109.8 %copy-start.10 = (bf16[1,2048,352]{1,2,0:T(8,128)(2,1)S(1)}, bf16[1,2048,352]{1,2,0:T(8,128)(2,1)}, u32[]{:S(2)}) copy-start(bf16[1,2048,352]{1,2,0:T(8,128)(2,1)} %param.30) | copy-start | bytes 4325380
  184.5 1.8 copy-start.11
  229.1 34.5 %all-to-all-start.5 = ((bf16[64,16,512]{2,1,0:T(8,128)(2,1)}), bf16[64,16,512]{2,1,0:T(8,128)(2,1)S(1)}, u32[]{:S(2)}, u32[]{:S(2)}) async-start(bf16[64,16,512]{2,1,0:T(8,128)(2,1)} %bitcast.164), calls=%async_computation.5 | async-start | bytes 2097152 | tf_op jit(solution)/shard_map/all_to_all | solution.py:84
  239.8 28.0 %copy-start.9 = (f32[128,6]{0,1:T(8,128)S(1)}, f32[128,6]{0,1:T(8,128)}, u32[]{:S(2)}) copy-start(f32[128,6]{0,1:T(8,128)} %param.29) | copy-start | bytes 9220
  263.6 14.4 %all-to-all-start.2 = ((bf16[4,128,512]{2,1,0:T(8,128)(2,1)}), bf16[4,128,512]{2,1,0:T(8,128)(2,1)}, u32[]{:S(2)}, u32[]{:S(2)}) async-start(bf16[4,128,512]{2,1,0:T(8,128)(2,1)} %bitcast.124), calls=%async_computation.2 | async-start | bytes 1048576 | tf_op jit(solution)/shard_map/all_to_all | solution.py:67
Sparse Core Ops, SparseCore 0:
  10.1 95.2 all-gather.1

commit v3 on v2

--- a/solution.py
+++ b/solution.py
@@ -158,15 +158,13 @@
     codes = (expert_ids * capacity + slot_index).reshape(tok_rows, route_count)
     slots = jnp.arange(experts * capacity, dtype=jnp.int32)
     placing = jnp.any(codes[None, :, :] == slots[:, None, None], axis=2).astype(jnp.bfloat16)
-    buffer = jnp.dot(placing, normed_rows, preferred_element_type=jnp.float32).astype(jnp.bfloat16)
-    buffer = buffer.reshape(experts, capacity, normed_rows.shape[1])
+    own_normed = lax.dynamic_slice_in_dim(normed_rows, col_start, quarter, 1)
+    buffer = jnp.dot(placing, own_normed, preferred_element_type=jnp.float32).astype(jnp.bfloat16)
+    buffer = buffer.reshape(experts, capacity, quarter)
+    received = lax.all_to_all(buffer, "dp", split_axis=0, concat_axis=0, tiled=True)
     results = run_experts(
-        lax.all_to_all(
-            buffer,
-            "dp",
-            split_axis=0,
-            concat_axis=0,
-            tiled=True,
+        gather_mp(received.reshape(experts * capacity, quarter), 1).reshape(
+            experts, capacity, model_width
         ),
         w_gate,
         w_up,

time: 288 us -> 272 us (0.944)
  blocking collectives: 148 us -> 132 us
    all_to_all x1, blocking collectives: 110 us -> 42.8 us  [on_device(): lax.all_to_all(buffer, 'dp', split_axis=0, concat_axis=0, tiled=True)]
    all_to_all x1 -> x2, blocking collectives: 37.8 us -> 88.9 us  [gather_mp(): lax.all_to_all(copies, 'mp', split_axis=0, concat_axis=0, tiled=True)]
  transfers between devices with their start and end apart: 5 -> 5, of which waited for: 4 -> 4; matrix products, arithmetic and copies ran while one was open for 21% -> 22% of each run, Pallas kernels for 0% -> 0%
where the time goes in v3:
time: 272 us; the launch traced here: 271 us
  blocking collectives  132 us (49%)
  waiting for transfers between devices  41.3 us (15%)
  local copies, waits for them, and re-layouts  27.6 us (10%)
  matrix products  26.1 us (10%)
  starting transfers between devices  18.6 us (7%)
  between operations  13.7 us (5%)
  other arithmetic  11.9 us (4%)
    all_to_all x2, blocking collectives, gather_mp(): lax.all_to_all(copies, 'mp', split_axis=0, concat_axis=0, tiled=True)  88.9 us
    all_to_all x1, blocking collectives, on_device(): lax.all_to_all(buffer, 'dp', split_axis=0, concat_axis=0, tiled=True)  42.8 us
    all_to_all x2, waiting for transfers between devices, scatter_sum_mp(): lax.all_to_all(blocks, 'mp', split_axis=0, concat_axis=0, tiled=True)  18.7 us
    all_to_all x1, waiting for transfers between devices, run_experts(): lax.all_to_all(outputs, 'dp', split_axis=0, concat_axis=0, tiled=True)  15.6 us
    all_to_all x2, starting transfers between devices, scatter_sum_mp(): lax.all_to_all(blocks, 'mp', split_axis=0, concat_axis=0, tiled=True)  8.42 us
    dot_general x1, matrix products, shared_experts(): jnp.einsum('th,dh->td', shared_hidden, gathered[:, 2 * hidden_width:], pr...  7.37 us
    all_to_all x1, waiting for transfers between devices, gather_mp(): lax.all_to_all(copies, 'mp', split_axis=0, concat_axis=0, tiled=True)  7 us
    all_to_all x1, starting transfers between devices, run_experts(): lax.all_to_all(outputs, 'dp', split_axis=0, concat_axis=0, tiled=True)  6.75 us
  transfers between devices with their start and end apart: 5, of which 4 were waited for; matrix products, arithmetic and copies ran while one was open for 22% of the time, Pallas kernels for 0%

profile of v3, /device:TPU:32, one launch (start us, length us, event | category | flops | bytes accessed | tf_op | source)
XLA Modules:
  0.0 271.3 jit_solution(6164510138250001464)
XLA Ops:
  6.5 1.7 concatenate.3
  8.3 1.0 fusion.79
  9.3 0.6 copy.66
  9.9 0.6 copy.67
  10.5 0.9 reshape.147
  11.5 0.7 copy.49
  12.2 0.8 broadcast_compare_fusion
  13.2 0.8 eq.50
  14.0 18.0 %while.10 = (s32[]{:T(128)}, bf16[2,256,128]{2,1,0:T(8,128)(2,1)}, s32[2]{0:T(128)}, bf16[2,256,128]{2,1,0:T(8,128)(2,1)}, s32[2,32]{1,0:T(2,128)}, /*index=5*/b...) while((s32[]{:T(128)}, bf16[2,256,128]{2,1,0:T(8,128)(2,1)}, ...), condition=%wide.region_5.6_spmd, body=%wide.region_0.5_spmd.sunk | while | flops 554947200 | bytes 25811812 | solution.py:48
  14.0 0.7 fusion.111
  14.7 2.7 gather_fusion
  17.6 0.4 copy-done.17
  18.0 0.5 dynamic_slice.85
  18.6 0.5 iota_compare_fusion.5
  19.1 0.8 fusion.113
  20.2 0.9 fusion.116
  21.2 0.9 fusion.115
  22.3 0.6 copy-done.10
  23.0 0.7 fusion.111
  23.7 2.7 %gather_fusion = bf16[32,2,128,128]{3,2,1,0:T(8,128)(2,1)S(1)} fusion(bf16[40,2,128,128]{3,2,1,0:T(8,128)(2,1)} %get-tuple-element.173, s32[1024]{0:T(1024)S(1)} %pad_clamp_fusion.3), kind=kCustom, calls=%fused_computation.clone.1 | custom fusion | bytes 4194432 | tf_op jit(solution)/shard_map/while/body/eval_jaxpr/gather | solution.py:22
  26.6 0.4 copy-done.17
  27.1 0.5 dynamic_slice.85
  27.6 0.5 iota_compare_fusion.5
  28.2 0.8 fusion.113
  29.2 0.9 fusion.116
  30.2 0.9 fusion.115
  31.4 0.6 copy-done.10
  32.0 1.0 copy.53
  33.0 0.7 reshape.175
  33.7 2.9 %copy.65 = bf16[2048,512]{1,0:T(8,128)(2,1)S(1)} copy(bf16[2048,512]{0,1:T(8,128)(2,1)} %bitcast.166) | data formatting | bytes 4194304 | tf_op jit(solution)/shard_map/dot_general | solution.py:142
  36.6 2.8 %convolution_bitcast_fusion = f32[4,128,512]{2,1,0:T(8,128)} fusion(bf16[128,512,1]{1,0,2:T(8,128)(2,1)} %reshape.175, bf16[4,512,512]{2,1,0:T(8,128)(2,1)S(1)} %bitcast.159), kind=kOutput, calls=%fused_computation.59 | convolution fusion | flops 268435456 | bytes 3276800 | tf_op jit(solution)/shard_map/dot_general | solution.py:142
  39.4 4.3 %all-to-all-start = ((f32[4,128,512]{2,1,0:T(8,128)}), f32[4,128,512]{2,1,0:T(8,128)S(1)}, u32[]{:S(2)}, u32[]{:S(2)}) async-start(f32[4,128,512]{2,1,0:T(8,128)} %convolution_bitcast_fusion), calls=%async_computation | async-start | bytes 2097152 | tf_op jit(solution)/shard_map/all_to_all | solution.py:67
  44.1 1.8 reduce-window.6
  45.9 0.3 slice_reduce_fusion
  46.2 12.5 %all-to-all-done = f32[4,128,512]{2,1,0:T(8,128)S(1)} async-done(((f32[4,128,512]{2,1,0:T(8,128)}), f32[4,128,512]{2,1,0:T(8,128)S(1)}, u32[]{:S(2)}, u32[]{:S(2)}) %all-to-all-start) | async-done | bytes 1048608 | tf_op jit(solution)/shard_map/all_to_all | solution.py:67
  58.8 0.9 add_convert_fusion
  59.9 0.9 broadcast_in_dim.61
  60.8 3.5 %all-to-all-start.1 = ((bf16[4,128,512]{1,2,0:T(8,128)(2,1)}), bf16[4,128,512]{1,2,0:T(8,128)(2,1)S(1)}, u32[]{:S(2)}, u32[]{:S(2)}) async-start(bf16[4,128,512]{1,2,0:T(8,128)(2,1)} %broadcast_in_dim.61), calls=%async_computation.1 | async-start | bytes 1048576 | tf_op jit(solution)/shard_map/all_to_all | solution.py:56
  64.6 0.6 broadcast_multiply_fusion
  65.3 0.5 fusion.39
  65.8 7.0 %all-to-all-done.1 = bf16[4,128,512]{1,2,0:T(8,128)(2,1)S(1)} async-done(((bf16[4,128,512]{1,2,0:T(8,128)(2,1)}), bf16[4,128,512]{1,2,0:T(8,128)(2,1)S(1)}, u32[]{:S(2)}, u32[]{:S(2)}) %all-to-all-start.1) | async-done | bytes 524320 | tf_op jit(solution)/shard_map/all_to_all | solution.py:56
  72.8 0.3 multiply_reduce_fusion
  73.1 0.3 fusion.59
  73.5 0.4 convolution_convert_fusion.1
  73.9 42.8 %all_to_all.35 = bf16[64,16,512]{2,1,0:T(8,128)(2,1)S(1)} all-to-all(bf16[64,16,512]{2,1,0:T(8,128)(2,1)S(1)} %bitcast.163), channel_id=1, replica_groups=mesh['dp'=64,'mp'=4] {'dp'}, dimensions={0} | all-to-all | bytes 2097152 | tf_op jit(solution)/shard_map/all_to_all | solution.py:164
  116.7 0.5 copy.62
  117.2 0.5 broadcast_in_dim.63
  117.8 52.5 %all_to_all.36 = bf16[4,1024,512]{1,2,0:T(8,128)(2,1)S(1)} all-to-all(bf16[4,1024,512]{1,2,0:T(8,128)(2,1)S(1)} %broadcast_in_dim.63), channel_id=1, replica_groups=mesh['dp'=64,'mp'=4] {'mp'}, dimensions={0} | all-to-all | bytes 8388608 | tf_op jit(solution)/shard_map/all_to_all | solution.py:56
  170.3 1.7 fusion.45
  172.0 1.8 fusion.47
  173.8 0.4 broadcast_in_dim.64
  174.2 36.4 %all_to_all.37 = bf16[4,1024,352]{1,2,0:T(8,128)(2,1)S(1)} all-to-all(bf16[4,1024,352]{1,2,0:T(8,128)(2,1)S(1)} %broadcast_in_dim.64), channel_id=1, replica_groups=mesh['dp'=64,'mp'=4] {'mp'}, dimensions={0} | all-to-all | bytes 5767168 | tf_op jit(solution)/shard_map/all_to_all | solution.py:56
  210.6 2.9 %convolution_convert_fusion = bf16[1024,512]{1,0:T(8,128)(2,1)} fusion(bf16[1024,1408]{0,1:T(8,128)(2,1)S(1)} %bitcast.165, bf16[1,1408,512]{2,1,0:T(8,128)(2,1)S(1)} %copy-done), kind=kOutput, calls=%fused_computation.51 | convolution fusion | flops 1476919296 | bytes 5373952 | tf_op jit(solution)/shard_map/dot_general | solution.py:78
  213.5 6.8 %all-to-all-start.6 = ((bf16[64,16,512]{2,1,0:T(8,128)(2,1)}), bf16[64,16,512]{2,1,0:T(8,128)(2,1)S(1)}, u32[]{:S(2)}, u32[]{:S(2)}) async-start(bf16[64,16,512]{2,1,0:T(8,128)(2,1)} %bitcast.34), calls=%async_computation.6 | async-start | bytes 2097152 | tf_op jit(solution)/shard_map/all_to_all | solution.py:84
  220.4 3.9 %fusion.37 = f32[128,704]{0,1:T(8,128)} fusion(bf16[128,2048]{0,1:T(8,128)(2,1)S(1)} %copy-done.6, bf16[2048,2112]{1,0:T(8,128)(2,1)} %all-gather.2.cloned.1.call-done), kind=kOutput, calls=%fused_computation.46 | convolution fusion | flops 369098752 | bytes 4030464 | tf_op jit(solution)/shard_map/dot_general | solution.py:91
  224.4 7.4 %fusion.40 = bf16[128,2048]{1,0:T(8,128)(2,1)S(1)} fusion(bf16[2048,2112]{1,0:T(8,128)(2,1)} %all-gather.2.cloned.1.call-done, bf16[128,2048]{0,1:T(8,128)(2,1)S(1)} %copy-done.6, f32[128,704]{0,1:T(8,128)} %fusion.37), kind=kOutput, calls=%fused_computation.50 | convolution fusion | flops 739000320 | bytes 7700480 | tf_op jit(solution)/shard_map/th,dh->td/dot_general | solution.py:98
  231.7 0.8 copy.73
  232.6 15.6 %all-to-all-done.6 = bf16[64,16,512]{2,1,0:T(8,128)(2,1)S(1)} async-done(((bf16[64,16,512]{2,1,0:T(8,128)(2,1)}), bf16[64,16,512]{2,1,0:T(8,128)(2,1)S(1)}, u32[]{:S(2)}, u32[]{:S(2)}) %all-to-all-start.6) | async-done | bytes 1048608 | tf_op jit(solution)/shard_map/all_to_all | solution.py:84
  248.2 4.1 %all-to-all-start.2 = ((bf16[4,128,512]{2,1,0:T(8,128)(2,1)}), bf16[4,128,512]{2,1,0:T(8,128)(2,1)}, u32[]{:S(2)}, u32[]{:S(2)}) async-start(bf16[4,128,512]{2,1,0:T(8,128)(2,1)} %bitcast.126), calls=%async_computation.2 | async-start | bytes 1048576 | tf_op jit(solution)/shard_map/all_to_all | solution.py:67
  252.5 2.7 gather_fusion.1
  255.4 1.0 fusion.80
  256.4 6.1 %all-to-all-done.2 = bf16[4,128,512]{2,1,0:T(8,128)(2,1)} async-done(((bf16[4,128,512]{2,1,0:T(8,128)(2,1)}), bf16[4,128,512]{2,1,0:T(8,128)(2,1)}, u32[]{:S(2)}, u32[]{:S(2)}) %all-to-all-start.2) | async-done | bytes 524320 | tf_op jit(solution)/shard_map/all_to_all | solution.py:67
  262.5 1.1 convert_reduce_fusion
  263.7 0.7 fusion.65
  (82 shorter events, 3.1 us)
Async XLA Ops:
  6.5 204.1 %copy-start = (bf16[1,1408,512]{2,1,0:T(8,128)(2,1)S(1)}, bf16[1,1408,512]{2,1,0:T(8,128)(2,1)}, u32[]{:S(2)}) copy-start(bf16[1,1408,512]{2,1,0:T(8,128)(2,1)} %param.32) | copy-start | bytes 4325380
  6.5 213.9 %all-gather.2.cloned.1.call-start = ((), (), s32[]{:S(2)}) async-start(), calls=%async_computation.7 | async-start | bytes 9052160 | tf_op jit(solution)/shard_map/all_gather | solution.py:90
  17.4 0.7 copy-start.17
  17.4 1.8 copy-start.1
  17.6 2.4 copy-start.4
  17.6 2.4 copy-start.7
  21.1 0.9 copy-start.9
  21.2 0.9 copy-start.11
  22.3 0.7 copy-start.10
  26.4 0.7 copy-start.17
  26.4 1.8 copy-start.1
  26.6 2.4 copy-start.4
  26.6 2.4 copy-start.7
  30.2 0.9 copy-start.9
  30.2 0.9 copy-start.11
  31.3 0.7 copy-start.10
  36.6 7.0 %copy-start.13 = (s32[128,6]{0,1:T(8,128)S(1)}, s32[128,6]{0,1:T(8,128)}, u32[]{:S(2)}) copy-start(s32[128,6]{0,1:T(8,128)} %param.28) | copy-start | bytes 9220
  39.4 19.3 %all-to-all-start = ((f32[4,128,512]{2,1,0:T(8,128)}), f32[4,128,512]{2,1,0:T(8,128)S(1)}, u32[]{:S(2)}, u32[]{:S(2)}) async-start(f32[4,128,512]{2,1,0:T(8,128)} %convolution_bitcast_fusion), calls=%async_computation | async-start | bytes 2097152 | tf_op jit(solution)/shard_map/all_to_all | solution.py:67
  44.1 29.0 %copy-start.12 = (f32[2048]{0:T(1024)S(1)}, f32[2048]{0:T(1024)}, u32[]{:S(2)}) copy-start(f32[2048]{0:T(1024)} %param.27) | copy-start | bytes 24580
  59.7 1.1 copy-start.2
  60.8 12.0 %all-to-all-start.1 = ((bf16[4,128,512]{1,2,0:T(8,128)(2,1)}), bf16[4,128,512]{1,2,0:T(8,128)(2,1)S(1)}, u32[]{:S(2)}, u32[]{:S(2)}) async-start(bf16[4,128,512]{1,2,0:T(8,128)(2,1)} %broadcast_in_dim.61), calls=%async_computation.1 | async-start | bytes 1048576 | tf_op jit(solution)/shard_map/all_to_all | solution.py:56
  73.4 43.3 %copy-start.5 = (bf16[128,2048]{0,1:T(8,128)(2,1)}, bf16[128,2048]{0,1:T(8,128)(2,1)S(1)}, u32[]{:S(2)}) copy-start(bf16[128,2048]{0,1:T(8,128)(2,1)S(1)} %fusion.59) | copy-start | bytes 1572868
  117.8 52.5 %copy-start.15 = (bf16[1,2048,352]{1,2,0:T(8,128)(2,1)S(1)}, bf16[1,2048,352]{1,2,0:T(8,128)(2,1)}, u32[]{:S(2)}) copy-start(bf16[1,2048,352]{1,2,0:T(8,128)(2,1)} %param.30) | copy-start | bytes 4325380
  170.3 1.7 copy-start.16
  210.6 9.6 %copy-start.8 = (s32[128,6]{1,0:T(8,128)S(1)}, s32[128,6]{1,0:T(8,128)}, u32[]{:S(2)}) copy-start(s32[128,6]{1,0:T(8,128)} %get-tuple-element.77) | copy-start | bytes 9220
  210.6 9.8 %copy-start.6 = (bf16[128,2048]{0,1:T(8,128)(2,1)S(1)}, bf16[128,2048]{0,1:T(8,128)(2,1)}, u32[]{:S(2)}) copy-start(bf16[128,2048]{0,1:T(8,128)(2,1)} %copy-done.5) | copy-start | bytes 1572868
  213.5 34.7 %all-to-all-start.6 = ((bf16[64,16,512]{2,1,0:T(8,128)(2,1)}), bf16[64,16,512]{2,1,0:T(8,128)(2,1)S(1)}, u32[]{:S(2)}, u32[]{:S(2)}) async-start(bf16[64,16,512]{2,1,0:T(8,128)(2,1)} %bitcast.34), calls=%async_computation.6 | async-start | bytes 2097152 | tf_op jit(solution)/shard_map/all_to_all | solution.py:84
  224.3 28.0 %copy-start.14 = (f32[128,6]{0,1:T(8,128)S(1)}, f32[128,6]{0,1:T(8,128)}, u32[]{:S(2)}) copy-start(f32[128,6]{0,1:T(8,128)} %param.29) | copy-start | bytes 9220
  248.2 14.4 %all-to-all-start.2 = ((bf16[4,128,512]{2,1,0:T(8,128)(2,1)}), bf16[4,128,512]{2,1,0:T(8,128)(2,1)}, u32[]{:S(2)}, u32[]{:S(2)}) async-start(bf16[4,128,512]{2,1,0:T(8,128)(2,1)} %bitcast.126), calls=%async_computation.2 | async-start | bytes 1048576 | tf_op jit(solution)/shard_map/all_to_all | solution.py:67
  255.2 8.5 %copy-start.3 = (bf16[128,512]{1,0:T(8,128)(2,1)S(1)}, bf16[128,512]{1,0:T(8,128)(2,1)}, u32[]{:S(2)}) copy-start(bf16[128,512]{1,0:T(8,128)(2,1)} %copy-done.2) | copy-start | bytes 393220
Sparse Core Ops, SparseCore 0:
  10.1 99.2 all-gather.1

commit v4 on v3

--- a/solution.py
+++ b/solution.py
@@ -158,14 +158,27 @@
     codes = (expert_ids * capacity + slot_index).reshape(tok_rows, route_count)
     slots = jnp.arange(experts * capacity, dtype=jnp.int32)
     placing = jnp.any(codes[None, :, :] == slots[:, None, None], axis=2).astype(jnp.bfloat16)
-    own_normed = lax.dynamic_slice_in_dim(normed_rows, col_start, quarter, 1)
-    buffer = jnp.dot(placing, own_normed, preferred_element_type=jnp.float32).astype(jnp.bfloat16)
-    buffer = buffer.reshape(experts, capacity, quarter)
+    parts = lax.axis_size("mp")
+    mp_index = lax.axis_index("mp")
+    normed_blocks = normed_rows.reshape(tok_rows, parts, quarter)
+    pair = jnp.take(normed_blocks, (mp_index + jnp.arange(2)) % parts, axis=1)
+    pair = pair.reshape(tok_rows, 2 * quarter)
+    buffer = jnp.dot(placing, pair, preferred_element_type=jnp.float32).astype(jnp.bfloat16)
+    buffer = buffer.reshape(experts, capacity, 2 * quarter)
     received = lax.all_to_all(buffer, "dp", split_axis=0, concat_axis=0, tiled=True)
+    received = received.reshape(experts * capacity, 2, quarter)
+    from_left = lax.ppermute(
+        received[:, 0], "mp", [(k, (k + 1) % parts) for k in range(parts)]
+    )
+    from_right = lax.ppermute(
+        received[:, 1], "mp", [(k, (k - 1) % parts) for k in range(parts)]
+    )
+    rotated = jnp.concatenate(
+        [received.reshape(experts * capacity, 2 * quarter), from_right, from_left], axis=1
+    )
+    full_rows = jnp.roll(rotated, mp_index * quarter, axis=1)
     results = run_experts(
-        gather_mp(received.reshape(experts * capacity, quarter), 1).reshape(
-            experts, capacity, model_width
-        ),
+        full_rows.reshape(experts, capacity, model_width),
         w_gate,
         w_up,
         w_down,

time: 272 us -> 286 us (1.051)
  blocking collectives: 132 us -> 99.1 us
  waiting for transfers between devices: 41.3 us -> 64.8 us
  local copies, waits for them, and re-layouts: 27.6 us -> 43.4 us
  matrix products: 26.1 us -> 29.4 us
    all_to_all x2 -> x1, blocking collectives: 88.9 us -> 36.3 us  [gather_mp(): lax.all_to_all(copies, 'mp', split_axis=0, concat_axis=0, tiled=True)]
    ppermute x0 -> x2, waiting for transfers between devices: none -> 24.5 us  [the longest x1 21.9 us: on_device(): lax.ppermute(received[:, 1], 'mp', [(k, (k - 1) % parts) for k in range(p...]
    all_to_all x1, blocking collectives: 42.8 us -> 62.7 us  [on_device(): lax.all_to_all(buffer, 'dp', split_axis=0, concat_axis=0, tiled=True)]
    unnamed x26 -> x35, local copies, waits for them, and re-layouts: 1.49 us -> 8.51 us
    slice x1 -> x2, local copies, waits for them, and re-layouts: 0.28 us -> 5.95 us  [the longest x1 5.67 us: on_device(): received[:, 0]]
  transfers between devices with their start and end apart: 5 -> 7, of which waited for: 4 -> 6; matrix products, arithmetic and copies ran while one was open for 22% -> 28% of each run, Pallas kernels for 0% -> 0%
where the time goes in v4:
time: 286 us; the launch traced here: 285 us
  blocking collectives  99.1 us (35%)
  waiting for transfers between devices  64.8 us (23%)
  local copies, waits for them, and re-layouts  43.4 us (15%)
  matrix products  29.4 us (10%)
  starting transfers between devices  20.7 us (7%)
  between operations  13.8 us (5%)
  other arithmetic  13.3 us (5%)
    all_to_all x1, blocking collectives, on_device(): lax.all_to_all(buffer, 'dp', split_axis=0, concat_axis=0, tiled=True)  62.7 us
    all_to_all x1, blocking collectives, gather_mp(): lax.all_to_all(copies, 'mp', split_axis=0, concat_axis=0, tiled=True)  36.3 us
    ppermute x1, waiting for transfers between devices, on_device(): lax.ppermute(received[:, 1], 'mp', [(k, (k - 1) % parts) for k in range(p...  21.9 us
    all_to_all x2, waiting for transfers between devices, scatter_sum_mp(): lax.all_to_all(blocks, 'mp', split_axis=0, concat_axis=0, tiled=True)  17.8 us
    all_to_all x1, waiting for transfers between devices, run_experts(): lax.all_to_all(outputs, 'dp', split_axis=0, concat_axis=0, tiled=True)  14.7 us
    unnamed x35, local copies, waits for them, and re-layouts  8.51 us
    all_to_all x2, starting transfers between devices, scatter_sum_mp(): lax.all_to_all(blocks, 'mp', split_axis=0, concat_axis=0, tiled=True)  8.43 us
    all_to_all x1, waiting for transfers between devices, gather_mp(): lax.all_to_all(copies, 'mp', split_axis=0, concat_axis=0, tiled=True)  7.81 us
  transfers between devices with their start and end apart: 7, of which 6 were waited for; matrix products, arithmetic and copies ran while one was open for 28% of the time, Pallas kernels for 0%

profile of v4, /device:TPU:32, one launch (start us, length us, event | category | flops | bytes accessed | tf_op | source)
XLA Modules:
  0.0 284.9 jit_solution(4223669517747038667)
XLA Ops:
  6.5 1.7 concatenate.9
  8.3 0.9 broadcast_compare_fusion
  9.5 0.9 reshape.216
  10.5 1.0 fusion.88
  12.1 21.9 %while.10 = (s32[]{:T(128)}, bf16[2,256,128]{2,1,0:T(8,128)(2,1)}, s32[2]{0:T(128)}, bf16[2,256,128]{2,1,0:T(8,128)(2,1)S(1)}, s32[2,32]{1,0:T(2,128)}, /*index=...) while((s32[]{:T(128)}, bf16[2,256,128]{2,1,0:T(8,128)(2,1)}, ...), condition=%wide.region_5.6_spmd, body=%wide.region_0.5_spmd.sunk | while | flops 554947200 | bytes 26860448 | solution.py:48
  12.1 1.3 dynamic_slice.90
  13.5 0.7 fusion.119
  14.2 0.7 iota_compare_fusion.5
  14.9 0.8 fusion.122
  15.7 2.7 gather_fusion
  18.5 1.7 fusion.121
  20.2 0.9 fusion.123
  21.2 0.9 fusion.124
  22.4 0.6 copy-done.14
  23.1 1.4 dynamic_slice.90
  24.4 0.7 fusion.119
  25.1 0.7 iota_compare_fusion.5
  25.8 0.8 fusion.122
  26.6 2.7 gather_fusion
  29.4 1.7 fusion.121
  31.1 0.9 fusion.123
  32.1 0.9 fusion.124
  33.3 0.6 copy-done.14
  34.0 1.0 copy.62
  35.0 0.7 reshape.253
  35.7 2.9 %copy.73 = bf16[2048,512]{1,0:T(8,128)(2,1)S(1)} copy(bf16[2048,512]{0,1:T(8,128)(2,1)} %bitcast.175) | data formatting | bytes 4194304 | tf_op jit(solution)/shard_map/dot_general | solution.py:142
  38.6 2.7 convolution_bitcast_fusion
  41.3 4.3 %all-to-all-start = ((f32[4,128,512]{2,1,0:T(8,128)}), f32[4,128,512]{2,1,0:T(8,128)S(1)}, u32[]{:S(2)}, u32[]{:S(2)}) async-start(f32[4,128,512]{2,1,0:T(8,128)} %convolution_bitcast_fusion), calls=%async_computation | async-start | bytes 2097152 | tf_op jit(solution)/shard_map/all_to_all | solution.py:67
  46.1 1.8 reduce-window.6
  48.4 0.6 broadcast_multiply_fusion
  49.1 11.7 %all-to-all-done = f32[4,128,512]{2,1,0:T(8,128)S(1)} async-done(((f32[4,128,512]{2,1,0:T(8,128)}), f32[4,128,512]{2,1,0:T(8,128)S(1)}, u32[]{:S(2)}, u32[]{:S(2)}) %all-to-all-start) | async-done | bytes 1048608 | tf_op jit(solution)/shard_map/all_to_all | solution.py:67
  60.8 0.9 add_convert_fusion
  61.9 0.9 broadcast_in_dim.68
  62.8 3.5 %all-to-all-start.1 = ((bf16[4,128,512]{1,2,0:T(8,128)(2,1)}), bf16[4,128,512]{1,2,0:T(8,128)(2,1)S(1)}, u32[]{:S(2)}, u32[]{:S(2)}) async-start(bf16[4,128,512]{1,2,0:T(8,128)(2,1)} %broadcast_in_dim.68), calls=%async_computation.1 | async-start | bytes 1048576 | tf_op jit(solution)/shard_map/all_to_all | solution.py:56
  67.0 7.8 %all-to-all-done.1 = bf16[4,128,512]{1,2,0:T(8,128)(2,1)S(1)} async-done(((bf16[4,128,512]{1,2,0:T(8,128)(2,1)}), bf16[4,128,512]{1,2,0:T(8,128)(2,1)S(1)}, u32[]{:S(2)}, u32[]{:S(2)}) %all-to-all-start.1) | async-done | bytes 524320 | tf_op jit(solution)/shard_map/all_to_all | solution.py:56
  76.8 0.7 convolution_convert_fusion
  77.5 62.7 %all_to_all.30 = bf16[64,16,1024]{2,1,0:T(8,128)(2,1)S(1)} all-to-all(bf16[64,16,1024]{2,1,0:T(8,128)(2,1)S(1)} %bitcast.171), channel_id=1, replica_groups=mesh['dp'=64,'mp'=4] {'dp'}, dimensions={0} | all-to-all | bytes 4194304 | tf_op jit(solution)/shard_map/all_to_all | solution.py:168
  140.3 2.8 reshape.223
  143.1 5.7 %fusion.87 = (bf16[1024,1,512]{2,1,0:T(2,128)(2,1)S(1)}, bf16[1024,1,512]{2,1,0:T(2,128)(2,1)S(1)}) fusion(bf16[1024,2,512]{2,1,0:T(2,128)(2,1)} %reshape.223), kind=kLoop, calls=%fused_computation.126 | loop fusion | bytes 4194304 | tf_op jit(solution)/shard_map/slice | solution.py:171
  148.8 1.3 copy.86
  150.0 2.0 collective-permute-start
  152.0 1.3 copy.85
  153.6 21.9 %collective-permute-done = bf16[1024,512]{1,0:T(8,128)(2,1)} collective-permute-done((bf16[1024,512]{1,0:T(8,128)(2,1)}, bf16[1024,512]{1,0:T(8,128)(2,1)}, u32[]{:S(2)}, u32[]{:S(2)}) %collective-permute-start) | collective-permute-done | bytes 1048608 | tf_op jit(solution)/shard_map/ppermute | solution.py:173
  175.5 1.3 constant_dynamic-update-slice_fusion.4
  176.8 2.6 collective-permute-done.1
  179.4 1.3 constant_dynamic-update-slice_fusion.3
  181.0 1.5 constant_dynamic-update-slice_fusion.1
  182.5 1.3 constant_dynamic-update-slice_fusion
  183.8 1.8 fusion.35
  185.6 1.8 multiply_convert_fusion
  187.9 36.3 %all_to_all.31 = bf16[4,1024,352]{1,2,0:T(8,128)(2,1)S(1)} all-to-all(bf16[4,1024,352]{1,2,0:T(8,128)(2,1)S(1)} %broadcast_in_dim.73), channel_id=1, replica_groups=mesh['dp'=64,'mp'=4] {'mp'}, dimensions={0} | all-to-all | bytes 5767168 | tf_op jit(solution)/shard_map/all_to_all | solution.py:56
  224.2 2.9 %convolution_convert_fusion.1 = bf16[1024,512]{1,0:T(8,128)(2,1)} fusion(bf16[1024,1408]{0,1:T(8,128)(2,1)S(1)} %bitcast.174, bf16[1,1408,512]{2,1,0:T(8,128)(2,1)S(1)} %copy-done), kind=kOutput, calls=%fused_computation.57 | convolution fusion | flops 1476919296 | bytes 5373952 | tf_op jit(solution)/shard_map/dot_general | solution.py:78
  227.1 6.8 %all-to-all-start.5 = ((bf16[64,16,512]{2,1,0:T(8,128)(2,1)}), bf16[64,16,512]{2,1,0:T(8,128)(2,1)S(1)}, u32[]{:S(2)}, u32[]{:S(2)}) async-start(bf16[64,16,512]{2,1,0:T(8,128)(2,1)} %bitcast.176), calls=%async_computation.5 | async-start | bytes 2097152 | tf_op jit(solution)/shard_map/all_to_all | solution.py:84
  234.0 0.9 fusion.59
  235.0 3.9 %fusion.41 = f32[128,704]{0,1:T(8,128)} fusion(bf16[128,2048]{0,1:T(8,128)(2,1)S(1)} %fusion.59, bf16[2048,2112]{1,0:T(8,128)(2,1)} %all-gather.2.cloned.1.call-done), kind=kOutput, calls=%fused_computation.51 | convolution fusion | flops 369098752 | bytes 4030464 | tf_op jit(solution)/shard_map/dot_general | solution.py:91
  238.9 7.4 %fusion.44 = bf16[128,2048]{1,0:T(8,128)(2,1)S(1)} fusion(bf16[2048,2112]{1,0:T(8,128)(2,1)} %all-gather.2.cloned.1.call-done, bf16[128,2048]{0,1:T(8,128)(2,1)S(1)} %fusion.59, f32[128,704]{0,1:T(8,128)} %fusion.41), kind=kOutput, calls=%fused_computation.55 | convolution fusion | flops 739000320 | bytes 7700480 | tf_op jit(solution)/shard_map/th,dh->td/dot_general | solution.py:98
  246.3 0.8 copy.87
  247.1 14.7 %all-to-all-done.5 = bf16[64,16,512]{2,1,0:T(8,128)(2,1)S(1)} async-done(((bf16[64,16,512]{2,1,0:T(8,128)(2,1)}), bf16[64,16,512]{2,1,0:T(8,128)(2,1)S(1)}, u32[]{:S(2)}, u32[]{:S(2)}) %all-to-all-start.5) | async-done | bytes 1048608 | tf_op jit(solution)/shard_map/all_to_all | solution.py:84
  261.8 4.1 %all-to-all-start.2 = ((bf16[4,128,512]{2,1,0:T(8,128)(2,1)}), bf16[4,128,512]{2,1,0:T(8,128)(2,1)}, u32[]{:S(2)}, u32[]{:S(2)}) async-start(bf16[4,128,512]{2,1,0:T(8,128)(2,1)} %bitcast.136), calls=%async_computation.2 | async-start | bytes 1048576 | tf_op jit(solution)/shard_map/all_to_all | solution.py:67
  266.1 2.7 gather_fusion.2
  269.1 1.0 fusion.89
  270.0 6.1 %all-to-all-done.2 = bf16[4,128,512]{2,1,0:T(8,128)(2,1)} async-done(((bf16[4,128,512]{2,1,0:T(8,128)(2,1)}), bf16[4,128,512]{2,1,0:T(8,128)(2,1)}, u32[]{:S(2)}, u32[]{:S(2)}) %all-to-all-start.2) | async-done | bytes 524320 | tf_op jit(solution)/shard_map/all_to_all | solution.py:67
  276.2 1.1 convert_reduce_fusion
  277.3 0.7 fusion.66
  (116 shorter events, 7.2 us)
Async XLA Ops:
  6.5 217.7 %copy-start = (bf16[1,1408,512]{2,1,0:T(8,128)(2,1)S(1)}, bf16[1,1408,512]{2,1,0:T(8,128)(2,1)}, u32[]{:S(2)}) copy-start(bf16[1,1408,512]{2,1,0:T(8,128)(2,1)} %param.32) | copy-start | bytes 4325380
  6.5 228.4 %all-gather.2.cloned.1.call-start = ((), (), s32[]{:S(2)}) async-start(), calls=%async_computation.6 | async-start | bytes 9052160 | tf_op jit(solution)/shard_map/all_gather | solution.py:90
  12.1 3.5 %copy-start.4 = (bf16[2,256,128]{2,1,0:T(8,128)(2,1)}, bf16[2,256,128]{2,1,0:T(8,128)(2,1)S(1)}, u32[]{:S(2)}) copy-start(bf16[2,256,128]{2,1,0:T(8,128)(2,1)S(1)} %get-tuple-element.173) | copy-start | bytes 393220 | tf_op jit(solution)/shard_map/while
  12.1 3.5 %copy-start.8 = (pred[2,256,64]{1,2,0:T(32,128)(4,1)}, pred[2,256,64]{1,2,0:T(32,128)(4,1)S(1)}, u32[]{:S(2)}) copy-start(pred[2,256,64]{1,2,0:T(32,128)(4,1)S(1)} %get-tuple-element.176) | copy-start | bytes 98308 | tf_op jit(solution)/shard_map/while
  12.1 3.5 %copy-start.10 = (bf16[2,64,128]{2,1,0:T(8,128)(2,1)}, bf16[2,64,128]{2,1,0:T(8,128)(2,1)S(1)}, u32[]{:S(2)}) copy-start(bf16[2,64,128]{2,1,0:T(8,128)(2,1)S(1)} %get-tuple-element.177) | copy-start | bytes 98308 | tf_op jit(solution)/shard_map/while
  21.1 1.0 copy-start.3
  21.1 1.0 copy-start.9
  21.1 1.0 copy-start.13
  21.1 1.0 copy-start.16
  21.1 1.9 copy-start.5
  21.1 1.9 copy-start.11
  22.4 0.7 copy-start.14
  23.0 3.5 %copy-start.4 = (bf16[2,256,128]{2,1,0:T(8,128)(2,1)}, bf16[2,256,128]{2,1,0:T(8,128)(2,1)S(1)}, u32[]{:S(2)}) copy-start(bf16[2,256,128]{2,1,0:T(8,128)(2,1)S(1)} %get-tuple-element.173) | copy-start | bytes 393220 | tf_op jit(solution)/shard_map/while
  23.0 3.5 %copy-start.8 = (pred[2,256,64]{1,2,0:T(32,128)(4,1)}, pred[2,256,64]{1,2,0:T(32,128)(4,1)S(1)}, u32[]{:S(2)}) copy-start(pred[2,256,64]{1,2,0:T(32,128)(4,1)S(1)} %get-tuple-element.176) | copy-start | bytes 98308 | tf_op jit(solution)/shard_map/while
  23.1 3.5 %copy-start.10 = (bf16[2,64,128]{2,1,0:T(8,128)(2,1)}, bf16[2,64,128]{2,1,0:T(8,128)(2,1)S(1)}, u32[]{:S(2)}) copy-start(bf16[2,64,128]{2,1,0:T(8,128)(2,1)S(1)} %get-tuple-element.177) | copy-start | bytes 98308 | tf_op jit(solution)/shard_map/while
  32.0 1.0 copy-start.3
  32.0 1.0 copy-start.9
  32.1 1.0 copy-start.13
  32.1 1.0 copy-start.16
  32.1 1.9 copy-start.5
  32.1 1.9 copy-start.11
  33.3 0.7 copy-start.14
  38.6 7.1 %copy-start.17 = (s32[128,6]{0,1:T(8,128)S(1)}, s32[128,6]{0,1:T(8,128)}, u32[]{:S(2)}) copy-start(s32[128,6]{0,1:T(8,128)} %param.28) | copy-start | bytes 9220
  41.3 19.4 %all-to-all-start = ((f32[4,128,512]{2,1,0:T(8,128)}), f32[4,128,512]{2,1,0:T(8,128)S(1)}, u32[]{:S(2)}, u32[]{:S(2)}) async-start(f32[4,128,512]{2,1,0:T(8,128)} %convolution_bitcast_fusion), calls=%async_computation | async-start | bytes 2097152 | tf_op jit(solution)/shard_map/all_to_all | solution.py:67
  45.6 20.8 %copy-start.15 = (f32[2048]{0:T(1024)S(1)}, f32[2048]{0:T(1024)}, u32[]{:S(2)}) copy-start(f32[2048]{0:T(1024)} %param.27) | copy-start | bytes 24580
  61.8 1.1 copy-start.6
  62.8 12.0 %all-to-all-start.1 = ((bf16[4,128,512]{1,2,0:T(8,128)(2,1)}), bf16[4,128,512]{1,2,0:T(8,128)(2,1)S(1)}, u32[]{:S(2)}, u32[]{:S(2)}) async-start(bf16[4,128,512]{1,2,0:T(8,128)(2,1)} %broadcast_in_dim.68), calls=%async_computation.1 | async-start | bytes 1048576 | tf_op jit(solution)/shard_map/all_to_all | solution.py:56
  74.9 2.7 copy-start.1
  75.2 0.5 copy-start.19
  150.0 25.5 %collective-permute-start = (bf16[1024,512]{1,0:T(8,128)(2,1)}, bf16[1024,512]{1,0:T(8,128)(2,1)}, u32[]{:S(2)}, u32[]{:S(2)}) collective-permute-start(bf16[1024,512]{1,0:T(8,128)(2,1)} %bitcast.134), channel_id=1, source_target_pairs={{0,3},{1,0},{2,1},{3,2},{4,7},{5,4},{6,5},{7,6},{8,11},{9,8},{10,9... | collective-permute-start | bytes 3145736 | tf_op jit(solution)/shard_map/ppermute | solution.py:173
  153.3 26.1 %collective-permute-start.1 = (bf16[1024,512]{1,0:T(8,128)(2,1)}, bf16[1024,512]{1,0:T(8,128)(2,1)}, u32[]{:S(2)}, u32[]{:S(2)}) collective-permute-start(bf16[1024,512]{1,0:T(8,128)(2,1)} %bitcast.133), channel_id=1, source_target_pairs={{0,1},{1,2},{2,3},{3,0},{4,5},{5,6},{6,7},{7,4},{8,9},{9,10},{10,1... | collective-permute-start | bytes 3145736 | tf_op jit(solution)/shard_map/ppermute | solution.py:170
  181.0 2.8 copy-start.20
  183.8 1.8 copy-start.21
  224.2 9.7 %copy-start.12 = (s32[128,6]{1,0:T(8,128)S(1)}, s32[128,6]{1,0:T(8,128)}, u32[]{:S(2)}) copy-start(s32[128,6]{1,0:T(8,128)} %get-tuple-element.79) | copy-start | bytes 9220
  224.2 9.8 %copy-start.2 = (bf16[4,128,512]{1,2,0:T(8,128)(2,1)S(1)}, bf16[4,128,512]{1,2,0:T(8,128)(2,1)}, u32[]{:S(2)}) copy-start(bf16[4,128,512]{1,2,0:T(8,128)(2,1)} %copy-done.1) | copy-start | bytes 1572868
  227.1 34.7 %all-to-all-start.5 = ((bf16[64,16,512]{2,1,0:T(8,128)(2,1)}), bf16[64,16,512]{2,1,0:T(8,128)(2,1)S(1)}, u32[]{:S(2)}, u32[]{:S(2)}) async-start(bf16[64,16,512]{2,1,0:T(8,128)(2,1)} %bitcast.176), calls=%async_computation.5 | async-start | bytes 2097152 | tf_op jit(solution)/shard_map/all_to_all | solution.py:84
  238.9 27.1 %copy-start.18 = (f32[128,6]{0,1:T(8,128)S(1)}, f32[128,6]{0,1:T(8,128)}, u32[]{:S(2)}) copy-start(f32[128,6]{0,1:T(8,128)} %param.29) | copy-start | bytes 9220
  261.8 14.4 %all-to-all-start.2 = ((bf16[4,128,512]{2,1,0:T(8,128)(2,1)}), bf16[4,128,512]{2,1,0:T(8,128)(2,1)}, u32[]{:S(2)}, u32[]{:S(2)}) async-start(bf16[4,128,512]{2,1,0:T(8,128)(2,1)} %bitcast.136), calls=%async_computation.2 | async-start | bytes 1048576 | tf_op jit(solution)/shard_map/all_to_all | solution.py:67
  268.8 8.5 %copy-start.7 = (bf16[128,512]{1,0:T(8,128)(2,1)S(1)}, bf16[128,512]{1,0:T(8,128)(2,1)}, u32[]{:S(2)}) copy-start(bf16[128,512]{1,0:T(8,128)(2,1)} %copy-done.6) | copy-start | bytes 393220
Sparse Core Ops, SparseCore 0:
  10.1 91.9 all-gather.1

commit v5 on v3

--- a/solution.py
+++ b/solution.py
@@ -84,9 +84,10 @@
     return lax.all_to_all(outputs, "dp", split_axis=0, concat_axis=0, tiled=True)
 
 
-def shared_experts(normed_rows, shared_gate, shared_up, shared_down):
+def shared_experts(normed_rows, shared_gate, shared_up, shared_down, after):
     hidden_width = shared_gate.shape[1]
     packed = jnp.concatenate([shared_gate, shared_up, shared_down.T], axis=1)
+    packed, after = lax.optimization_barrier((packed, after))
     gathered = lax.all_gather(packed, "dp", axis=0, tiled=True)
     gate_total = jnp.dot(
         normed_rows, gathered[:, :hidden_width], preferred_element_type=jnp.float32
@@ -170,7 +171,7 @@
         w_up,
         w_down,
     )
-    shared_out = shared_experts(normed_rows, shared_gate, shared_up, shared_down)
+    shared_out = shared_experts(normed_rows, shared_gate, shared_up, shared_down, received)
     result_rows = results.reshape(experts * capacity, quarter)
     picked = (
         result_rows[expert_ids * capacity + slot_index]

time: 272 us -> 269 us (0.989)
  blocking collectives: 132 us -> 89.3 us
  waiting for transfers between devices: 41.3 us -> 68.3 us
  starting transfers between devices: 18.6 us -> 29.6 us
    all_to_all x1 -> x0, blocking collectives: 42.8 us -> none  [on_device(): lax.all_to_all(buffer, 'dp', split_axis=0, concat_axis=0, tiled=True)]
    all_to_all x0 -> x1, waiting for transfers between devices: none -> 27.1 us  [on_device(): lax.all_to_all(buffer, 'dp', split_axis=0, concat_axis=0, tiled=True)]
    all_to_all x0 -> x1, starting transfers between devices: none -> 11.8 us  [on_device(): lax.all_to_all(buffer, 'dp', split_axis=0, concat_axis=0, tiled=True)]
  transfers between devices with their start and end apart: 5 -> 6, of which waited for: 4 -> 5; matrix products, arithmetic and copies ran while one was open for 22% -> 11% of each run, Pallas kernels for 0% -> 0%
where the time goes in v5:
time: 269 us; the launch traced here: 268 us
  blocking collectives  89.3 us (33%)
  waiting for transfers between devices  68.3 us (25%)
  starting transfers between devices  29.6 us (11%)
  local copies, waits for them, and re-layouts  27.6 us (10%)
  matrix products  27 us (10%)
  between operations  13.8 us (5%)
  other arithmetic  12.1 us (4%)
    all_to_all x2, blocking collectives, gather_mp(): lax.all_to_all(copies, 'mp', split_axis=0, concat_axis=0, tiled=True)  89.3 us
    all_to_all x1, waiting for transfers between devices, on_device(): lax.all_to_all(buffer, 'dp', split_axis=0, concat_axis=0, tiled=True)  27.1 us
    all_to_all x2, waiting for transfers between devices, scatter_sum_mp(): lax.all_to_all(blocks, 'mp', split_axis=0, concat_axis=0, tiled=True)  18.7 us
    all_to_all x1, waiting for transfers between devices, run_experts(): lax.all_to_all(outputs, 'dp', split_axis=0, concat_axis=0, tiled=True)  15.5 us
    all_to_all x1, starting transfers between devices, on_device(): lax.all_to_all(buffer, 'dp', split_axis=0, concat_axis=0, tiled=True)  11.8 us
    all_to_all x2, starting transfers between devices, scatter_sum_mp(): lax.all_to_all(blocks, 'mp', split_axis=0, concat_axis=0, tiled=True)  8.42 us
    dot_general x1, matrix products, shared_experts(): jnp.einsum('th,dh->td', shared_hidden, gathered[:, 2 * hidden_width:], pr...  7.37 us
    all_to_all x1, waiting for transfers between devices, gather_mp(): lax.all_to_all(copies, 'mp', split_axis=0, concat_axis=0, tiled=True)  7 us
  transfers between devices with their start and end apart: 6, of which 5 were waited for; matrix products, arithmetic and copies ran while one was open for 11% of the time, Pallas kernels for 0%

profile of v5, /device:TPU:32, one launch (start us, length us, event | category | flops | bytes accessed | tf_op | source)
XLA Modules:
  0.0 267.9 jit_solution(6958083471482409767)
XLA Ops:
  6.5 1.1 reshape.147
  7.6 0.7 copy.49
  8.3 0.8 broadcast_compare_fusion
  9.3 0.8 eq.50
  10.1 1.0 fusion.79
  11.1 0.6 copy.66
  11.7 0.6 copy.67
  12.4 18.3 %while.10 = (s32[]{:T(128)}, bf16[2,256,128]{2,1,0:T(8,128)(2,1)}, s32[2]{0:T(128)}, bf16[2,256,128]{2,1,0:T(8,128)(2,1)}, s32[2,32]{1,0:T(2,128)}, /*index=5*/b...) while((s32[]{:T(128)}, bf16[2,256,128]{2,1,0:T(8,128)(2,1)}, ...), condition=%wide.region_5.6_spmd, body=%wide.region_0.5_spmd.sunk | while | flops 554947200 | bytes 25811820 | solution.py:48
  12.4 0.7 fusion.111
  13.0 2.7 %gather_fusion = bf16[32,2,128,128]{3,2,1,0:T(8,128)(2,1)S(1)} fusion(bf16[40,2,128,128]{3,2,1,0:T(8,128)(2,1)} %get-tuple-element.175, s32[1024]{0:T(1024)S(1)} %pad_clamp_fusion.3), kind=kCustom, calls=%fused_computation.clone.1 | custom fusion | bytes 4194432 | tf_op jit(solution)/shard_map/while/body/eval_jaxpr/gather | solution.py:22
  15.9 0.5 copy-done.20
  16.4 0.6 dynamic_slice.85
  17.0 0.6 iota_compare_fusion.5
  17.7 0.8 fusion.113
  18.7 0.9 fusion.115
  19.6 0.9 fusion.116
  20.9 0.6 copy-done.10
  21.5 0.7 fusion.111
  22.2 2.7 %gather_fusion = bf16[32,2,128,128]{3,2,1,0:T(8,128)(2,1)S(1)} fusion(bf16[40,2,128,128]{3,2,1,0:T(8,128)(2,1)} %get-tuple-element.175, s32[1024]{0:T(1024)S(1)} %pad_clamp_fusion.3), kind=kCustom, calls=%fused_computation.clone.1 | custom fusion | bytes 4194432 | tf_op jit(solution)/shard_map/while/body/eval_jaxpr/gather | solution.py:22
  25.1 0.5 copy-done.20
  25.6 0.6 dynamic_slice.85
  26.2 0.6 iota_compare_fusion.5
  26.8 0.8 fusion.113
  27.9 0.9 fusion.115
  28.8 0.9 fusion.116
  30.0 0.6 copy-done.10
  30.6 1.0 copy.53
  31.7 0.7 reshape.175
  32.4 2.9 %copy.65 = bf16[2048,512]{1,0:T(8,128)(2,1)S(1)} copy(bf16[2048,512]{0,1:T(8,128)(2,1)} %bitcast.165) | data formatting | bytes 4194304 | tf_op jit(solution)/shard_map/dot_general | solution.py:143
  35.3 2.7 %convolution_bitcast_fusion = f32[4,128,512]{2,1,0:T(8,128)} fusion(bf16[128,512,1]{1,0,2:T(8,128)(2,1)} %reshape.175, bf16[4,512,512]{2,1,0:T(8,128)(2,1)S(1)} %bitcast.159), kind=kOutput, calls=%fused_computation.59 | convolution fusion | flops 268435456 | bytes 3276800 | tf_op jit(solution)/shard_map/dot_general | solution.py:143
  37.9 4.3 %all-to-all-start = ((f32[4,128,512]{2,1,0:T(8,128)}), f32[4,128,512]{2,1,0:T(8,128)S(1)}, u32[]{:S(2)}, u32[]{:S(2)}) async-start(f32[4,128,512]{2,1,0:T(8,128)} %convolution_bitcast_fusion), calls=%async_computation | async-start | bytes 2097152 | tf_op jit(solution)/shard_map/all_to_all | solution.py:67
  42.7 1.8 reduce-window.6
  44.8 12.6 %all-to-all-done = f32[4,128,512]{2,1,0:T(8,128)S(1)} async-done(((f32[4,128,512]{2,1,0:T(8,128)}), f32[4,128,512]{2,1,0:T(8,128)S(1)}, u32[]{:S(2)}, u32[]{:S(2)}) %all-to-all-start) | async-done | bytes 1048608 | tf_op jit(solution)/shard_map/all_to_all | solution.py:67
  57.4 0.9 add_convert_fusion
  58.5 0.9 broadcast_in_dim.61
  59.4 3.5 %all-to-all-start.1 = ((bf16[4,128,512]{1,2,0:T(8,128)(2,1)}), bf16[4,128,512]{1,2,0:T(8,128)(2,1)S(1)}, u32[]{:S(2)}, u32[]{:S(2)}) async-start(bf16[4,128,512]{1,2,0:T(8,128)(2,1)} %broadcast_in_dim.61), calls=%async_computation.1 | async-start | bytes 1048576 | tf_op jit(solution)/shard_map/all_to_all | solution.py:56
  63.1 0.6 broadcast_multiply_fusion
  63.8 0.5 fusion.39
  64.3 7.0 %all-to-all-done.1 = bf16[4,128,512]{1,2,0:T(8,128)(2,1)S(1)} async-done(((bf16[4,128,512]{1,2,0:T(8,128)(2,1)}), bf16[4,128,512]{1,2,0:T(8,128)(2,1)S(1)}, u32[]{:S(2)}, u32[]{:S(2)}) %all-to-all-start.1) | async-done | bytes 524320 | tf_op jit(solution)/shard_map/all_to_all | solution.py:56
  71.7 0.3 fusion.59
  72.0 0.8 copy-done.5
  72.8 1.4 convolution_convert_fusion.1
  74.2 11.8 %all-to-all-start.2 = ((bf16[64,16,512]{2,1,0:T(8,128)(2,1)}), bf16[64,16,512]{2,1,0:T(8,128)(2,1)S(1)}, u32[]{:S(2)}, u32[]{:S(2)}) async-start(bf16[64,16,512]{2,1,0:T(8,128)(2,1)} %bitcast.23), calls=%async_computation.2 | async-start | bytes 2097152 | tf_op jit(solution)/shard_map/all_to_all | solution.py:165
  86.1 0.8 concatenate.3
  86.8 27.1 %all-to-all-done.2 = bf16[64,16,512]{2,1,0:T(8,128)(2,1)S(1)} async-done(((bf16[64,16,512]{2,1,0:T(8,128)(2,1)}), bf16[64,16,512]{2,1,0:T(8,128)(2,1)S(1)}, u32[]{:S(2)}, u32[]{:S(2)}) %all-to-all-start.2) | async-done | bytes 1048608 | tf_op jit(solution)/shard_map/all_to_all | solution.py:165
  114.0 0.5 copy.62
  114.5 0.5 broadcast_in_dim.63
  115.0 52.2 %all_to_all.35 = bf16[4,1024,512]{1,2,0:T(8,128)(2,1)S(1)} all-to-all(bf16[4,1024,512]{1,2,0:T(8,128)(2,1)S(1)} %broadcast_in_dim.63), channel_id=1, replica_groups=mesh['dp'=64,'mp'=4] {'mp'}, dimensions={0} | all-to-all | bytes 8388608 | tf_op jit(solution)/shard_map/all_to_all | solution.py:56
  167.2 1.7 fusion.45
  169.0 1.8 fusion.47
  170.8 0.4 broadcast_in_dim.64
  171.1 37.1 %all_to_all.36 = bf16[4,1024,352]{1,2,0:T(8,128)(2,1)S(1)} all-to-all(bf16[4,1024,352]{1,2,0:T(8,128)(2,1)S(1)} %broadcast_in_dim.64), channel_id=1, replica_groups=mesh['dp'=64,'mp'=4] {'mp'}, dimensions={0} | all-to-all | bytes 5767168 | tf_op jit(solution)/shard_map/all_to_all | solution.py:56
  208.2 2.8 %convolution_convert_fusion = bf16[1024,512]{1,0:T(8,128)(2,1)} fusion(bf16[1024,1408]{0,1:T(8,128)(2,1)S(1)} %bitcast.164, bf16[1,1408,512]{2,1,0:T(8,128)(2,1)S(1)} %copy-done), kind=kOutput, calls=%fused_computation.51 | convolution fusion | flops 1476919296 | bytes 5373952 | tf_op jit(solution)/shard_map/dot_general | solution.py:78
  211.0 5.9 %all-to-all-start.6 = ((bf16[64,16,512]{2,1,0:T(8,128)(2,1)}), bf16[64,16,512]{2,1,0:T(8,128)(2,1)S(1)}, u32[]{:S(2)}, u32[]{:S(2)}) async-start(bf16[64,16,512]{2,1,0:T(8,128)(2,1)} %bitcast.34), calls=%async_computation.6 | async-start | bytes 2097152 | tf_op jit(solution)/shard_map/all_to_all | solution.py:84
  217.1 4.0 %fusion.37 = f32[128,704]{0,1:T(8,128)} fusion(bf16[128,2048]{0,1:T(8,128)(2,1)S(1)} %copy-done.6, bf16[2048,2112]{1,0:T(8,128)(2,1)} %all-gather.2.cloned.1.call-done), kind=kOutput, calls=%fused_computation.46 | convolution fusion | flops 369098752 | bytes 4030464 | tf_op jit(solution)/shard_map/dot_general | solution.py:92
  221.1 7.4 %fusion.40 = bf16[128,2048]{1,0:T(8,128)(2,1)S(1)} fusion(bf16[2048,2112]{1,0:T(8,128)(2,1)} %all-gather.2.cloned.1.call-done, bf16[128,2048]{0,1:T(8,128)(2,1)S(1)} %copy-done.6, f32[128,704]{0,1:T(8,128)} %fusion.37), kind=kOutput, calls=%fused_computation.50 | convolution fusion | flops 739000320 | bytes 7700480 | tf_op jit(solution)/shard_map/th,dh->td/dot_general | solution.py:99
  228.5 0.9 copy.73
  229.3 15.5 %all-to-all-done.6 = bf16[64,16,512]{2,1,0:T(8,128)(2,1)S(1)} async-done(((bf16[64,16,512]{2,1,0:T(8,128)(2,1)}), bf16[64,16,512]{2,1,0:T(8,128)(2,1)S(1)}, u32[]{:S(2)}, u32[]{:S(2)}) %all-to-all-start.6) | async-done | bytes 1048608 | tf_op jit(solution)/shard_map/all_to_all | solution.py:84
  244.9 4.1 %all-to-all-start.3 = ((bf16[4,128,512]{2,1,0:T(8,128)(2,1)}), bf16[4,128,512]{2,1,0:T(8,128)(2,1)}, u32[]{:S(2)}, u32[]{:S(2)}) async-start(bf16[4,128,512]{2,1,0:T(8,128)(2,1)} %bitcast.126), calls=%async_computation.3 | async-start | bytes 1048576 | tf_op jit(solution)/shard_map/all_to_all | solution.py:67
  249.1 2.7 %gather_fusion.1 = bf16[768,512]{1,0:T(8,128)(2,1)S(1)} fusion(bf16[1024,512]{1,0:T(8,128)(2,1)S(1)} %bitcast.157, s32[1024]{0:T(1024)S(1)} %pad_clamp_fusion.1), kind=kCustom, calls=%fused_computation.1 | custom fusion | bytes 1575936 | tf_op jit(solution)/shard_map/gather | solution.py:177
  252.1 1.0 fusion.80
  253.1 6.1 %all-to-all-done.3 = bf16[4,128,512]{2,1,0:T(8,128)(2,1)} async-done(((bf16[4,128,512]{2,1,0:T(8,128)(2,1)}), bf16[4,128,512]{2,1,0:T(8,128)(2,1)}, u32[]{:S(2)}, u32[]{:S(2)}) %all-to-all-start.3) | async-done | bytes 524320 | tf_op jit(solution)/shard_map/all_to_all | solution.py:67
  259.2 1.1 convert_reduce_fusion
  260.4 0.7 fusion.65
  (89 shorter events, 3.6 us)
Async XLA Ops:
  6.5 201.7 %copy-start = (bf16[1,1408,512]{2,1,0:T(8,128)(2,1)S(1)}, bf16[1,1408,512]{2,1,0:T(8,128)(2,1)}, u32[]{:S(2)}) copy-start(bf16[1,1408,512]{2,1,0:T(8,128)(2,1)} %param.32) | copy-start | bytes 4325380
  15.7 0.7 copy-start.20
  15.8 1.9 copy-start.1
  15.9 2.6 copy-start.4
  15.9 2.6 copy-start.7
  19.6 1.0 copy-start.9
  19.6 1.0 copy-start.14
  20.8 0.7 copy-start.10
  24.9 0.7 copy-start.20
  24.9 1.9 copy-start.1
  25.1 2.6 copy-start.4
  25.1 2.6 copy-start.7
  28.8 1.0 copy-start.9
  28.8 1.0 copy-start.14
  30.0 0.7 copy-start.10
  35.2 7.0 %copy-start.16 = (s32[128,6]{0,1:T(8,128)S(1)}, s32[128,6]{0,1:T(8,128)}, u32[]{:S(2)}) copy-start(s32[128,6]{0,1:T(8,128)} %param.28) | copy-start | bytes 9220
  37.9 19.4 %all-to-all-start = ((f32[4,128,512]{2,1,0:T(8,128)}), f32[4,128,512]{2,1,0:T(8,128)S(1)}, u32[]{:S(2)}, u32[]{:S(2)}) async-start(f32[4,128,512]{2,1,0:T(8,128)} %convolution_bitcast_fusion), calls=%async_computation | async-start | bytes 2097152 | tf_op jit(solution)/shard_map/all_to_all | solution.py:67
  42.7 29.0 %copy-start.15 = (f32[2048]{0:T(1024)S(1)}, f32[2048]{0:T(1024)}, u32[]{:S(2)}) copy-start(f32[2048]{0:T(1024)} %param.27) | copy-start | bytes 24580
  58.4 1.0 copy-start.2
  59.4 12.0 %all-to-all-start.1 = ((bf16[4,128,512]{1,2,0:T(8,128)(2,1)}), bf16[4,128,512]{1,2,0:T(8,128)(2,1)S(1)}, u32[]{:S(2)}, u32[]{:S(2)}) async-start(bf16[4,128,512]{1,2,0:T(8,128)(2,1)} %broadcast_in_dim.61), calls=%async_computation.1 | async-start | bytes 1048576 | tf_op jit(solution)/shard_map/all_to_all | solution.py:56
  62.8 23.2 %copy-start.11 = (bf16[32,704]{1,0:T(8,128)(2,1)S(1)}, bf16[32,704]{1,0:T(8,128)(2,1)}, u32[]{:S(2)}) copy-start(bf16[32,704]{1,0:T(8,128)(2,1)} %param.33) | copy-start | bytes 135172
  62.8 23.2 %copy-start.12 = (bf16[32,704]{1,0:T(8,128)(2,1)S(1)}, bf16[32,704]{1,0:T(8,128)(2,1)}, u32[]{:S(2)}) copy-start(bf16[32,704]{1,0:T(8,128)(2,1)} %param.34) | copy-start | bytes 135172
  62.9 23.2 %copy-start.13 = (bf16[704,32]{0,1:T(8,128)(2,1)S(1)}, bf16[704,32]{0,1:T(8,128)(2,1)}, u32[]{:S(2)}) copy-start(bf16[704,32]{0,1:T(8,128)(2,1)} %param.35) | copy-start | bytes 135172
  72.0 0.8 copy-start.5
  74.2 39.7 %all-to-all-start.2 = ((bf16[64,16,512]{2,1,0:T(8,128)(2,1)}), bf16[64,16,512]{2,1,0:T(8,128)(2,1)S(1)}, u32[]{:S(2)}, u32[]{:S(2)}) async-start(bf16[64,16,512]{2,1,0:T(8,128)(2,1)} %bitcast.23), calls=%async_computation.2 | async-start | bytes 2097152 | tf_op jit(solution)/shard_map/all_to_all | solution.py:165
  86.0 131.1 %all-gather.2.cloned.1.call-start = ((), (), s32[]{:S(2)}) async-start(), calls=%async_computation.7 | async-start | bytes 9052160 | tf_op jit(solution)/shard_map/all_gather | solution.py:91
  115.0 52.2 %copy-start.18 = (bf16[1,2048,352]{1,2,0:T(8,128)(2,1)S(1)}, bf16[1,2048,352]{1,2,0:T(8,128)(2,1)}, u32[]{:S(2)}) copy-start(bf16[1,2048,352]{1,2,0:T(8,128)(2,1)} %param.30) | copy-start | bytes 4325380
  167.2 1.7 copy-start.19
  208.2 8.7 %copy-start.8 = (s32[128,6]{1,0:T(8,128)S(1)}, s32[128,6]{1,0:T(8,128)}, u32[]{:S(2)}) copy-start(s32[128,6]{1,0:T(8,128)} %get-tuple-element.79) | copy-start | bytes 9220
  208.2 8.9 %copy-start.6 = (bf16[128,2048]{0,1:T(8,128)(2,1)S(1)}, bf16[128,2048]{0,1:T(8,128)(2,1)}, u32[]{:S(2)}) copy-start(bf16[128,2048]{0,1:T(8,128)(2,1)} %copy-done.5) | copy-start | bytes 1572868
  211.0 33.8 %all-to-all-start.6 = ((bf16[64,16,512]{2,1,0:T(8,128)(2,1)}), bf16[64,16,512]{2,1,0:T(8,128)(2,1)S(1)}, u32[]{:S(2)}, u32[]{:S(2)}) async-start(bf16[64,16,512]{2,1,0:T(8,128)(2,1)} %bitcast.34), calls=%async_computation.6 | async-start | bytes 2097152 | tf_op jit(solution)/shard_map/all_to_all | solution.py:84
  221.1 27.9 %copy-start.17 = (f32[128,6]{0,1:T(8,128)S(1)}, f32[128,6]{0,1:T(8,128)}, u32[]{:S(2)}) copy-start(f32[128,6]{0,1:T(8,128)} %param.29) | copy-start | bytes 9220
  244.9 14.4 %all-to-all-start.3 = ((bf16[4,128,512]{2,1,0:T(8,128)(2,1)}), bf16[4,128,512]{2,1,0:T(8,128)(2,1)}, u32[]{:S(2)}, u32[]{:S(2)}) async-start(bf16[4,128,512]{2,1,0:T(8,128)(2,1)} %bitcast.126), calls=%async_computation.3 | async-start | bytes 1048576 | tf_op jit(solution)/shard_map/all_to_all | solution.py:67
  251.8 8.5 %copy-start.3 = (bf16[128,512]{1,0:T(8,128)(2,1)S(1)}, bf16[128,512]{1,0:T(8,128)(2,1)}, u32[]{:S(2)}) copy-start(bf16[128,512]{1,0:T(8,128)(2,1)} %copy-done.2) | copy-start | bytes 393220
Sparse Core Ops, SparseCore 0:
  114.1 79.5 all-gather.1

commit v6 on v5

--- a/solution.py
+++ b/solution.py
@@ -16,38 +16,42 @@
 def attend_requests(
     queries, tree_keys, tree_values, tree_allow, kv_cache, page_table, cache_len, score_scale
 ):
-
-    def per_request(request_item):
-        q_rows, own_keys, own_values, allow_rows, table_row, length = request_item
-        kv_pages = kv_cache[table_row]
-        cache_keys = kv_pages[:, 0].reshape(-1, kv_pages.shape[-1])
-        cache_values = kv_pages[:, 1].reshape(-1, kv_pages.shape[-1])
-        live_mask = (jnp.arange(cache_keys.shape[0], dtype=jnp.int32) < length)[None, :]
-        cache_scores = (
-            jnp.einsum("qd,kd->qk", q_rows, cache_keys, preferred_element_type=jnp.float32)
-            * score_scale
-        )
-        cache_scores = jnp.where(live_mask, cache_scores, NEGATIVE_FILL)
-        tree_scores = (
-            jnp.einsum("qd,ud->qu", q_rows, own_keys, preferred_element_type=jnp.float32)
-            * score_scale
-        )
-        tree_scores = jnp.where(allow_rows, tree_scores, NEGATIVE_FILL)
-        row_peak = jnp.maximum(jnp.max(cache_scores, axis=1), jnp.max(tree_scores, axis=1))[:, None]
-        cache_probs = jnp.where(live_mask, jnp.exp(cache_scores - row_peak), 0.0)
-        tree_probs = jnp.where(allow_rows, jnp.exp(tree_scores - row_peak), 0.0)
-        denom_sum = jnp.sum(cache_probs, axis=1) + jnp.sum(tree_probs, axis=1)
-        weighted = jnp.dot(
-            cache_probs.astype(jnp.bfloat16), cache_values, preferred_element_type=jnp.float32
-        )
-        weighted = weighted + jnp.dot(
-            tree_probs.astype(jnp.bfloat16), own_values, preferred_element_type=jnp.float32
-        )
-        return (weighted / denom_sum[:, None]).astype(jnp.bfloat16)
-
-    return lax.map(
-        per_request, (queries, tree_keys, tree_values, tree_allow, page_table, cache_len)
-    )
+    pool_pages, _, page_rows, head_width = kv_cache.shape
+    pool_keys = kv_cache[:, 0].reshape(pool_pages * page_rows, head_width)
+    pool_values = kv_cache[:, 1].reshape(pool_pages * page_rows, head_width)
+    page_start = jnp.arange(page_table.shape[1], dtype=jnp.int32) * page_rows
+    rows_left = cache_len[:, None] - page_start[None, :]
+    live_rows = jnp.where(rows_left > 0, jnp.minimum(rows_left, page_rows), 0)
+    slot_ids = jnp.arange(pool_pages, dtype=jnp.int32)
+    owns = page_table[:, :, None] == slot_ids[None, None, :]
+    slot_rows = jnp.sum(jnp.where(owns, live_rows[:, :, None], 0), axis=1)
+    row_ids = jnp.arange(page_rows, dtype=jnp.int32)
+    live_mask = (row_ids[None, None, :] < slot_rows[:, :, None]).reshape(
+        cache_len.shape[0], 1, pool_pages * page_rows
+    )
+    cache_scores = (
+        jnp.einsum("rqd,kd->rqk", queries, pool_keys, preferred_element_type=jnp.float32)
+        * score_scale
+    )
+    cache_scores = jnp.where(live_mask, cache_scores, NEGATIVE_FILL)
+    tree_scores = (
+        jnp.einsum("rqd,rud->rqu", queries, tree_keys, preferred_element_type=jnp.float32)
+        * score_scale
+    )
+    tree_scores = jnp.where(tree_allow, tree_scores, NEGATIVE_FILL)
+    row_peak = jnp.maximum(jnp.max(cache_scores, axis=2), jnp.max(tree_scores, axis=2))[..., None]
+    cache_probs = jnp.where(live_mask, jnp.exp(cache_scores - row_peak), 0.0)
+    tree_probs = jnp.where(tree_allow, jnp.exp(tree_scores - row_peak), 0.0)
+    denom_sum = jnp.sum(cache_probs, axis=2) + jnp.sum(tree_probs, axis=2)
+    weighted = jnp.einsum(
+        "rqk,kd->rqd", cache_probs.astype(jnp.bfloat16), pool_values,
+        preferred_element_type=jnp.float32,
+    )
+    weighted = weighted + jnp.einsum(
+        "rqu,rud->rqd", tree_probs.astype(jnp.bfloat16), tree_values,
+        preferred_element_type=jnp.float32,
+    )
+    return (weighted / denom_sum[..., None]).astype(jnp.bfloat16)
 
 
 def gather_mp(block, axis):

time: 269 us -> 258 us (0.959)
  local copies, waits for them, and re-layouts: 27.6 us -> 16.2 us
    gather x2 -> x0, local copies, waits for them, and re-layouts: 5.38 us -> none  [per_request(): kv_pages = kv_cache[table_row]]
    slice x3 -> x2, local copies, waits for them, and re-layouts: 0.55 us -> 3.33 us  [the longest x1 3.05 us: attend_requests(): pool_keys = kv_cache[:, 0].reshape(pool_pages * page_rows, head_width)]
where the time goes in v6:
time: 258 us; the launch traced here: 257 us
  blocking collectives  89.3 us (35%)
  waiting for transfers between devices  68.3 us (26%)
  starting transfers between devices  29.7 us (12%)
  matrix products  28.1 us (11%)
  local copies, waits for them, and re-layouts  16.2 us (6%)
  between operations  13.9 us (5%)
  other arithmetic  11.3 us (4%)
    all_to_all x2, blocking collectives, gather_mp(): lax.all_to_all(copies, 'mp', split_axis=0, concat_axis=0, tiled=True)  89.3 us
    all_to_all x1, waiting for transfers between devices, on_device(): lax.all_to_all(buffer, 'dp', split_axis=0, concat_axis=0, tiled=True)  27.1 us
    all_to_all x2, waiting for transfers between devices, scatter_sum_mp(): lax.all_to_all(blocks, 'mp', split_axis=0, concat_axis=0, tiled=True)  18.7 us
    all_to_all x1, waiting for transfers between devices, run_experts(): lax.all_to_all(outputs, 'dp', split_axis=0, concat_axis=0, tiled=True)  15.4 us
    all_to_all x1, starting transfers between devices, on_device(): lax.all_to_all(buffer, 'dp', split_axis=0, concat_axis=0, tiled=True)  11.8 us
    all_to_all x2, starting transfers between devices, scatter_sum_mp(): lax.all_to_all(blocks, 'mp', split_axis=0, concat_axis=0, tiled=True)  8.42 us
    dot_general x1, matrix products, shared_experts(): jnp.einsum('th,dh->td', shared_hidden, gathered[:, 2 * hidden_width:], pr...  7.37 us
    all_to_all x1, waiting for transfers between devices, gather_mp(): lax.all_to_all(copies, 'mp', split_axis=0, concat_axis=0, tiled=True)  7.05 us
  transfers between devices with their start and end apart: 6, of which 5 were waited for; matrix products, arithmetic and copies ran while one was open for 11% of the time, Pallas kernels for 0%

profile of v6, /device:TPU:32, one launch (start us, length us, event | category | flops | bytes accessed | tf_op | source)
XLA Modules:
  0.0 256.8 jit_solution(10157943678279274435)
XLA Ops:
  6.6 0.9 compare_select_fusion.1
  7.4 0.8 select_reduce_fusion
  8.2 0.1 broadcast_bitcast_fusion
  8.3 3.1 %fusion.61 = (bf16[40,1,128,128]{3,2,1,0:T(8,128)(2,1)S(1)}, bf16[40,1,128,128]{3,2,1,0:T(8,128)(2,1)}) fusion(bf16[40,2,128,128]{3,2,1,0:T(8,128)(2,1)} %param.19), kind=kLoop, calls=%fused_computation.84 | loop fusion | bytes 5242880 | tf_op jit(solution)/shard_map/slice | solution.py:20
  11.4 0.1 copy.50
  11.5 0.1 tile.2
  11.6 0.2 eq.66
  11.8 0.1 fusion.62
  11.9 1.8 fusion
  13.8 0.2 fusion.63
  14.0 2.9 %fusion.1 = f32[2,256]{1,0:T(2,128)S(1)} fusion(f32[2,256,5120]{2,1,0:T(8,128)S(1)} %get-tuple-element.14, f32[2,256]{1,0:T(2,128)S(1)} %max.7, pred[2,5120]{1,0:T(4,128)(4,1)S(1)} %bitcast_compare_fusion), kind=kLoop, calls=%fused_computation.4 | loop fusion | flops 13106688 | bytes 10500096 | tf_op jit(solution)/shard_map/reduce_sum | solution.py:45
  16.9 3.0 %fusion.3 = f32[2,256,128]{2,1,0:T(8,128)S(1)} fusion(bf16[5120,128,1]{1,0,2:T(8,128)(2,1)S(1)} %bitcast.111, f32[2,256,5120]{2,1,0:T(8,128)S(1)} %get-tuple-element.14, f32[2,256]{1,0:T(2,128)S(1)} %max.7, pred[2,5120]{1,0:T(4,128)(4,1)S(1)} %bitcast_compare_fusion), kind=kOutput, calls=%fused_computation.6 | convolution fusion | flops 684195840 | bytes 12070912 | tf_op jit(solution)/shard_map/rqk,kd->rqd/dot_general | solution.py:46
  19.9 0.2 fusion.32
  20.2 0.1 copy.53
  20.3 0.7 reshape.189
  21.0 2.9 %copy.65 = bf16[2048,512]{1,0:T(8,128)(2,1)S(1)} copy(bf16[2048,512]{0,1:T(8,128)(2,1)} %bitcast.110) | data formatting | bytes 4194304 | tf_op jit(solution)/shard_map/dot_general | solution.py:147
  23.9 2.7 %convolution_bitcast_fusion = f32[4,128,512]{2,1,0:T(8,128)} fusion(bf16[128,512,1]{1,0,2:T(8,128)(2,1)} %reshape.189, bf16[4,512,512]{2,1,0:T(8,128)(2,1)S(1)} %bitcast.104), kind=kOutput, calls=%fused_computation.25 | convolution fusion | flops 268435456 | bytes 3276800 | tf_op jit(solution)/shard_map/dot_general | solution.py:147
  26.6 4.3 %all-to-all-start = ((f32[4,128,512]{2,1,0:T(8,128)}), f32[4,128,512]{2,1,0:T(8,128)S(1)}, u32[]{:S(2)}, u32[]{:S(2)}) async-start(f32[4,128,512]{2,1,0:T(8,128)} %convolution_bitcast_fusion), calls=%async_computation | async-start | bytes 2097152 | tf_op jit(solution)/shard_map/all_to_all | solution.py:71
  30.9 0.1 copy.56
  31.0 0.1 eq.71
  31.1 0.1 eq.67
  31.3 1.8 reduce-window.6
  33.1 0.3 slice_reduce_fusion
  33.4 12.6 %all-to-all-done = f32[4,128,512]{2,1,0:T(8,128)S(1)} async-done(((f32[4,128,512]{2,1,0:T(8,128)}), f32[4,128,512]{2,1,0:T(8,128)S(1)}, u32[]{:S(2)}, u32[]{:S(2)}) %all-to-all-start) | async-done | bytes 1048608 | tf_op jit(solution)/shard_map/all_to_all | solution.py:71
  46.0 0.1 reduce_sum.70
  46.1 0.9 add_convert_fusion
  47.0 0.1 copy.55
  47.1 0.9 broadcast_in_dim.79
  48.0 3.6 %all-to-all-start.1 = ((bf16[4,128,512]{1,2,0:T(8,128)(2,1)}), bf16[4,128,512]{1,2,0:T(8,128)(2,1)S(1)}, u32[]{:S(2)}, u32[]{:S(2)}) async-start(bf16[4,128,512]{1,2,0:T(8,128)(2,1)} %broadcast_in_dim.79), calls=%async_computation.1 | async-start | bytes 1048576 | tf_op jit(solution)/shard_map/all_to_all | solution.py:60
  51.6 0.1 fusion.44
  51.8 0.1 reduce_sum.73
  51.9 0.6 broadcast_multiply_fusion
  52.5 0.1 copy.60
  52.6 0.5 fusion.12
  53.1 7.0 %all-to-all-done.1 = bf16[4,128,512]{1,2,0:T(8,128)(2,1)S(1)} async-done(((bf16[4,128,512]{1,2,0:T(8,128)(2,1)}), bf16[4,128,512]{1,2,0:T(8,128)(2,1)S(1)}, u32[]{:S(2)}, u32[]{:S(2)}) %all-to-all-start.1) | async-done | bytes 524320 | tf_op jit(solution)/shard_map/all_to_all | solution.py:60
  60.2 0.3 multiply_reduce_fusion
  60.5 0.3 fusion.35
  60.8 0.8 copy-done.4
  61.6 1.4 convolution_convert_fusion.1
  63.1 11.8 %all-to-all-start.2 = ((bf16[64,16,512]{2,1,0:T(8,128)(2,1)}), bf16[64,16,512]{2,1,0:T(8,128)(2,1)S(1)}, u32[]{:S(2)}, u32[]{:S(2)}) async-start(bf16[64,16,512]{2,1,0:T(8,128)(2,1)} %bitcast.18), calls=%async_computation.2 | async-start | bytes 2097152 | tf_op jit(solution)/shard_map/all_to_all | solution.py:169
  74.9 0.8 concatenate.3
  75.7 27.1 %all-to-all-done.2 = bf16[64,16,512]{2,1,0:T(8,128)(2,1)S(1)} async-done(((bf16[64,16,512]{2,1,0:T(8,128)(2,1)}), bf16[64,16,512]{2,1,0:T(8,128)(2,1)S(1)}, u32[]{:S(2)}, u32[]{:S(2)}) %all-to-all-start.2) | async-done | bytes 1048608 | tf_op jit(solution)/shard_map/all_to_all | solution.py:169
  102.8 0.5 copy.62
  103.3 0.5 broadcast_in_dim.81
  103.9 52.2 %all_to_all.35 = bf16[4,1024,512]{1,2,0:T(8,128)(2,1)S(1)} all-to-all(bf16[4,1024,512]{1,2,0:T(8,128)(2,1)S(1)} %broadcast_in_dim.81), channel_id=1, replica_groups=mesh['dp'=64,'mp'=4] {'mp'}, dimensions={0} | all-to-all | bytes 8388608 | tf_op jit(solution)/shard_map/all_to_all | solution.py:60
  156.1 1.7 fusion.18
  157.8 1.8 fusion.20
  159.6 0.4 broadcast_in_dim.82
  160.0 37.1 %all_to_all.36 = bf16[4,1024,352]{1,2,0:T(8,128)(2,1)S(1)} all-to-all(bf16[4,1024,352]{1,2,0:T(8,128)(2,1)S(1)} %broadcast_in_dim.82), channel_id=1, replica_groups=mesh['dp'=64,'mp'=4] {'mp'}, dimensions={0} | all-to-all | bytes 5767168 | tf_op jit(solution)/shard_map/all_to_all | solution.py:60
  197.1 2.8 %convolution_convert_fusion = bf16[1024,512]{1,0:T(8,128)(2,1)} fusion(bf16[1024,1408]{0,1:T(8,128)(2,1)S(1)} %bitcast.109, bf16[1,1408,512]{2,1,0:T(8,128)(2,1)S(1)} %copy-done), kind=kOutput, calls=%fused_computation.17 | convolution fusion | flops 1476919296 | bytes 5373952 | tf_op jit(solution)/shard_map/dot_general | solution.py:82
  199.9 5.9 %all-to-all-start.6 = ((bf16[64,16,512]{2,1,0:T(8,128)(2,1)}), bf16[64,16,512]{2,1,0:T(8,128)(2,1)S(1)}, u32[]{:S(2)}, u32[]{:S(2)}) async-start(bf16[64,16,512]{2,1,0:T(8,128)(2,1)} %bitcast.29), calls=%async_computation.6 | async-start | bytes 2097152 | tf_op jit(solution)/shard_map/all_to_all | solution.py:88
  205.8 0.1 mul.97
  206.0 4.0 %fusion.10 = f32[128,704]{0,1:T(8,128)} fusion(bf16[128,2048]{0,1:T(8,128)(2,1)S(1)} %copy-done.5, bf16[2048,2112]{1,0:T(8,128)(2,1)} %all-gather.2.cloned.1.call-done), kind=kOutput, calls=%fused_computation.12 | convolution fusion | flops 369098752 | bytes 4030464 | tf_op jit(solution)/shard_map/dot_general | solution.py:96
  210.0 7.4 %fusion.13 = bf16[128,2048]{1,0:T(8,128)(2,1)S(1)} fusion(bf16[2048,2112]{1,0:T(8,128)(2,1)} %all-gather.2.cloned.1.call-done, bf16[128,2048]{0,1:T(8,128)(2,1)S(1)} %copy-done.5, f32[128,704]{0,1:T(8,128)} %fusion.10), kind=kOutput, calls=%fused_computation.16 | convolution fusion | flops 739000320 | bytes 7700480 | tf_op jit(solution)/shard_map/th,dh->td/dot_general | solution.py:103
  217.4 0.9 copy.75
  218.3 15.4 %all-to-all-done.6 = bf16[64,16,512]{2,1,0:T(8,128)(2,1)S(1)} async-done(((bf16[64,16,512]{2,1,0:T(8,128)(2,1)}), bf16[64,16,512]{2,1,0:T(8,128)(2,1)S(1)}, u32[]{:S(2)}, u32[]{:S(2)}) %all-to-all-start.6) | async-done | bytes 1048608 | tf_op jit(solution)/shard_map/all_to_all | solution.py:88
  233.7 4.1 %all-to-all-start.3 = ((bf16[4,128,512]{2,1,0:T(8,128)(2,1)}), bf16[4,128,512]{2,1,0:T(8,128)(2,1)}, u32[]{:S(2)}, u32[]{:S(2)}) async-start(bf16[4,128,512]{2,1,0:T(8,128)(2,1)} %bitcast.101), calls=%async_computation.3 | async-start | bytes 1048576 | tf_op jit(solution)/shard_map/all_to_all | solution.py:71
  237.9 0.1 copy.63
  238.0 2.7 %gather_fusion = bf16[768,512]{1,0:T(8,128)(2,1)S(1)} fusion(bf16[1024,512]{1,0:T(8,128)(2,1)S(1)} %bitcast.103, s32[1024]{0:T(1024)S(1)} %pad_clamp_fusion), kind=kCustom, calls=%fused_computation | custom fusion | bytes 1575936 | tf_op jit(solution)/shard_map/gather | solution.py:181
  240.7 0.3 reshape.177
  241.0 1.0 fusion.64
  241.9 6.1 %all-to-all-done.3 = bf16[4,128,512]{2,1,0:T(8,128)(2,1)} async-done(((bf16[4,128,512]{2,1,0:T(8,128)(2,1)}), bf16[4,128,512]{2,1,0:T(8,128)(2,1)}, u32[]{:S(2)}, u32[]{:S(2)}) %all-to-all-start.3) | async-done | bytes 524320 | tf_op jit(solution)/shard_map/all_to_all | solution.py:71
  248.1 1.1 convert_reduce_fusion
  249.2 0.7 fusion.41
  (54 shorter events, 0.4 us)
Async XLA Ops:
  6.5 190.5 %copy-start = (bf16[1,1408,512]{2,1,0:T(8,128)(2,1)S(1)}, bf16[1,1408,512]{2,1,0:T(8,128)(2,1)}, u32[]{:S(2)}) copy-start(bf16[1,1408,512]{2,1,0:T(8,128)(2,1)} %param.30) | copy-start | bytes 4325380
  6.5 4.8 %copy-start.8 = (bf16[128,512]{1,0:T(8,128)(2,1)S(1)}, bf16[128,512]{1,0:T(8,128)(2,1)}, u32[]{:S(2)}) copy-start(bf16[128,512]{1,0:T(8,128)(2,1)} %param.17) | copy-start | bytes 393220
  6.5 4.8 %copy-start.9 = (s32[2,64,64]{2,1,0:T(8,128)S(1)}, s32[2,64,64]{2,1,0:T(8,128)}, u32[]{:S(2)}) copy-start(s32[2,64,64]{2,1,0:T(8,128)} %param.22) | copy-start | bytes 98308
  6.5 5.2 %copy-start.6 = (bf16[128,2,128]{2,1,0:T(2,128)(2,1)S(1)}, bf16[128,2,128]{2,1,0:T(2,128)(2,1)}, u32[]{:S(2)}) copy-start(bf16[128,2,128]{2,1,0:T(2,128)(2,1)} %param.18) | copy-start | bytes 196612
  14.0 3.0 %copy-start.1 = (bf16[40,1,128,128]{3,2,1,0:T(8,128)(2,1)S(1)}, bf16[40,1,128,128]{3,2,1,0:T(8,128)(2,1)}, u32[]{:S(2)}) copy-start(bf16[40,1,128,128]{3,2,1,0:T(8,128)(2,1)} %get-tuple-element.8) | copy-start | bytes 3932164
  23.9 7.0 %copy-start.14 = (s32[128,6]{0,1:T(8,128)S(1)}, s32[128,6]{0,1:T(8,128)}, u32[]{:S(2)}) copy-start(s32[128,6]{0,1:T(8,128)} %param.26) | copy-start | bytes 9220
  26.6 19.4 %all-to-all-start = ((f32[4,128,512]{2,1,0:T(8,128)}), f32[4,128,512]{2,1,0:T(8,128)S(1)}, u32[]{:S(2)}, u32[]{:S(2)}) async-start(f32[4,128,512]{2,1,0:T(8,128)} %convolution_bitcast_fusion), calls=%async_computation | async-start | bytes 2097152 | tf_op jit(solution)/shard_map/all_to_all | solution.py:71
  30.9 29.6 %copy-start.13 = (f32[2048]{0:T(1024)S(1)}, f32[2048]{0:T(1024)}, u32[]{:S(2)}) copy-start(f32[2048]{0:T(1024)} %param.25) | copy-start | bytes 24580
  47.0 1.0 copy-start.2
  48.0 26.9 %copy-start.10 = (bf16[32,704]{1,0:T(8,128)(2,1)S(1)}, bf16[32,704]{1,0:T(8,128)(2,1)}, u32[]{:S(2)}) copy-start(bf16[32,704]{1,0:T(8,128)(2,1)} %param.31) | copy-start | bytes 135172
  48.0 26.9 %copy-start.11 = (bf16[32,704]{1,0:T(8,128)(2,1)S(1)}, bf16[32,704]{1,0:T(8,128)(2,1)}, u32[]{:S(2)}) copy-start(bf16[32,704]{1,0:T(8,128)(2,1)} %param.32) | copy-start | bytes 135172
  48.0 26.9 %copy-start.12 = (bf16[704,32]{0,1:T(8,128)(2,1)S(1)}, bf16[704,32]{0,1:T(8,128)(2,1)}, u32[]{:S(2)}) copy-start(bf16[704,32]{0,1:T(8,128)(2,1)} %param.33) | copy-start | bytes 135172
  48.0 12.2 %all-to-all-start.1 = ((bf16[4,128,512]{1,2,0:T(8,128)(2,1)}), bf16[4,128,512]{1,2,0:T(8,128)(2,1)S(1)}, u32[]{:S(2)}, u32[]{:S(2)}) async-start(bf16[4,128,512]{1,2,0:T(8,128)(2,1)} %broadcast_in_dim.79), calls=%async_computation.1 | async-start | bytes 1048576 | tf_op jit(solution)/shard_map/all_to_all | solution.py:60
  60.8 0.8 copy-start.4
  63.1 39.7 %all-to-all-start.2 = ((bf16[64,16,512]{2,1,0:T(8,128)(2,1)}), bf16[64,16,512]{2,1,0:T(8,128)(2,1)S(1)}, u32[]{:S(2)}, u32[]{:S(2)}) async-start(bf16[64,16,512]{2,1,0:T(8,128)(2,1)} %bitcast.18), calls=%async_computation.2 | async-start | bytes 2097152 | tf_op jit(solution)/shard_map/all_to_all | solution.py:169
  74.8 131.1 %all-gather.2.cloned.1.call-start = ((), (), s32[]{:S(2)}) async-start(), calls=%async_computation.7 | async-start | bytes 9052160 | tf_op jit(solution)/shard_map/all_gather | solution.py:95
  103.9 52.2 %copy-start.16 = (bf16[1,2048,352]{1,2,0:T(8,128)(2,1)S(1)}, bf16[1,2048,352]{1,2,0:T(8,128)(2,1)}, u32[]{:S(2)}) copy-start(bf16[1,2048,352]{1,2,0:T(8,128)(2,1)} %param.28) | copy-start | bytes 4325380
  156.1 1.7 copy-start.17
  197.1 8.7 %copy-start.7 = (s32[128,6]{1,0:T(8,128)S(1)}, s32[128,6]{1,0:T(8,128)}, u32[]{:S(2)}) copy-start(s32[128,6]{1,0:T(8,128)} %get-tuple-element.9) | copy-start | bytes 9220
  197.1 8.9 %copy-start.5 = (bf16[128,2048]{0,1:T(8,128)(2,1)S(1)}, bf16[128,2048]{0,1:T(8,128)(2,1)}, u32[]{:S(2)}) copy-start(bf16[128,2048]{0,1:T(8,128)(2,1)} %copy-done.4) | copy-start | bytes 1572868
  199.9 33.8 %all-to-all-start.6 = ((bf16[64,16,512]{2,1,0:T(8,128)(2,1)}), bf16[64,16,512]{2,1,0:T(8,128)(2,1)S(1)}, u32[]{:S(2)}, u32[]{:S(2)}) async-start(bf16[64,16,512]{2,1,0:T(8,128)(2,1)} %bitcast.29), calls=%async_computation.6 | async-start | bytes 2097152 | tf_op jit(solution)/shard_map/all_to_all | solution.py:88
  210.0 27.9 %copy-start.15 = (f32[128,6]{0,1:T(8,128)S(1)}, f32[128,6]{0,1:T(8,128)}, u32[]{:S(2)}) copy-start(f32[128,6]{0,1:T(8,128)} %param.27) | copy-start | bytes 9220
  233.7 14.4 %all-to-all-start.3 = ((bf16[4,128,512]{2,1,0:T(8,128)(2,1)}), bf16[4,128,512]{2,1,0:T(8,128)(2,1)}, u32[]{:S(2)}, u32[]{:S(2)}) async-start(bf16[4,128,512]{2,1,0:T(8,128)(2,1)} %bitcast.101), calls=%async_computation.3 | async-start | bytes 1048576 | tf_op jit(solution)/shard_map/all_to_all | solution.py:71
  240.7 8.5 %copy-start.3 = (bf16[128,512]{1,0:T(8,128)(2,1)S(1)}, bf16[128,512]{1,0:T(8,128)(2,1)}, u32[]{:S(2)}) copy-start(bf16[128,512]{1,0:T(8,128)(2,1)} %copy-done.2) | copy-start | bytes 393220
Sparse Core Ops, SparseCore 0:
  102.9 79.5 all-gather.1

commit v7 on v6

--- a/solution.py
+++ b/solution.py
@@ -4,6 +4,7 @@
 from jax.sharding import PartitionSpec as P
 
 NEGATIVE_FILL = -1e30
+DP = ("dpo", "core")
 EPSILON = 1e-05
 
 
@@ -72,6 +73,16 @@
     return jnp.sum(pieces.astype(jnp.float32), axis=0)
 
 
+def exchange_dp(blocks):
+    cores = lax.axis_size("core")
+    chips = lax.axis_size("dpo")
+    rest = blocks.shape[1:]
+    split = blocks.reshape((chips, cores) + rest)
+    split = lax.all_to_all(split, "core", split_axis=1, concat_axis=1, tiled=True)
+    split = lax.all_to_all(split, "dpo", split_axis=0, concat_axis=0, tiled=True)
+    return split.reshape(blocks.shape)
+
+
 def run_experts(rows, w_gate, w_up, w_down):
     source_count, slot_count, model_width = rows.shape
     flat_rows = rows.reshape(source_count * slot_count, model_width)
@@ -85,14 +96,14 @@
         preferred_element_type=jnp.float32,
     )
     outputs = summed.astype(jnp.bfloat16).reshape(source_count, slot_count, w_down.shape[2])
-    return lax.all_to_all(outputs, "dp", split_axis=0, concat_axis=0, tiled=True)
+    return exchange_dp(outputs)
 
 
 def shared_experts(normed_rows, shared_gate, shared_up, shared_down, after):
     hidden_width = shared_gate.shape[1]
     packed = jnp.concatenate([shared_gate, shared_up, shared_down.T], axis=1)
     packed, after = lax.optimization_barrier((packed, after))
-    gathered = lax.all_gather(packed, "dp", axis=0, tiled=True)
+    gathered = lax.all_gather(packed, DP, axis=0, tiled=True)
     gate_total = jnp.dot(
         normed_rows, gathered[:, :hidden_width], preferred_element_type=jnp.float32
     )
@@ -148,7 +159,7 @@
     model_width = residual_in.shape[1]
     quarter = model_width // lax.axis_size("mp")
     col_start = lax.axis_index("mp") * quarter
-    experts = lax.axis_size("dp") * w_gate.shape[0]
+    experts = lax.axis_size(DP) * w_gate.shape[0]
     route_count = route_ids.shape[1]
     capacity = min(tok_rows, 4 * tok_rows * route_count // (3 * experts))
     expert_ids = route_ids.reshape(-1)
@@ -166,7 +177,7 @@
     own_normed = lax.dynamic_slice_in_dim(normed_rows, col_start, quarter, 1)
     buffer = jnp.dot(placing, own_normed, preferred_element_type=jnp.float32).astype(jnp.bfloat16)
     buffer = buffer.reshape(experts, capacity, quarter)
-    received = lax.all_to_all(buffer, "dp", split_axis=0, concat_axis=0, tiled=True)
+    received = exchange_dp(buffer)
     results = run_experts(
         gather_mp(received.reshape(experts * capacity, quarter), 1).reshape(
             experts, capacity, model_width
@@ -189,28 +200,32 @@
 
 
 def solution(mesh):
+    dp_size, mp_size = mesh.devices.shape
+    split_mesh = jax.sharding.Mesh(
+        mesh.devices.reshape(dp_size // 2, 2, mp_size), ("dpo", "core", "mp")
+    )
     return jax.shard_map(
         on_device,
-        mesh=mesh,
+        mesh=split_mesh,
         in_specs=(
-            P("dp", "mp"),
-            P("dp", None, "mp"),
-            P("dp", None, None, "mp"),
-            P("dp", None),
-            P("dp"),
-            P("dp", None, None),
+            P(DP, "mp"),
+            P(DP, None, "mp"),
+            P(DP, None, None, "mp"),
+            P(DP, None),
+            P(DP),
+            P(DP, None, None),
             P("mp", None),
-            P("dp", None),
+            P(DP, None),
             P(),
-            P("dp", None),
-            P("dp", None),
-            P("dp", None, "mp"),
-            P("dp", None, "mp"),
-            P("dp", None, "mp"),
-            P("dp", "mp"),
-            P("dp", "mp"),
-            P("mp", "dp"),
+            P(DP, None),
+            P(DP, None),
+            P(DP, None, "mp"),
+            P(DP, None, "mp"),
+            P(DP, None, "mp"),
+            P(DP, "mp"),
+            P(DP, "mp"),
+            P("mp", DP),
         ),
-        out_specs=P("dp", "mp"),
+        out_specs=P(DP, "mp"),
         check_vma=False,
     )

time: 258 us -> 272 us (1.054)
  blocking collectives: 89.3 us -> 145 us
  waiting for transfers between devices: 68.3 us -> 39.2 us
  starting transfers between devices: 29.7 us -> 17.9 us
    all_to_all x0 -> x3, blocking collectives: none -> 58.3 us  [the longest x1 49 us: exchange_dp(): lax.all_to_all(split, 'dpo', split_axis=0, concat_axis=0, tiled=True)]
    all_to_all x2 -> x1, waiting for transfers between devices: 42.5 us -> 15.1 us  [exchange_dp(): lax.all_to_all(split, 'dpo', split_axis=0, concat_axis=0, tiled=True)]
    all_to_all x2 -> x1, starting transfers between devices: 17.6 us -> 6.02 us  [exchange_dp(): lax.all_to_all(split, 'dpo', split_axis=0, concat_axis=0, tiled=True)]
  transfers between devices with their start and end apart: 6 -> 5, of which waited for: 5 -> 4; matrix products, arithmetic and copies ran while one was open for 11% -> 19% of each run, Pallas kernels for 0% -> 0%
where the time goes in v7:
time: 272 us; the launch traced here: 270 us
  blocking collectives  145 us (53%)
  waiting for transfers between devices  39.2 us (14%)
  matrix products  26 us (10%)
  local copies, waits for them, and re-layouts  18.2 us (7%)
  starting transfers between devices  17.9 us (7%)
  between operations  13.9 us (5%)
  other arithmetic  9.84 us (4%)
    all_to_all x2, blocking collectives, gather_mp(): lax.all_to_all(copies, 'mp', split_axis=0, concat_axis=0, tiled=True)  86.9 us
    all_to_all x1, blocking collectives, exchange_dp(): lax.all_to_all(split, 'dpo', split_axis=0, concat_axis=0, tiled=True)  49 us
    all_to_all x2, waiting for transfers between devices, scatter_sum_mp(): lax.all_to_all(blocks, 'mp', split_axis=0, concat_axis=0, tiled=True)  17 us
    all_to_all x1, waiting for transfers between devices, exchange_dp(): lax.all_to_all(split, 'dpo', split_axis=0, concat_axis=0, tiled=True)  15.1 us
    all_to_all x2, blocking collectives, exchange_dp(): lax.all_to_all(split, 'core', split_axis=1, concat_axis=1, tiled=True)  9.33 us
    all_to_all x2, starting transfers between devices, scatter_sum_mp(): lax.all_to_all(blocks, 'mp', split_axis=0, concat_axis=0, tiled=True)  8.44 us
    dot_general x1, matrix products, shared_experts(): jnp.einsum('th,dh->td', shared_hidden, gathered[:, 2 * hidden_width:], pr...  7.37 us
    all_to_all x1, waiting for transfers between devices, gather_mp(): lax.all_to_all(copies, 'mp', split_axis=0, concat_axis=0, tiled=True)  7.04 us
  transfers between devices with their start and end apart: 5, of which 4 were waited for; matrix products, arithmetic and copies ran while one was open for 19% of the time, Pallas kernels for 0%

profile of v7, /device:TPU:32, one launch (start us, length us, event | category | flops | bytes accessed | tf_op | source)
XLA Modules:
  0.0 270.4 jit_solution(8917685990053730588)
XLA Ops:
  6.5 1.7 concatenate.3
  8.3 3.1 %fusion.61 = (bf16[40,1,128,128]{3,2,1,0:T(8,128)(2,1)S(1)}, bf16[40,1,128,128]{3,2,1,0:T(8,128)(2,1)}) fusion(bf16[40,2,128,128]{3,2,1,0:T(8,128)(2,1)} %param.19), kind=kLoop, calls=%fused_computation.84 | loop fusion | bytes 5242880 | tf_op jit(solution)/shard_map/slice | solution.py:21
  11.5 0.1 copy.86
  11.6 0.1 tile.2
  11.7 0.2 eq.66
  11.9 0.1 fusion.62
  12.1 0.1 select_reduce_fusion
  12.2 0.2 fusion.63
  12.5 1.8 fusion
  14.4 2.9 %fusion.1 = f32[2,256]{1,0:T(2,128)S(1)} fusion(f32[2,256,5120]{2,1,0:T(8,128)S(1)} %get-tuple-element.12, f32[2,256]{1,0:T(2,128)S(1)} %max.7, pred[2,5120]{1,0:T(4,128)(4,1)S(1)} %bitcast_compare_fusion), kind=kLoop, calls=%fused_computation.4 | loop fusion | flops 13106688 | bytes 10500096 | tf_op jit(solution)/shard_map/reduce_sum | solution.py:46
  17.3 3.0 %fusion.3 = f32[2,256,128]{2,1,0:T(8,128)S(1)} fusion(bf16[5120,128,1]{1,0,2:T(8,128)(2,1)S(1)} %bitcast.112, f32[2,256,5120]{2,1,0:T(8,128)S(1)} %get-tuple-element.12, f32[2,256]{1,0:T(2,128)S(1)} %max.7, pred[2,5120]{1,0:T(4,128)(4,1)S(1)} %bitcast_compare_fusion), kind=kOutput, calls=%fused_computation.6 | convolution fusion | flops 684195840 | bytes 12070912 | tf_op jit(solution)/shard_map/rqk,kd->rqd/dot_general | solution.py:47
  20.3 0.2 fusion.32
  20.6 0.1 copy.89
  20.7 0.7 reshape.178
  21.4 2.9 %copy.105 = bf16[2048,512]{1,0:T(8,128)(2,1)S(1)} copy(bf16[2048,512]{0,1:T(8,128)(2,1)} %bitcast.111) | data formatting | bytes 4194304 | tf_op jit(solution)/shard_map/dot_general | solution.py:158
  24.3 2.8 %convolution_bitcast_fusion = f32[4,128,512]{2,1,0:T(8,128)} fusion(bf16[128,512,1]{1,0,2:T(8,128)(2,1)} %reshape.178, bf16[4,512,512]{2,1,0:T(8,128)(2,1)S(1)} %bitcast.104), kind=kOutput, calls=%fused_computation.25 | convolution fusion | flops 268435456 | bytes 3276800 | tf_op jit(solution)/shard_map/dot_general | solution.py:158
  27.0 4.3 %all-to-all-start = ((f32[4,128,512]{2,1,0:T(8,128)}), f32[4,128,512]{2,1,0:T(8,128)S(1)}, u32[]{:S(2)}, u32[]{:S(2)}) async-start(f32[4,128,512]{2,1,0:T(8,128)} %convolution_bitcast_fusion), calls=%async_computation | async-start | bytes 2097152 | tf_op jit(solution)/shard_map/all_to_all | solution.py:72
  31.3 0.1 copy.93
  31.4 0.1 eq.71
  31.6 0.1 eq.67
  31.7 1.8 reduce-window.6
  33.5 0.3 slice_reduce_fusion
  33.8 12.6 %all-to-all-done = f32[4,128,512]{2,1,0:T(8,128)S(1)} async-done(((f32[4,128,512]{2,1,0:T(8,128)}), f32[4,128,512]{2,1,0:T(8,128)S(1)}, u32[]{:S(2)}, u32[]{:S(2)}) %all-to-all-start) | async-done | bytes 1048608 | tf_op jit(solution)/shard_map/all_to_all | solution.py:72
  46.4 0.1 reduce_sum.70
  46.5 0.9 add_convert_fusion
  47.5 0.1 copy.91
  47.6 0.9 broadcast_in_dim.79
  48.5 3.5 %all-to-all-start.1 = ((bf16[4,128,512]{1,2,0:T(8,128)(2,1)}), bf16[4,128,512]{1,2,0:T(8,128)(2,1)S(1)}, u32[]{:S(2)}, u32[]{:S(2)}) async-start(bf16[4,128,512]{1,2,0:T(8,128)(2,1)} %broadcast_in_dim.79), calls=%async_computation.1 | async-start | bytes 1048576 | tf_op jit(solution)/shard_map/all_to_all | solution.py:61
  52.0 0.1 fusion.44
  52.1 0.1 reduce_sum.74
  52.3 0.6 broadcast_multiply_fusion
  53.0 0.5 fusion.12
  53.5 7.0 %all-to-all-done.1 = bf16[4,128,512]{1,2,0:T(8,128)(2,1)S(1)} async-done(((bf16[4,128,512]{1,2,0:T(8,128)(2,1)}), bf16[4,128,512]{1,2,0:T(8,128)(2,1)S(1)}, u32[]{:S(2)}, u32[]{:S(2)}) %all-to-all-start.1) | async-done | bytes 524320 | tf_op jit(solution)/shard_map/all_to_all | solution.py:61
  60.5 0.3 multiply_reduce_fusion
  60.8 0.3 fusion.35
  61.2 0.5 convolution_convert_fusion.1
  61.6 0.3 copy-done.4
  62.0 4.6 %all_to_all.45 = bf16[32,2,16,512]{3,2,0,1:T(8,128)(2,1)S(1)} all-to-all(bf16[32,2,16,512]{3,2,0,1:T(8,128)(2,1)S(1)} %copy.98), channel_id=1, replica_groups=mesh['dpo'=32,'core'=2,'mp'=4] {'core'}, dimensions={1} | all-to-all | bytes 2097152 | tf_op jit(solution)/shard_map/all_to_all | solution.py:81
  66.7 0.1 copy.99
  66.8 49.0 %all_to_all.46 = bf16[32,2,16,512]{3,2,1,0:T(8,128)(2,1)S(1)} all-to-all(bf16[32,2,16,512]{3,2,1,0:T(8,128)(2,1)S(1)} %copy.99), channel_id=1, replica_groups=mesh['dpo'=32,'core'=2,'mp'=4] {'dpo'}, dimensions={0} | all-to-all | bytes 2097152 | tf_op jit(solution)/shard_map/all_to_all | solution.py:82
  115.8 0.5 copy.100
  116.3 0.5 broadcast_in_dim.81
  116.9 51.3 %all_to_all.47 = bf16[4,1024,512]{1,2,0:T(8,128)(2,1)S(1)} all-to-all(bf16[4,1024,512]{1,2,0:T(8,128)(2,1)S(1)} %broadcast_in_dim.81), channel_id=1, replica_groups=mesh['dpo'=32,'core'=2,'mp'=4] {'mp'}, dimensions={0} | all-to-all | bytes 8388608 | tf_op jit(solution)/shard_map/all_to_all | solution.py:61
  168.2 1.7 fusion.18
  169.9 1.8 fusion.20
  171.7 0.4 broadcast_in_dim.82
  172.1 35.6 %all_to_all.48 = bf16[4,1024,352]{1,2,0:T(8,128)(2,1)S(1)} all-to-all(bf16[4,1024,352]{1,2,0:T(8,128)(2,1)S(1)} %broadcast_in_dim.82), channel_id=1, replica_groups=mesh['dpo'=32,'core'=2,'mp'=4] {'mp'}, dimensions={0} | all-to-all | bytes 5767168 | tf_op jit(solution)/shard_map/all_to_all | solution.py:61
  207.7 1.8 convolution_convert_fusion
  209.6 4.7 %all_to_all.49 = bf16[32,2,16,512]{3,2,0,1:T(8,128)(2,1)S(1)} all-to-all(bf16[32,2,16,512]{3,2,0,1:T(8,128)(2,1)S(1)} %copy.101), channel_id=1, replica_groups=mesh['dpo'=32,'core'=2,'mp'=4] {'core'}, dimensions={1} | all-to-all | bytes 2097152 | tf_op jit(solution)/shard_map/all_to_all | solution.py:81
  214.3 1.1 copy.102
  215.5 6.0 %all-to-all-start.8 = ((bf16[32,2,16,512]{3,2,1,0:T(8,128)(2,1)}), bf16[32,2,16,512]{3,2,1,0:T(8,128)(2,1)S(1)}, u32[]{:S(2)}, u32[]{:S(2)}) async-start(bf16[32,2,16,512]{3,2,1,0:T(8,128)(2,1)} %copy.102), calls=%async_computation.8 | async-start | bytes 2097152 | tf_op jit(solution)/shard_map/all_to_all | solution.py:82
  221.5 0.1 mul.97
  221.7 3.9 %fusion.10 = f32[128,704]{0,1:T(8,128)} fusion(bf16[128,2048]{0,1:T(8,128)(2,1)S(1)} %copy-done.5, bf16[2048,2112]{1,0:T(8,128)(2,1)} %all-gather.2.cloned.1.call-done), kind=kOutput, calls=%fused_computation.12 | convolution fusion | flops 369098752 | bytes 4030464 | tf_op jit(solution)/shard_map/dot_general | solution.py:107
  225.6 7.4 %fusion.13 = bf16[128,2048]{1,0:T(8,128)(2,1)S(1)} fusion(bf16[2048,2112]{1,0:T(8,128)(2,1)} %all-gather.2.cloned.1.call-done, bf16[128,2048]{0,1:T(8,128)(2,1)S(1)} %copy-done.5, f32[128,704]{0,1:T(8,128)} %fusion.10), kind=kOutput, calls=%fused_computation.16 | convolution fusion | flops 739000320 | bytes 7700480 | tf_op jit(solution)/shard_map/th,dh->td/dot_general | solution.py:114
  233.0 0.8 copy.115
  233.8 15.1 %all-to-all-done.8 = bf16[32,2,16,512]{3,2,1,0:T(8,128)(2,1)S(1)} async-done(((bf16[32,2,16,512]{3,2,1,0:T(8,128)(2,1)}), bf16[32,2,16,512]{3,2,1,0:T(8,128)(2,1)S(1)}, u32[]{:S(2)}, u32[]{:S(2)}) %all-to-all-start.8) | async-done | bytes 1048608 | tf_op jit(solution)/shard_map/all_to_all | solution.py:82
  249.0 4.1 %all-to-all-start.2 = ((bf16[4,128,512]{2,1,0:T(8,128)(2,1)}), bf16[4,128,512]{2,1,0:T(8,128)(2,1)}, u32[]{:S(2)}, u32[]{:S(2)}) async-start(bf16[4,128,512]{2,1,0:T(8,128)(2,1)} %bitcast.101), calls=%async_computation.2 | async-start | bytes 1048576 | tf_op jit(solution)/shard_map/all_to_all | solution.py:72
  253.2 0.1 copy.103
  253.3 2.7 gather_fusion
  256.0 0.3 reshape.166
  256.3 1.0 fusion.64
  257.2 4.4 %all-to-all-done.2 = bf16[4,128,512]{2,1,0:T(8,128)(2,1)} async-done(((bf16[4,128,512]{2,1,0:T(8,128)(2,1)}), bf16[4,128,512]{2,1,0:T(8,128)(2,1)}, u32[]{:S(2)}, u32[]{:S(2)}) %all-to-all-start.2) | async-done | bytes 524320 | tf_op jit(solution)/shard_map/all_to_all | solution.py:72
  261.7 1.1 convert_reduce_fusion
  262.8 0.7 fusion.41
  (57 shorter events, 0.7 us)
Async XLA Ops:
  6.5 201.2 %copy-start = (bf16[1,1408,512]{2,1,0:T(8,128)(2,1)S(1)}, bf16[1,1408,512]{2,1,0:T(8,128)(2,1)}, u32[]{:S(2)}) copy-start(bf16[1,1408,512]{2,1,0:T(8,128)(2,1)} %param.30) | copy-start | bytes 4325380
  6.5 4.9 %copy-start.8 = (bf16[128,512]{1,0:T(8,128)(2,1)S(1)}, bf16[128,512]{1,0:T(8,128)(2,1)}, u32[]{:S(2)}) copy-start(bf16[128,512]{1,0:T(8,128)(2,1)} %param.17) | copy-start | bytes 393220
  6.5 5.0 %copy-start.9 = (s32[2,64,64]{2,1,0:T(8,128)S(1)}, s32[2,64,64]{2,1,0:T(8,128)}, u32[]{:S(2)}) copy-start(s32[2,64,64]{2,1,0:T(8,128)} %param.22) | copy-start | bytes 98308
  6.5 215.1 %all-gather.2.cloned.1.call-start = ((), (), s32[]{:S(2)}) async-start(), calls=%async_computation.9 | async-start | bytes 9052160 | tf_op jit(solution)/shard_map/all_gather | solution.py:106
  8.3 3.6 %copy-start.6 = (bf16[128,2,128]{2,1,0:T(2,128)(2,1)S(1)}, bf16[128,2,128]{2,1,0:T(2,128)(2,1)}, u32[]{:S(2)}) copy-start(bf16[128,2,128]{2,1,0:T(2,128)(2,1)} %param.18) | copy-start | bytes 196612
  8.3 3.7 %copy-start.14 = (s32[2]{0:T(128)S(1)}, s32[2]{0:T(128)}, u32[]{:S(2)}) copy-start(s32[2]{0:T(128)} %param.21) | copy-start | bytes 28
  8.3 3.8 %copy-start.13 = (s32[2,32]{1,0:T(2,128)S(1)}, s32[2,32]{1,0:T(2,128)}, u32[]{:S(2)}) copy-start(s32[2,32]{1,0:T(2,128)} %param.20) | copy-start | bytes 772
  14.4 2.9 %copy-start.1 = (bf16[40,1,128,128]{3,2,1,0:T(8,128)(2,1)S(1)}, bf16[40,1,128,128]{3,2,1,0:T(8,128)(2,1)}, u32[]{:S(2)}) copy-start(bf16[40,1,128,128]{3,2,1,0:T(8,128)(2,1)} %get-tuple-element.6) | copy-start | bytes 3932164
  24.3 7.1 %copy-start.11 = (s32[128,6]{0,1:T(8,128)S(1)}, s32[128,6]{0,1:T(8,128)}, u32[]{:S(2)}) copy-start(s32[128,6]{0,1:T(8,128)} %param.26) | copy-start | bytes 9220
  27.0 19.4 %all-to-all-start = ((f32[4,128,512]{2,1,0:T(8,128)}), f32[4,128,512]{2,1,0:T(8,128)S(1)}, u32[]{:S(2)}, u32[]{:S(2)}) async-start(f32[4,128,512]{2,1,0:T(8,128)} %convolution_bitcast_fusion), calls=%async_computation | async-start | bytes 2097152 | tf_op jit(solution)/shard_map/all_to_all | solution.py:72
  31.3 29.5 %copy-start.10 = (f32[2048]{0:T(1024)S(1)}, f32[2048]{0:T(1024)}, u32[]{:S(2)}) copy-start(f32[2048]{0:T(1024)} %param.25) | copy-start | bytes 24580
  47.4 1.1 copy-start.2
  48.5 12.0 %all-to-all-start.1 = ((bf16[4,128,512]{1,2,0:T(8,128)(2,1)}), bf16[4,128,512]{1,2,0:T(8,128)(2,1)S(1)}, u32[]{:S(2)}, u32[]{:S(2)}) async-start(bf16[4,128,512]{1,2,0:T(8,128)(2,1)} %broadcast_in_dim.79), calls=%async_computation.1 | async-start | bytes 1048576 | tf_op jit(solution)/shard_map/all_to_all | solution.py:61
  61.2 0.8 copy-start.4
  116.8 51.4 %copy-start.15 = (bf16[1,2048,352]{1,2,0:T(8,128)(2,1)S(1)}, bf16[1,2048,352]{1,2,0:T(8,128)(2,1)}, u32[]{:S(2)}) copy-start(bf16[1,2048,352]{1,2,0:T(8,128)(2,1)} %param.28) | copy-start | bytes 4325380
  168.2 1.7 copy-start.16
  209.6 11.9 %copy-start.7 = (s32[128,6]{1,0:T(8,128)S(1)}, s32[128,6]{1,0:T(8,128)}, u32[]{:S(2)}) copy-start(s32[128,6]{1,0:T(8,128)} %get-tuple-element.7) | copy-start | bytes 9220
  209.6 12.1 %copy-start.5 = (bf16[128,2048]{0,1:T(8,128)(2,1)S(1)}, bf16[128,2048]{0,1:T(8,128)(2,1)}, u32[]{:S(2)}) copy-start(bf16[128,2048]{0,1:T(8,128)(2,1)} %copy-done.4) | copy-start | bytes 1572868
  215.5 33.5 %all-to-all-start.8 = ((bf16[32,2,16,512]{3,2,1,0:T(8,128)(2,1)}), bf16[32,2,16,512]{3,2,1,0:T(8,128)(2,1)S(1)}, u32[]{:S(2)}, u32[]{:S(2)}) async-start(bf16[32,2,16,512]{3,2,1,0:T(8,128)(2,1)} %copy.102), calls=%async_computation.8 | async-start | bytes 2097152 | tf_op jit(solution)/shard_map/all_to_all | solution.py:82
  225.6 27.5 %copy-start.12 = (f32[128,6]{0,1:T(8,128)S(1)}, f32[128,6]{0,1:T(8,128)}, u32[]{:S(2)}) copy-start(f32[128,6]{0,1:T(8,128)} %param.27) | copy-start | bytes 9220
  249.0 12.7 %all-to-all-start.2 = ((bf16[4,128,512]{2,1,0:T(8,128)(2,1)}), bf16[4,128,512]{2,1,0:T(8,128)(2,1)}, u32[]{:S(2)}, u32[]{:S(2)}) async-start(bf16[4,128,512]{2,1,0:T(8,128)(2,1)} %bitcast.101), calls=%async_computation.2 | async-start | bytes 1048576 | tf_op jit(solution)/shard_map/all_to_all | solution.py:72
  256.0 6.8 %copy-start.3 = (bf16[128,512]{1,0:T(8,128)(2,1)S(1)}, bf16[128,512]{1,0:T(8,128)(2,1)}, u32[]{:S(2)}) copy-start(bf16[128,512]{1,0:T(8,128)(2,1)} %copy-done.2) | copy-start | bytes 393220
Sparse Core Ops, SparseCore 0:
  10.1 104.0 all-gather.1

commit v8 on v6

--- a/solution.py
+++ b/solution.py
@@ -64,6 +64,21 @@
     return pieces.reshape(shape)
 
 
+def ring_gather_mp(block):
+    parts = lax.axis_size("mp")
+    rows, width = block.shape
+    half = rows // 2
+    to_right = [(k, (k + 1) % parts) for k in range(parts)]
+    to_left = [(k, (k - 1) % parts) for k in range(parts)]
+    from_left = lax.ppermute(block, "mp", to_right)
+    from_right = lax.ppermute(block, "mp", to_left)
+    far_top = lax.ppermute(from_right[:half], "mp", to_left)
+    far_bottom = lax.ppermute(from_left[half:], "mp", to_right)
+    far = jnp.concatenate([far_top, far_bottom], axis=0)
+    rotated = jnp.concatenate([block, from_right, far, from_left], axis=1)
+    return jnp.roll(rotated, lax.axis_index("mp") * width, axis=1)
+
+
 def scatter_sum_mp(terms):
     parts = lax.axis_size("mp")
     rows, width = terms.shape
@@ -80,7 +95,7 @@
     hidden_act = (jax.nn.silu(gate_proj) * up_proj).astype(jnp.bfloat16)
     down_rows = w_down[0]
     summed = jnp.dot(
-        gather_mp(hidden_act, 1),
+        ring_gather_mp(hidden_act),
         down_rows,
         preferred_element_type=jnp.float32,
     )
@@ -168,7 +183,7 @@
     buffer = buffer.reshape(experts, capacity, quarter)
     received = lax.all_to_all(buffer, "dp", split_axis=0, concat_axis=0, tiled=True)
     results = run_experts(
-        gather_mp(received.reshape(experts * capacity, quarter), 1).reshape(
+        ring_gather_mp(received.reshape(experts * capacity, quarter)).reshape(
             experts, capacity, model_width
         ),
         w_gate,

time: 258 us -> 264 us (1.023)
  blocking collectives: 89.3 us -> 0 us
  waiting for transfers between devices: 68.3 us -> 120 us
  local copies, waits for them, and re-layouts: 16.2 us -> 32.8 us
  starting transfers between devices: 29.7 us -> 43.8 us
  other arithmetic: 11.3 us -> 19.8 us
  matrix products: 28.1 us -> 32.7 us
    all_to_all x2 -> x0, blocking collectives: 89.3 us -> none  [gather_mp(): lax.all_to_all(copies, 'mp', split_axis=0, concat_axis=0, tiled=True)]
    ppermute x0 -> x8, waiting for transfers between devices: none -> 51.5 us  [the longest x2 37.8 us: ring_gather_mp(): from_left = lax.ppermute(block, 'mp', to_right)]
    ppermute x0 -> x8, starting transfers between devices: none -> 13 us  [the longest x2 6.47 us: ring_gather_mp(): far_top = lax.ppermute(from_right[:half], 'mp', to_left)]
    unnamed x41 -> x52, local copies, waits for them, and re-layouts: 1.2 us -> 10.7 us
    unnamed x0 -> x4, other arithmetic: none -> 7.04 us
    slice x1 -> x5, local copies, waits for them, and re-layouts: 0.28 us -> 3.48 us  [the longest x2 1.61 us: ring_gather_mp(): far_bottom = lax.ppermute(from_left[half:], 'mp', to_right)]
  transfers between devices with their start and end apart: 6 -> 14, of which waited for: 5 -> 11; matrix products, arithmetic and copies ran while one was open for 11% -> 18% of each run, Pallas kernels for 0% -> 0%
where the time goes in v8:
time: 264 us; the launch traced here: 263 us
  waiting for transfers between devices  120 us (45%)
  starting transfers between devices  43.8 us (17%)
  local copies, waits for them, and re-layouts  32.8 us (12%)
  matrix products  32.7 us (12%)
  other arithmetic  19.8 us (8%)
  between operations  13.9 us (5%)
    ppermute x2, waiting for transfers between devices, ring_gather_mp(): from_left = lax.ppermute(block, 'mp', to_right)  37.8 us
    all_to_all x1, waiting for transfers between devices, on_device(): lax.all_to_all(buffer, 'dp', split_axis=0, concat_axis=0, tiled=True)  27.1 us
    all_to_all x2, waiting for transfers between devices, scatter_sum_mp(): lax.all_to_all(blocks, 'mp', split_axis=0, concat_axis=0, tiled=True)  18.5 us
    all_to_all x1, waiting for transfers between devices, run_experts(): lax.all_to_all(outputs, 'dp', split_axis=0, concat_axis=0, tiled=True)  15.6 us
    ppermute x2, waiting for transfers between devices, ring_gather_mp(): far_bottom = lax.ppermute(from_left[half:], 'mp', to_right)  12.6 us
    all_to_all x1, starting transfers between devices, on_device(): lax.all_to_all(buffer, 'dp', split_axis=0, concat_axis=0, tiled=True)  11.8 us
    unnamed x52, local copies, waits for them, and re-layouts  10.7 us
    all_to_all x2, starting transfers between devices, scatter_sum_mp(): lax.all_to_all(blocks, 'mp', split_axis=0, concat_axis=0, tiled=True)  9.25 us
  transfers between devices with their start and end apart: 14, of which 11 were waited for; matrix products, arithmetic and copies ran while one was open for 18% of the time, Pallas kernels for 0%

profile of v8, /device:TPU:32, one launch (start us, length us, event | category | flops | bytes accessed | tf_op | source)
XLA Modules:
  0.0 262.8 jit_solution(5207142616456479053)
XLA Ops:
  7.1 0.8 broadcast_compare_fusion
  8.8 0.8 select_reduce_fusion
  10.4 0.8 eq.71
  11.2 0.9 reshape.165
  12.8 1.0 fusion.78
  15.0 2.9 %copy.61 = bf16[2048,512]{1,0:T(8,128)(2,1)S(1)} copy(bf16[2048,512]{0,1:T(8,128)(2,1)} %bitcast.103) | data formatting | bytes 4194304 | tf_op jit(solution)/shard_map/dot_general | solution.py:162
  17.9 2.0 fusion.77
  19.9 0.8 bitcast_compare_fusion
  20.7 1.1 fusion.79
  21.9 2.7 %fusion = (f32[2,256]{1,0:T(2,128)S(1)}, f32[2,256,5120]{2,1,0:T(8,128)S(1)}) fusion(pred[2,5120]{1,0:T(4,128)(4,1)S(1)} %bitcast_compare_fusion, bf16[2,256,128]{2,1,0:T(8,128)(2,1)} %bitcast.106, bf16[5120,128,1]{1,0,2:T(8,128)(2,1)S(1)} %bitcast.102), kind=kOutput, calls=%fused_computation.3 | convolution fusion | flops 678952448 | bytes 11939840 | tf_op jit(solution)/shard_map/rqd,kd->rqk/dot_general | solution.py:33
  24.6 2.9 %fusion.1 = f32[2,256]{1,0:T(2,128)S(1)} fusion(f32[2,256,5120]{2,1,0:T(8,128)S(1)} %get-tuple-element.14, f32[2,256]{1,0:T(2,128)S(1)} %max.7, pred[2,5120]{1,0:T(4,128)(4,1)S(1)} %bitcast_compare_fusion), kind=kLoop, calls=%fused_computation.4 | loop fusion | flops 13106688 | bytes 10500096 | tf_op jit(solution)/shard_map/reduce_sum | solution.py:45
  27.5 3.0 %fusion.3 = f32[2,256,128]{2,1,0:T(8,128)S(1)} fusion(bf16[5120,128,1]{1,0,2:T(8,128)(2,1)S(1)} %bitcast.104, f32[2,256,5120]{2,1,0:T(8,128)S(1)} %get-tuple-element.14, f32[2,256]{1,0:T(2,128)S(1)} %max.7, pred[2,5120]{1,0:T(4,128)(4,1)S(1)} %bitcast_compare_fusion), kind=kOutput, calls=%fused_computation.6 | convolution fusion | flops 684195840 | bytes 12070912 | tf_op jit(solution)/shard_map/rqk,kd->rqd/dot_general | solution.py:46
  30.9 0.8 copy.50
  31.6 1.6 reshape.187
  33.2 2.7 %convolution_bitcast_fusion = f32[4,128,512]{2,1,0:T(8,128)} fusion(bf16[128,512,1]{1,0,2:T(8,128)(2,1)} %reshape.187, bf16[4,512,512]{2,1,0:T(8,128)(2,1)S(1)} %bitcast.101), kind=kOutput, calls=%fused_computation.29 | convolution fusion | flops 268435456 | bytes 3276800 | tf_op jit(solution)/shard_map/dot_general | solution.py:162
  35.9 4.3 %all-to-all-start = ((f32[4,128,512]{2,1,0:T(8,128)}), f32[4,128,512]{2,1,0:T(8,128)S(1)}, u32[]{:S(2)}, u32[]{:S(2)}) async-start(f32[4,128,512]{2,1,0:T(8,128)} %convolution_bitcast_fusion), calls=%async_computation | async-start | bytes 2097152 | tf_op jit(solution)/shard_map/all_to_all | solution.py:86
  40.7 1.8 reduce-window.6
  42.8 12.5 %all-to-all-done = f32[4,128,512]{2,1,0:T(8,128)S(1)} async-done(((f32[4,128,512]{2,1,0:T(8,128)}), f32[4,128,512]{2,1,0:T(8,128)S(1)}, u32[]{:S(2)}, u32[]{:S(2)}) %all-to-all-start) | async-done | bytes 1048608 | tf_op jit(solution)/shard_map/all_to_all | solution.py:86
  55.4 0.9 add_convert_fusion
  56.5 0.9 broadcast_in_dim.66
  57.3 3.5 %all-to-all-start.1 = ((bf16[4,128,512]{1,2,0:T(8,128)(2,1)}), bf16[4,128,512]{1,2,0:T(8,128)(2,1)S(1)}, u32[]{:S(2)}, u32[]{:S(2)}) async-start(bf16[4,128,512]{1,2,0:T(8,128)(2,1)} %broadcast_in_dim.66), calls=%async_computation.1 | async-start | bytes 1048576 | tf_op jit(solution)/shard_map/all_to_all | solution.py:60
  62.3 7.0 %all-to-all-done.1 = bf16[4,128,512]{1,2,0:T(8,128)(2,1)S(1)} async-done(((bf16[4,128,512]{1,2,0:T(8,128)(2,1)}), bf16[4,128,512]{1,2,0:T(8,128)(2,1)S(1)}, u32[]{:S(2)}, u32[]{:S(2)}) %all-to-all-start.1) | async-done | bytes 524320 | tf_op jit(solution)/shard_map/all_to_all | solution.py:60
  70.0 0.8 copy-done.5
  70.8 1.4 convolution_convert_fusion
  72.2 11.8 %all-to-all-start.2 = ((bf16[64,16,512]{2,1,0:T(8,128)(2,1)}), bf16[64,16,512]{2,1,0:T(8,128)(2,1)S(1)}, u32[]{:S(2)}, u32[]{:S(2)}) async-start(bf16[64,16,512]{2,1,0:T(8,128)(2,1)} %bitcast.18), calls=%async_computation.2 | async-start | bytes 2097152 | tf_op jit(solution)/shard_map/all_to_all | solution.py:184
  84.1 0.8 concatenate.21
  84.8 27.1 %all-to-all-done.2 = bf16[64,16,512]{2,1,0:T(8,128)(2,1)S(1)} async-done(((bf16[64,16,512]{2,1,0:T(8,128)(2,1)}), bf16[64,16,512]{2,1,0:T(8,128)(2,1)S(1)}, u32[]{:S(2)}, u32[]{:S(2)}) %all-to-all-start.2) | async-done | bytes 1048608 | tf_op jit(solution)/shard_map/all_to_all | solution.py:184
  112.6 2.7 %collective-permute-start = (bf16[1024,512]{1,0:T(8,128)(2,1)S(1)}, bf16[1024,512]{1,0:T(8,128)(2,1)S(1)}, u32[]{:S(2)}, u32[]{:S(2)}) collective-permute-start(bf16[1024,512]{1,0:T(8,128)(2,1)S(1)} %bitcast.98), channel_id=1, source_target_pairs={{0,3},{1,0},{2,1},{3,2},{4,7},{5,4},{6,5},{7,6},{8,11},{9,8},{10,9... | collective-permute-start | bytes 3145736 | tf_op jit(solution)/shard_map/ppermute | solution.py:74
  115.3 23.3 %collective-permute-done.2 = bf16[1024,512]{1,0:T(8,128)(2,1)S(1)} collective-permute-done((bf16[1024,512]{1,0:T(8,128)(2,1)S(1)}, bf16[1024,512]{1,0:T(8,128)(2,1)S(1)}, u32[]{:S(2)}, u32[]{:S(2)}) %collective-permute-start.2) | collective-permute-done | bytes 1048608 | tf_op jit(solution)/shard_map/ppermute | solution.py:73
  138.6 0.8 slice.59
  139.4 1.0 copy-done.1
  140.4 0.8 slice.58
  141.2 3.2 %collective-permute-start.1 = (bf16[512,512]{1,0:T(8,128)(2,1)}, bf16[512,512]{1,0:T(8,128)(2,1)}, u32[]{:S(2)}, u32[]{:S(2)}) collective-permute-start(bf16[512,512]{1,0:T(8,128)(2,1)} %slice.58), channel_id=1, source_target_pairs={{0,3},{1,0},{2,1},{3,2},{4,7},{5,4},{6,5},{7,6},{8,11},{9,8},{10,9... | collective-permute-start | bytes 1572872 | tf_op jit(solution)/shard_map/ppermute | solution.py:75
  144.6 1.4 constant_dynamic-update-slice_fusion.4
  146.0 8.2 %collective-permute-done.3 = bf16[512,512]{1,0:T(8,128)(2,1)} collective-permute-done((bf16[512,512]{1,0:T(8,128)(2,1)}, bf16[512,512]{1,0:T(8,128)(2,1)}, u32[]{:S(2)}, u32[]{:S(2)}) %collective-permute-start.3) | collective-permute-done | bytes 524320 | tf_op jit(solution)/shard_map/ppermute | solution.py:76
  154.2 1.1 collective-permute-done.1
  155.3 1.3 fusion.42
  157.0 1.8 fusion.41
  159.0 1.8 fusion.8
  160.8 2.7 %constant_dynamic-update-slice_fusion.11 = (bf16[1024,2816]{0,1:T(8,128)(2,1)}, bf16[1024,352]{0,1:T(8,128)(2,1)S(1)}) fusion(bf16[1,2048,352]{1,2,0:T(8,128)(2,1)S(1)} %copy-done, bf16[1024,4096]{1,0:T(8,128)(2,1)S(1)} %constant_dynamic-update-slice_fusion, s32[]{:T(128)S(6)} %select_n.71, f32[1024,352]{0,1:T(8,128)S(1)} %fusion.8), kind=kOutput, calls=%fused_computation.85 | convolution fusion | flops 1478557696 | bytes 8519684 | tf_op jit(solution)/shard_map/dot_general | solution.py:94
  163.5 3.2 %collective-permute-start.4 = (bf16[1024,352]{0,1:T(8,128)(2,1)S(1)}, bf16[1024,352]{0,1:T(8,128)(2,1)S(1)}, u32[]{:S(2)}, u32[]{:S(2)}) collective-permute-start(bf16[1024,352]{0,1:T(8,128)(2,1)S(1)} %get-tuple-element.18), channel_id=1, source_target_pairs={{0,3},{1,0},{2,1},{3,2},{4,7},{5,4},{6,5},{7,6},{8,11},{9,8},{10,9... | collective-permute-start | bytes 2162696 | tf_op jit(solution)/shard_map/ppermute | solution.py:74
  166.8 14.5 %collective-permute-done.6 = bf16[1024,352]{0,1:T(8,128)(2,1)S(1)} collective-permute-done((bf16[1024,352]{0,1:T(8,128)(2,1)S(1)}, bf16[1024,352]{0,1:T(8,128)(2,1)S(1)}, u32[]{:S(2)}, u32[]{:S(2)}) %collective-permute-start.6) | collective-permute-done | bytes 720928 | tf_op jit(solution)/shard_map/ppermute | solution.py:73
  181.3 0.8 slice.61
  182.1 0.8 slice.60
  182.8 3.2 %collective-permute-start.5 = (bf16[512,352]{0,1:T(8,128)(2,1)}, bf16[512,352]{0,1:T(8,128)(2,1)}, u32[]{:S(2)}, u32[]{:S(2)}) collective-permute-start(bf16[512,352]{0,1:T(8,128)(2,1)} %slice.60), channel_id=1, source_target_pairs={{0,3},{1,0},{2,1},{3,2},{4,7},{5,4},{6,5},{7,6},{8,11},{9,8},{10,9... | collective-permute-start | bytes 1081352 | tf_op jit(solution)/shard_map/ppermute | solution.py:75
  186.1 0.9 constant_dynamic-update-slice_fusion.10
  187.0 4.4 %collective-permute-done.7 = bf16[512,352]{0,1:T(8,128)(2,1)S(1)} collective-permute-done((bf16[512,352]{0,1:T(8,128)(2,1)}, bf16[512,352]{0,1:T(8,128)(2,1)S(1)}, u32[]{:S(2)}, u32[]{:S(2)}) %collective-permute-start.7) | collective-permute-done | bytes 360480 | tf_op jit(solution)/shard_map/ppermute | solution.py:76
  191.5 1.9 fusion.44
  193.4 0.9 constant_dynamic-update-slice_fusion.9
  194.3 2.0 constant_dynamic-update-slice_fusion.8
  196.4 0.9 constant_dynamic-update-slice_fusion.7
  197.3 2.0 fusion.43
  199.3 0.9 constant_dynamic-update-slice_fusion.6
  200.2 4.7 %fusion.22 = bf16[1024,512]{1,0:T(8,128)(2,1)} fusion(bf16[1024,2816]{0,1:T(8,128)(2,1)} %constant_dynamic-update-slice_fusion.6, s32[]{:T(128)S(6)} %select_n.73, bf16[1,1408,512]{2,1,0:T(8,128)(2,1)S(1)} %copy-done.18), kind=kOutput, calls=%fused_computation.24 | convolution fusion | flops 1476919296 | bytes 5373956 | tf_op jit(solution)/shard_map/dot_general | solution.py:97
  204.9 6.2 %all-to-all-start.4 = ((bf16[64,16,512]{2,1,0:T(8,128)(2,1)}), bf16[64,16,512]{2,1,0:T(8,128)(2,1)S(1)}, u32[]{:S(2)}, u32[]{:S(2)}) async-start(bf16[64,16,512]{2,1,0:T(8,128)(2,1)} %bitcast.24), calls=%async_computation.4 | async-start | bytes 2097152 | tf_op jit(solution)/shard_map/all_to_all | solution.py:103
  211.3 3.9 %fusion.14 = f32[128,704]{0,1:T(8,128)} fusion(bf16[128,2048]{0,1:T(8,128)(2,1)S(1)} %copy-done.6, bf16[2048,2112]{1,0:T(8,128)(2,1)} %all-gather.2.cloned.1.call-done), kind=kOutput, calls=%fused_computation.16 | convolution fusion | flops 369098752 | bytes 4030464 | tf_op jit(solution)/shard_map/dot_general | solution.py:111
  215.3 7.4 %fusion.19 = bf16[128,2048]{1,0:T(8,128)(2,1)S(1)} fusion(bf16[2048,2112]{1,0:T(8,128)(2,1)} %all-gather.2.cloned.1.call-done, bf16[128,2048]{0,1:T(8,128)(2,1)S(1)} %copy-done.6, f32[128,704]{0,1:T(8,128)} %fusion.14), kind=kOutput, calls=%fused_computation.22 | convolution fusion | flops 739000320 | bytes 7700480 | tf_op jit(solution)/shard_map/th,dh->td/dot_general | solution.py:118
  222.7 0.8 copy.71
  223.5 15.6 %all-to-all-done.4 = bf16[64,16,512]{2,1,0:T(8,128)(2,1)S(1)} async-done(((bf16[64,16,512]{2,1,0:T(8,128)(2,1)}), bf16[64,16,512]{2,1,0:T(8,128)(2,1)S(1)}, u32[]{:S(2)}, u32[]{:S(2)}) %all-to-all-start.4) | async-done | bytes 1048608 | tf_op jit(solution)/shard_map/all_to_all | solution.py:103
  239.1 5.0 %all-to-all-start.3 = ((bf16[4,128,512]{2,1,0:T(8,128)(2,1)}), bf16[4,128,512]{2,1,0:T(8,128)(2,1)}, u32[]{:S(2)}, u32[]{:S(2)}) async-start(bf16[4,128,512]{2,1,0:T(8,128)(2,1)} %bitcast.94), calls=%async_computation.3 | async-start | bytes 1048576 | tf_op jit(solution)/shard_map/all_to_all | solution.py:86
  244.2 2.7 %gather_fusion = bf16[768,512]{1,0:T(8,128)(2,1)S(1)} fusion(bf16[1024,512]{1,0:T(8,128)(2,1)S(1)} %bitcast.96, s32[1024]{0:T(1024)S(1)} %pad_clamp_fusion), kind=kCustom, calls=%fused_computation | custom fusion | bytes 1575936 | tf_op jit(solution)/shard_map/gather | solution.py:196
  247.2 1.0 fusion.80
  248.1 5.9 %all-to-all-done.3 = bf16[4,128,512]{2,1,0:T(8,128)(2,1)} async-done(((bf16[4,128,512]{2,1,0:T(8,128)(2,1)}), bf16[4,128,512]{2,1,0:T(8,128)(2,1)}, u32[]{:S(2)}, u32[]{:S(2)}) %all-to-all-start.3) | async-done | bytes 524320 | tf_op jit(solution)/shard_map/all_to_all | solution.py:86
  254.0 1.1 convert_reduce_fusion
  (86 shorter events, 10.2 us)
Async XLA Ops:
  6.5 154.3 %copy-start = (bf16[1,2048,352]{1,2,0:T(8,128)(2,1)S(1)}, bf16[1,2048,352]{1,2,0:T(8,128)(2,1)}, u32[]{:S(2)}) copy-start(bf16[1,2048,352]{1,2,0:T(8,128)(2,1)} %param.29) | copy-start | bytes 4325380
  27.5 3.0 %copy-start.8 = (pred[2,256,64]{1,2,0:T(32,128)(4,1)S(1)}, pred[2,256,64]{1,2,0:T(32,128)(4,1)}, u32[]{:S(2)}) copy-start(pred[2,256,64]{1,2,0:T(32,128)(4,1)} %eq.71) | copy-start | bytes 98308
  27.5 3.1 %copy-start.13 = (bf16[128,1,128]{2,0,1:T(8,128)(2,1)S(1)}, bf16[128,1,128]{2,0,1:T(8,128)(2,1)}, u32[]{:S(2)}) copy-start(bf16[128,1,128]{2,0,1:T(8,128)(2,1)} %copy.63) | copy-start | bytes 98308
  30.5 9.7 %copy-start.15 = (s32[128,6]{0,1:T(8,128)S(1)}, s32[128,6]{0,1:T(8,128)}, u32[]{:S(2)}) copy-start(s32[128,6]{0,1:T(8,128)} %param.26) | copy-start | bytes 9220
  33.2 36.4 %copy-start.14 = (f32[2048]{0:T(1024)S(1)}, f32[2048]{0:T(1024)}, u32[]{:S(2)}) copy-start(f32[2048]{0:T(1024)} %param.25) | copy-start | bytes 24580
  35.9 19.4 %all-to-all-start = ((f32[4,128,512]{2,1,0:T(8,128)}), f32[4,128,512]{2,1,0:T(8,128)S(1)}, u32[]{:S(2)}, u32[]{:S(2)}) async-start(f32[4,128,512]{2,1,0:T(8,128)} %convolution_bitcast_fusion), calls=%async_computation | async-start | bytes 2097152 | tf_op jit(solution)/shard_map/all_to_all | solution.py:86
  40.2 43.8 %copy-start.10 = (bf16[32,704]{1,0:T(8,128)(2,1)S(1)}, bf16[32,704]{1,0:T(8,128)(2,1)}, u32[]{:S(2)}) copy-start(bf16[32,704]{1,0:T(8,128)(2,1)} %param.31) | copy-start | bytes 135172
  40.2 43.9 %copy-start.11 = (bf16[32,704]{1,0:T(8,128)(2,1)S(1)}, bf16[32,704]{1,0:T(8,128)(2,1)}, u32[]{:S(2)}) copy-start(bf16[32,704]{1,0:T(8,128)(2,1)} %param.32) | copy-start | bytes 135172
  40.2 43.9 %copy-start.12 = (bf16[704,32]{0,1:T(8,128)(2,1)S(1)}, bf16[704,32]{0,1:T(8,128)(2,1)}, u32[]{:S(2)}) copy-start(bf16[704,32]{0,1:T(8,128)(2,1)} %param.33) | copy-start | bytes 135172
  56.3 1.0 copy-start.3
  57.3 12.0 %all-to-all-start.1 = ((bf16[4,128,512]{1,2,0:T(8,128)(2,1)}), bf16[4,128,512]{1,2,0:T(8,128)(2,1)S(1)}, u32[]{:S(2)}, u32[]{:S(2)}) async-start(bf16[4,128,512]{1,2,0:T(8,128)(2,1)} %broadcast_in_dim.66), calls=%async_computation.1 | async-start | bytes 1048576 | tf_op jit(solution)/shard_map/all_to_all | solution.py:60
  70.0 0.8 copy-start.5
  72.2 39.7 %all-to-all-start.2 = ((bf16[64,16,512]{2,1,0:T(8,128)(2,1)}), bf16[64,16,512]{2,1,0:T(8,128)(2,1)S(1)}, u32[]{:S(2)}, u32[]{:S(2)}) async-start(bf16[64,16,512]{2,1,0:T(8,128)(2,1)} %bitcast.18), calls=%async_computation.2 | async-start | bytes 2097152 | tf_op jit(solution)/shard_map/all_to_all | solution.py:184
  84.0 127.3 %all-gather.2.cloned.1.call-start = ((), (), s32[]{:S(2)}) async-start(), calls=%async_computation.5 | async-start | bytes 9052160 | tf_op jit(solution)/shard_map/all_gather | solution.py:110
  112.0 26.6 %collective-permute-start.2 = (bf16[1024,512]{1,0:T(8,128)(2,1)S(1)}, bf16[1024,512]{1,0:T(8,128)(2,1)S(1)}, u32[]{:S(2)}, u32[]{:S(2)}) collective-permute-start(bf16[1024,512]{1,0:T(8,128)(2,1)S(1)} %bitcast.97), channel_id=1, source_target_pairs={{0,1},{1,2},{2,3},{3,0},{4,5},{5,6},{6,7},{7,4},{8,9},{9,10},{10,1... | collective-permute-start | bytes 3145736 | tf_op jit(solution)/shard_map/ppermute | solution.py:73
  112.6 26.8 %collective-permute-start = (bf16[1024,512]{1,0:T(8,128)(2,1)S(1)}, bf16[1024,512]{1,0:T(8,128)(2,1)S(1)}, u32[]{:S(2)}, u32[]{:S(2)}) collective-permute-start(bf16[1024,512]{1,0:T(8,128)(2,1)S(1)} %bitcast.98), channel_id=1, source_target_pairs={{0,3},{1,0},{2,1},{3,2},{4,7},{5,4},{6,5},{7,6},{8,11},{9,8},{10,9... | collective-permute-start | bytes 3145736 | tf_op jit(solution)/shard_map/ppermute | solution.py:74
  139.4 14.8 %collective-permute-start.3 = (bf16[512,512]{1,0:T(8,128)(2,1)}, bf16[512,512]{1,0:T(8,128)(2,1)}, u32[]{:S(2)}, u32[]{:S(2)}) collective-permute-start(bf16[512,512]{1,0:T(8,128)(2,1)} %slice.59), channel_id=1, source_target_pairs={{0,1},{1,2},{2,3},{3,0},{4,5},{5,6},{6,7},{7,4},{8,9},{9,10},{10,1... | collective-permute-start | bytes 1572872 | tf_op jit(solution)/shard_map/ppermute | solution.py:76
  139.4 1.0 copy-start.1
  141.2 14.1 %collective-permute-start.1 = (bf16[512,512]{1,0:T(8,128)(2,1)}, bf16[512,512]{1,0:T(8,128)(2,1)}, u32[]{:S(2)}, u32[]{:S(2)}) collective-permute-start(bf16[512,512]{1,0:T(8,128)(2,1)} %slice.58), channel_id=1, source_target_pairs={{0,3},{1,0},{2,1},{3,2},{4,7},{5,4},{6,5},{7,6},{8,11},{9,8},{10,9... | collective-permute-start | bytes 1572872 | tf_op jit(solution)/shard_map/ppermute | solution.py:75
  144.4 12.4 %copy-start.2 = (bf16[1024,512]{1,0:T(8,128)(2,1)S(1)}, bf16[1024,512]{1,0:T(8,128)(2,1)}, u32[]{:S(2)}) copy-start(bf16[1024,512]{1,0:T(8,128)(2,1)} %copy-done.1) | copy-start | bytes 3145732
  156.6 2.4 copy-start.17
  163.5 18.5 %copy-start.7 = (bf16[1024,352]{0,1:T(8,128)(2,1)}, bf16[1024,352]{0,1:T(8,128)(2,1)S(1)}, u32[]{:S(2)}) copy-start(bf16[1024,352]{0,1:T(8,128)(2,1)S(1)} %get-tuple-element.18) | copy-start | bytes 2162692
  163.5 17.7 %collective-permute-start.6 = (bf16[1024,352]{0,1:T(8,128)(2,1)S(1)}, bf16[1024,352]{0,1:T(8,128)(2,1)S(1)}, u32[]{:S(2)}, u32[]{:S(2)}) collective-permute-start(bf16[1024,352]{0,1:T(8,128)(2,1)S(1)} %get-tuple-element.18), channel_id=1, source_target_pairs={{0,1},{1,2},{2,3},{3,0},{4,5},{5,6},{6,7},{7,4},{8,9},{9,10},{10,1... | collective-permute-start | bytes 2162696 | tf_op jit(solution)/shard_map/ppermute | solution.py:73
  163.5 18.5 %collective-permute-start.4 = (bf16[1024,352]{0,1:T(8,128)(2,1)S(1)}, bf16[1024,352]{0,1:T(8,128)(2,1)S(1)}, u32[]{:S(2)}, u32[]{:S(2)}) collective-permute-start(bf16[1024,352]{0,1:T(8,128)(2,1)S(1)} %get-tuple-element.18), channel_id=1, source_target_pairs={{0,3},{1,0},{2,1},{3,2},{4,7},{5,4},{6,5},{7,6},{8,11},{9,8},{10,9... | collective-permute-start | bytes 2162696 | tf_op jit(solution)/shard_map/ppermute | solution.py:74
  182.1 9.3 %collective-permute-start.7 = (bf16[512,352]{0,1:T(8,128)(2,1)}, bf16[512,352]{0,1:T(8,128)(2,1)S(1)}, u32[]{:S(2)}, u32[]{:S(2)}) collective-permute-start(bf16[512,352]{0,1:T(8,128)(2,1)} %slice.61), channel_id=1, source_target_pairs={{0,1},{1,2},{2,3},{3,0},{4,5},{5,6},{6,7},{7,4},{8,9},{9,10},{10,1... | collective-permute-start | bytes 1081352 | tf_op jit(solution)/shard_map/ppermute | solution.py:76
  182.8 8.7 %collective-permute-start.5 = (bf16[512,352]{0,1:T(8,128)(2,1)}, bf16[512,352]{0,1:T(8,128)(2,1)}, u32[]{:S(2)}, u32[]{:S(2)}) collective-permute-start(bf16[512,352]{0,1:T(8,128)(2,1)} %slice.60), channel_id=1, source_target_pairs={{0,3},{1,0},{2,1},{3,2},{4,7},{5,4},{6,5},{7,6},{8,11},{9,8},{10,9... | collective-permute-start | bytes 1081352 | tf_op jit(solution)/shard_map/ppermute | solution.py:75
  186.1 14.1 %copy-start.18 = (bf16[1,1408,512]{2,1,0:T(8,128)(2,1)S(1)}, bf16[1,1408,512]{2,1,0:T(8,128)(2,1)}, u32[]{:S(2)}) copy-start(bf16[1,1408,512]{2,1,0:T(8,128)(2,1)} %param.30) | copy-start | bytes 4325380
  200.2 11.0 %copy-start.9 = (s32[128,6]{1,0:T(8,128)S(1)}, s32[128,6]{1,0:T(8,128)}, u32[]{:S(2)}) copy-start(s32[128,6]{1,0:T(8,128)} %get-tuple-element.9) | copy-start | bytes 9220
  200.2 11.1 %copy-start.6 = (bf16[128,2048]{0,1:T(8,128)(2,1)S(1)}, bf16[128,2048]{0,1:T(8,128)(2,1)}, u32[]{:S(2)}) copy-start(bf16[128,2048]{0,1:T(8,128)(2,1)} %copy-done.5) | copy-start | bytes 1572868
  204.9 34.2 %all-to-all-start.4 = ((bf16[64,16,512]{2,1,0:T(8,128)(2,1)}), bf16[64,16,512]{2,1,0:T(8,128)(2,1)S(1)}, u32[]{:S(2)}, u32[]{:S(2)}) async-start(bf16[64,16,512]{2,1,0:T(8,128)(2,1)} %bitcast.24), calls=%async_computation.4 | async-start | bytes 2097152 | tf_op jit(solution)/shard_map/all_to_all | solution.py:103
  215.3 28.8 %copy-start.16 = (f32[128,6]{0,1:T(8,128)S(1)}, f32[128,6]{0,1:T(8,128)}, u32[]{:S(2)}) copy-start(f32[128,6]{0,1:T(8,128)} %param.27) | copy-start | bytes 9220
  239.1 15.0 %all-to-all-start.3 = ((bf16[4,128,512]{2,1,0:T(8,128)(2,1)}), bf16[4,128,512]{2,1,0:T(8,128)(2,1)}, u32[]{:S(2)}, u32[]{:S(2)}) async-start(bf16[4,128,512]{2,1,0:T(8,128)(2,1)} %bitcast.94), calls=%async_computation.3 | async-start | bytes 1048576 | tf_op jit(solution)/shard_map/all_to_all | solution.py:86
  244.0 11.1 %copy-start.4 = (bf16[128,512]{1,0:T(8,128)(2,1)S(1)}, bf16[128,512]{1,0:T(8,128)(2,1)}, u32[]{:S(2)}) copy-start(bf16[128,512]{1,0:T(8,128)(2,1)} %copy-done.3) | copy-start | bytes 393220
Sparse Core Ops, SparseCore 0:
  112.1 79.5 all-gather.1

commit v9 on v8

--- a/solution.py
+++ b/solution.py
@@ -64,10 +64,9 @@
     return pieces.reshape(shape)
 
 
-def ring_gather_mp(block):
-    parts = lax.axis_size("mp")
-    rows, width = block.shape
-    half = rows // 2
+def ring_blocks_mp(block):
+    parts = lax.axis_size("mp")
+    half = block.shape[0] // 2
     to_right = [(k, (k + 1) % parts) for k in range(parts)]
     to_left = [(k, (k - 1) % parts) for k in range(parts)]
     from_left = lax.ppermute(block, "mp", to_right)
@@ -75,8 +74,20 @@
     far_top = lax.ppermute(from_right[:half], "mp", to_left)
     far_bottom = lax.ppermute(from_left[half:], "mp", to_right)
     far = jnp.concatenate([far_top, far_bottom], axis=0)
-    rotated = jnp.concatenate([block, from_right, far, from_left], axis=1)
-    return jnp.roll(rotated, lax.axis_index("mp") * width, axis=1)
+    return [block, from_right, far, from_left]
+
+
+def blockwise_dot(blocks, weights):
+    parts = lax.axis_size("mp")
+    mp_index = lax.axis_index("mp")
+    width = blocks[0].shape[1]
+    total = None
+    for step, piece in enumerate(blocks):
+        start = ((mp_index + step) % parts) * width
+        rows = lax.dynamic_slice_in_dim(weights, start, width, 0)
+        term = jnp.dot(piece, rows, preferred_element_type=jnp.float32)
+        total = term if total is None else total + term
+    return total
 
 
 def scatter_sum_mp(terms):
@@ -87,18 +98,11 @@
     return jnp.sum(pieces.astype(jnp.float32), axis=0)
 
 
-def run_experts(rows, w_gate, w_up, w_down):
-    source_count, slot_count, model_width = rows.shape
-    flat_rows = rows.reshape(source_count * slot_count, model_width)
-    gate_proj = jnp.dot(flat_rows, w_gate[0], preferred_element_type=jnp.float32)
-    up_proj = jnp.dot(flat_rows, w_up[0], preferred_element_type=jnp.float32)
+def run_experts(row_blocks, source_count, slot_count, w_gate, w_up, w_down):
+    gate_proj = blockwise_dot(row_blocks, w_gate[0])
+    up_proj = blockwise_dot(row_blocks, w_up[0])
     hidden_act = (jax.nn.silu(gate_proj) * up_proj).astype(jnp.bfloat16)
-    down_rows = w_down[0]
-    summed = jnp.dot(
-        ring_gather_mp(hidden_act),
-        down_rows,
-        preferred_element_type=jnp.float32,
-    )
+    summed = blockwise_dot(ring_blocks_mp(hidden_act), w_down[0])
     outputs = summed.astype(jnp.bfloat16).reshape(source_count, slot_count, w_down.shape[2])
     return lax.all_to_all(outputs, "dp", split_axis=0, concat_axis=0, tiled=True)
 
@@ -183,9 +187,9 @@
     buffer = buffer.reshape(experts, capacity, quarter)
     received = lax.all_to_all(buffer, "dp", split_axis=0, concat_axis=0, tiled=True)
     results = run_experts(
-        ring_gather_mp(received.reshape(experts * capacity, quarter)).reshape(
-            experts, capacity, model_width
-        ),
+        ring_blocks_mp(received.reshape(experts * capacity, quarter)),
+        experts,
+        capacity,
         w_gate,
         w_up,
         w_down,

time: 264 us -> 237 us (0.90)
  local copies, waits for them, and re-layouts: 32.8 us -> 16 us
  other arithmetic: 19.8 us -> 11.3 us
  starting transfers between devices: 43.8 us -> 39.2 us
  matrix products: 32.7 us -> 36 us
    unnamed x52 -> x42, local copies, waits for them, and re-layouts: 10.7 us -> 1.2 us
    unnamed x4 -> x0, other arithmetic: 7.04 us -> none
    dot_general x3 -> x12, matrix products: 9.25 us -> 14.4 us  [blockwise_dot(): term = jnp.dot(piece, rows, preferred_element_type=jnp.float32)]
    ppermute x8, starting transfers between devices: 13 us -> 9.11 us  [the longest x2 4.07 us: ring_blocks_mp(): far_top = lax.ppermute(from_right[:half], 'mp', to_left)]
  transfers between devices with their start and end apart: 14 -> 14, of which waited for: 11 -> 11; matrix products, arithmetic and copies ran while one was open for 18% -> 16% of each run, Pallas kernels for 0% -> 0%
where the time goes in v9:
time: 237 us; the launch traced here: 236 us
  waiting for transfers between devices  119 us (50%)
  starting transfers between devices  39.2 us (17%)
  matrix products  36 us (15%)
  local copies, waits for them, and re-layouts  16 us (7%)
  between operations  13.9 us (6%)
  other arithmetic  11.3 us (5%)
    ppermute x2, waiting for transfers between devices, ring_blocks_mp(): from_right = lax.ppermute(block, 'mp', to_left)  35.6 us
    all_to_all x1, waiting for transfers between devices, on_device(): lax.all_to_all(buffer, 'dp', split_axis=0, concat_axis=0, tiled=True)  27.1 us
    all_to_all x2, waiting for transfers between devices, scatter_sum_mp(): lax.all_to_all(blocks, 'mp', split_axis=0, concat_axis=0, tiled=True)  18.7 us
    all_to_all x1, waiting for transfers between devices, run_experts(): lax.all_to_all(outputs, 'dp', split_axis=0, concat_axis=0, tiled=True)  15.6 us
    dot_general x12, matrix products, blockwise_dot(): term = jnp.dot(piece, rows, preferred_element_type=jnp.float32)  14.4 us
    all_to_all x1, starting transfers between devices, on_device(): lax.all_to_all(buffer, 'dp', split_axis=0, concat_axis=0, tiled=True)  11.7 us
    all_to_all x2, starting transfers between devices, scatter_sum_mp(): lax.all_to_all(blocks, 'mp', split_axis=0, concat_axis=0, tiled=True)  8.55 us
    ppermute x2, waiting for transfers between devices, ring_blocks_mp(): far_top = lax.ppermute(from_right[:half], 'mp', to_left)  7.73 us
  transfers between devices with their start and end apart: 14, of which 11 were waited for; matrix products, arithmetic and copies ran while one was open for 16% of the time, Pallas kernels for 0%

profile of v9, /device:TPU:32, one launch (start us, length us, event | category | flops | bytes accessed | tf_op | source)
XLA Modules:
  0.0 235.8 jit_solution(10895281285829470615)
XLA Ops:
  6.5 0.8 compare_select_fusion.1
  7.4 0.8 select_reduce_fusion
  8.2 3.1 %fusion.108 = (bf16[40,1,128,128]{3,2,1,0:T(8,128)(2,1)S(1)}, bf16[40,1,128,128]{3,2,1,0:T(8,128)(2,1)}) fusion(bf16[40,2,128,128]{3,2,1,0:T(8,128)(2,1)} %param.19), kind=kLoop, calls=%fused_computation.135 | loop fusion | bytes 5242880 | tf_op jit(solution)/shard_map/slice | solution.py:20
  11.9 1.8 fusion
  14.0 2.9 %fusion.1 = f32[2,256]{1,0:T(2,128)S(1)} fusion(f32[2,256,5120]{2,1,0:T(8,128)S(1)} %get-tuple-element.14, f32[2,256]{1,0:T(2,128)S(1)} %max.7, pred[2,5120]{1,0:T(4,128)(4,1)S(1)} %bitcast_compare_fusion), kind=kLoop, calls=%fused_computation.4 | loop fusion | flops 13106688 | bytes 10500096 | tf_op jit(solution)/shard_map/reduce_sum | solution.py:45
  16.9 3.0 %fusion.3 = f32[2,256,128]{2,1,0:T(8,128)S(1)} fusion(bf16[5120,128,1]{1,0,2:T(8,128)(2,1)S(1)} %bitcast.142, f32[2,256,5120]{2,1,0:T(8,128)S(1)} %get-tuple-element.14, f32[2,256]{1,0:T(2,128)S(1)} %max.7, pred[2,5120]{1,0:T(4,128)(4,1)S(1)} %bitcast_compare_fusion), kind=kOutput, calls=%fused_computation.6 | convolution fusion | flops 684195840 | bytes 12070912 | tf_op jit(solution)/shard_map/rqk,kd->rqd/dot_general | solution.py:46
  19.9 0.2 fusion.27
  20.3 0.7 reshape.199
  21.0 2.9 %copy.61 = bf16[2048,512]{1,0:T(8,128)(2,1)S(1)} copy(bf16[2048,512]{0,1:T(8,128)(2,1)} %bitcast.141) | data formatting | bytes 4194304 | tf_op jit(solution)/shard_map/dot_general | solution.py:166
  23.9 2.7 %convolution_bitcast_fusion = f32[4,128,512]{2,1,0:T(8,128)} fusion(bf16[128,512,1]{1,0,2:T(8,128)(2,1)} %reshape.199, bf16[4,512,512]{2,1,0:T(8,128)(2,1)S(1)} %bitcast.139), kind=kOutput, calls=%fused_computation.26 | convolution fusion | flops 268435456 | bytes 3276800 | tf_op jit(solution)/shard_map/dot_general | solution.py:166
  26.6 4.4 %all-to-all-start = ((f32[4,128,512]{2,1,0:T(8,128)}), f32[4,128,512]{2,1,0:T(8,128)S(1)}, u32[]{:S(2)}, u32[]{:S(2)}) async-start(f32[4,128,512]{2,1,0:T(8,128)} %convolution_bitcast_fusion), calls=%async_computation | async-start | bytes 2097152 | tf_op jit(solution)/shard_map/all_to_all | solution.py:97
  31.4 1.8 reduce-window.6
  33.2 0.3 slice_reduce_fusion
  33.5 12.6 %all-to-all-done = f32[4,128,512]{2,1,0:T(8,128)S(1)} async-done(((f32[4,128,512]{2,1,0:T(8,128)}), f32[4,128,512]{2,1,0:T(8,128)S(1)}, u32[]{:S(2)}, u32[]{:S(2)}) %all-to-all-start) | async-done | bytes 1048608 | tf_op jit(solution)/shard_map/all_to_all | solution.py:97
  46.2 0.9 add_convert_fusion.1
  47.3 0.9 broadcast_in_dim.66
  48.1 3.5 %all-to-all-start.1 = ((bf16[4,128,512]{1,2,0:T(8,128)(2,1)}), bf16[4,128,512]{1,2,0:T(8,128)(2,1)S(1)}, u32[]{:S(2)}, u32[]{:S(2)}) async-start(bf16[4,128,512]{1,2,0:T(8,128)(2,1)} %broadcast_in_dim.66), calls=%async_computation.1 | async-start | bytes 1048576 | tf_op jit(solution)/shard_map/all_to_all | solution.py:60
  51.9 0.6 broadcast_multiply_fusion
  52.6 0.5 fusion.12
  53.1 7.1 %all-to-all-done.1 = bf16[4,128,512]{1,2,0:T(8,128)(2,1)S(1)} async-done(((bf16[4,128,512]{1,2,0:T(8,128)(2,1)}), bf16[4,128,512]{1,2,0:T(8,128)(2,1)S(1)}, u32[]{:S(2)}, u32[]{:S(2)}) %all-to-all-start.1) | async-done | bytes 524320 | tf_op jit(solution)/shard_map/all_to_all | solution.py:60
  60.2 0.3 multiply_reduce_fusion
  60.5 0.3 fusion.30
  60.8 0.8 copy-done.5
  61.6 1.4 convolution_convert_fusion
  63.0 11.7 %all-to-all-start.2 = ((bf16[64,16,512]{2,1,0:T(8,128)(2,1)}), bf16[64,16,512]{2,1,0:T(8,128)(2,1)S(1)}, u32[]{:S(2)}, u32[]{:S(2)}) async-start(bf16[64,16,512]{2,1,0:T(8,128)(2,1)} %bitcast.18), calls=%async_computation.2 | async-start | bytes 2097152 | tf_op jit(solution)/shard_map/all_to_all | solution.py:188
  74.8 0.8 concatenate.9
  75.6 27.1 %all-to-all-done.2 = bf16[64,16,512]{2,1,0:T(8,128)(2,1)S(1)} async-done(((bf16[64,16,512]{2,1,0:T(8,128)(2,1)}), bf16[64,16,512]{2,1,0:T(8,128)(2,1)S(1)}, u32[]{:S(2)}, u32[]{:S(2)}) %all-to-all-start.2) | async-done | bytes 1048608 | tf_op jit(solution)/shard_map/all_to_all | solution.py:188
  102.7 1.3 collective-permute-start
  104.0 0.8 collective-permute-start.2
  104.8 1.7 fusion.50
  106.5 0.6 fusion.56
  107.1 21.0 %collective-permute-done = bf16[1024,512]{1,0:T(8,128)(2,1)S(1)} collective-permute-done((bf16[1024,512]{1,0:T(8,128)(2,1)S(1)}, bf16[1024,512]{1,0:T(8,128)(2,1)S(1)}, u32[]{:S(2)}, u32[]{:S(2)}) %collective-permute-start) | collective-permute-done | bytes 1048608 | tf_op jit(solution)/shard_map/ppermute | solution.py:73
  128.2 2.5 %collective-permute-start.1 = (bf16[512,512]{1,0:T(8,128)(2,1)S(1)}, bf16[512,512]{1,0:T(8,128)(2,1)S(1)}, u32[]{:S(2)}, u32[]{:S(2)}) collective-permute-start(bf16[512,512]{1,0:T(8,128)(2,1)S(1)} %slice.58), channel_id=1, source_target_pairs={{0,3},{1,0},{2,1},{3,2},{4,7},{5,4},{6,5},{7,6},{8,11},{9,8},{10,9... | collective-permute-start | bytes 1572872 | tf_op jit(solution)/shard_map/ppermute | solution.py:74
  130.7 1.1 slice.59
  131.8 1.9 fusion.52
  133.7 0.6 convolution_add_fusion.1
  134.3 1.8 fusion.44
  136.1 0.6 convolution_add_fusion.3
  136.7 4.9 %collective-permute-done.1 = bf16[512,512]{1,0:T(8,128)(2,1)S(1)} collective-permute-done((bf16[512,512]{1,0:T(8,128)(2,1)S(1)}, bf16[512,512]{1,0:T(8,128)(2,1)S(1)}, u32[]{:S(2)}, u32[]{:S(2)}) %collective-permute-start.1) | collective-permute-done | bytes 524320 | tf_op jit(solution)/shard_map/ppermute | solution.py:74
  141.6 4.5 %collective-permute-done.3 = bf16[512,512]{1,0:T(8,128)(2,1)S(1)} collective-permute-done((bf16[512,512]{1,0:T(8,128)(2,1)S(1)}, bf16[512,512]{1,0:T(8,128)(2,1)S(1)}, u32[]{:S(2)}, u32[]{:S(2)}) %collective-permute-start.3) | collective-permute-done | bytes 524320 | tf_op jit(solution)/shard_map/ppermute | solution.py:75
  146.2 0.6 fusion.17
  146.7 1.6 multiply_convert_fusion
  148.4 2.0 collective-permute-start.6
  150.4 14.6 %collective-permute-done.4 = bf16[1024,352]{0,1:T(8,128)(2,1)S(1)} collective-permute-done((bf16[1024,352]{0,1:T(8,128)(2,1)}, bf16[1024,352]{0,1:T(8,128)(2,1)S(1)}, u32[]{:S(2)}, u32[]{:S(2)}) %collective-permute-start.4) | collective-permute-done | bytes 720928 | tf_op jit(solution)/shard_map/ppermute | solution.py:73
  165.0 1.6 collective-permute-start.5
  166.6 0.8 collective-permute-start.7
  167.4 1.9 fusion.42
  169.3 0.7 fusion.40
  170.0 2.8 %collective-permute-done.5 = bf16[512,352]{0,1:T(8,128)(2,1)S(1)} collective-permute-done((bf16[512,352]{0,1:T(8,128)(2,1)S(1)}, bf16[512,352]{0,1:T(8,128)(2,1)S(1)}, u32[]{:S(2)}, u32[]{:S(2)}) %collective-permute-start.5) | collective-permute-done | bytes 360480 | tf_op jit(solution)/shard_map/ppermute | solution.py:74
  172.9 3.0 %collective-permute-done.7 = bf16[512,352]{0,1:T(8,128)(2,1)S(1)} collective-permute-done((bf16[512,352]{0,1:T(8,128)(2,1)S(1)}, bf16[512,352]{0,1:T(8,128)(2,1)S(1)}, u32[]{:S(2)}, u32[]{:S(2)}) %collective-permute-start.7) | collective-permute-done | bytes 360480 | tf_op jit(solution)/shard_map/ppermute | solution.py:75
  175.9 0.7 fusion.31
  176.7 1.8 add_convert_fusion
  178.5 6.3 %all-to-all-start.4 = ((bf16[64,16,512]{2,1,0:T(8,128)(2,1)}), bf16[64,16,512]{2,1,0:T(8,128)(2,1)S(1)}, u32[]{:S(2)}, u32[]{:S(2)}) async-start(bf16[64,16,512]{2,1,0:T(8,128)(2,1)} %bitcast.33), calls=%async_computation.4 | async-start | bytes 2097152 | tf_op jit(solution)/shard_map/all_to_all | solution.py:107
  185.0 3.9 %fusion.10 = f32[128,704]{0,1:T(8,128)} fusion(bf16[128,2048]{0,1:T(8,128)(2,1)S(1)} %copy-done.6, bf16[2048,2112]{1,0:T(8,128)(2,1)} %all-gather.2.cloned.1.call-done), kind=kOutput, calls=%fused_computation.12 | convolution fusion | flops 369098752 | bytes 4030464 | tf_op jit(solution)/shard_map/dot_general | solution.py:115
  188.9 7.4 %fusion.13 = bf16[128,2048]{1,0:T(8,128)(2,1)S(1)} fusion(bf16[2048,2112]{1,0:T(8,128)(2,1)} %all-gather.2.cloned.1.call-done, bf16[128,2048]{0,1:T(8,128)(2,1)S(1)} %copy-done.6, f32[128,704]{0,1:T(8,128)} %fusion.10), kind=kOutput, calls=%fused_computation.16 | convolution fusion | flops 739000320 | bytes 7700480 | tf_op jit(solution)/shard_map/th,dh->td/dot_general | solution.py:122
  196.3 0.8 copy.71
  197.1 15.6 %all-to-all-done.4 = bf16[64,16,512]{2,1,0:T(8,128)(2,1)S(1)} async-done(((bf16[64,16,512]{2,1,0:T(8,128)(2,1)}), bf16[64,16,512]{2,1,0:T(8,128)(2,1)S(1)}, u32[]{:S(2)}, u32[]{:S(2)}) %all-to-all-start.4) | async-done | bytes 1048608 | tf_op jit(solution)/shard_map/all_to_all | solution.py:107
  212.7 4.1 %all-to-all-start.3 = ((bf16[4,128,512]{2,1,0:T(8,128)(2,1)}), bf16[4,128,512]{2,1,0:T(8,128)(2,1)}, u32[]{:S(2)}, u32[]{:S(2)}) async-start(bf16[4,128,512]{2,1,0:T(8,128)(2,1)} %bitcast.132), calls=%async_computation.3 | async-start | bytes 1048576 | tf_op jit(solution)/shard_map/all_to_all | solution.py:97
  217.0 2.7 %gather_fusion = bf16[768,512]{1,0:T(8,128)(2,1)S(1)} fusion(bf16[1024,512]{1,0:T(8,128)(2,1)S(1)} %bitcast.134, s32[1024]{0:T(1024)S(1)} %pad_clamp_fusion), kind=kCustom, calls=%fused_computation | custom fusion | bytes 1575936 | tf_op jit(solution)/shard_map/gather | solution.py:200
  219.7 0.3 reshape.187
  220.0 1.0 fusion.111
  221.0 6.1 %all-to-all-done.3 = bf16[4,128,512]{2,1,0:T(8,128)(2,1)} async-done(((bf16[4,128,512]{2,1,0:T(8,128)(2,1)}), bf16[4,128,512]{2,1,0:T(8,128)(2,1)}, u32[]{:S(2)}, u32[]{:S(2)}) %all-to-all-start.3) | async-done | bytes 524320 | tf_op jit(solution)/shard_map/all_to_all | solution.py:97
  227.1 1.1 convert_reduce_fusion
  228.2 0.7 fusion.75
  (80 shorter events, 2.6 us)
Async XLA Ops:
  6.5 160.9 %copy-start = (bf16[1,1408,512]{2,1,0:T(8,128)(2,1)S(1)}, bf16[1,1408,512]{2,1,0:T(8,128)(2,1)}, u32[]{:S(2)}) copy-start(bf16[1,1408,512]{2,1,0:T(8,128)(2,1)} %param.30) | copy-start | bytes 4325380
  8.2 3.1 %copy-start.10 = (bf16[128,512]{1,0:T(8,128)(2,1)S(1)}, bf16[128,512]{1,0:T(8,128)(2,1)}, u32[]{:S(2)}) copy-start(bf16[128,512]{1,0:T(8,128)(2,1)} %param.17) | copy-start | bytes 393220
  8.2 3.2 %copy-start.11 = (s32[2,64,64]{2,1,0:T(8,128)S(1)}, s32[2,64,64]{2,1,0:T(8,128)}, u32[]{:S(2)}) copy-start(s32[2,64,64]{2,1,0:T(8,128)} %param.22) | copy-start | bytes 98308
  8.2 3.5 %copy-start.8 = (bf16[128,2,128]{2,1,0:T(2,128)(2,1)S(1)}, bf16[128,2,128]{2,1,0:T(2,128)(2,1)}, u32[]{:S(2)}) copy-start(bf16[128,2,128]{2,1,0:T(2,128)(2,1)} %param.18) | copy-start | bytes 196612
  14.0 3.0 %copy-start.2 = (bf16[40,1,128,128]{3,2,1,0:T(8,128)(2,1)S(1)}, bf16[40,1,128,128]{3,2,1,0:T(8,128)(2,1)}, u32[]{:S(2)}) copy-start(bf16[40,1,128,128]{3,2,1,0:T(8,128)(2,1)} %get-tuple-element.8) | copy-start | bytes 3932164
  26.6 4.4 %copy-start.16 = (s32[128,6]{0,1:T(8,128)S(1)}, s32[128,6]{0,1:T(8,128)}, u32[]{:S(2)}) copy-start(s32[128,6]{0,1:T(8,128)} %param.26) | copy-start | bytes 9220
  26.6 19.5 %all-to-all-start = ((f32[4,128,512]{2,1,0:T(8,128)}), f32[4,128,512]{2,1,0:T(8,128)S(1)}, u32[]{:S(2)}, u32[]{:S(2)}) async-start(f32[4,128,512]{2,1,0:T(8,128)} %convolution_bitcast_fusion), calls=%async_computation | async-start | bytes 2097152 | tf_op jit(solution)/shard_map/all_to_all | solution.py:97
  47.1 1.0 copy-start.3
  47.3 13.2 %copy-start.15 = (f32[2048]{0:T(1024)S(1)}, f32[2048]{0:T(1024)}, u32[]{:S(2)}) copy-start(f32[2048]{0:T(1024)} %param.25) | copy-start | bytes 24580
  48.1 12.0 %all-to-all-start.1 = ((bf16[4,128,512]{1,2,0:T(8,128)(2,1)}), bf16[4,128,512]{1,2,0:T(8,128)(2,1)S(1)}, u32[]{:S(2)}, u32[]{:S(2)}) async-start(bf16[4,128,512]{1,2,0:T(8,128)(2,1)} %broadcast_in_dim.66), calls=%async_computation.1 | async-start | bytes 1048576 | tf_op jit(solution)/shard_map/all_to_all | solution.py:60
  60.8 0.8 copy-start.5
  61.6 13.2 %copy-start.12 = (bf16[32,704]{1,0:T(8,128)(2,1)S(1)}, bf16[32,704]{1,0:T(8,128)(2,1)}, u32[]{:S(2)}) copy-start(bf16[32,704]{1,0:T(8,128)(2,1)} %param.31) | copy-start | bytes 135172
  61.6 13.2 %copy-start.13 = (bf16[32,704]{1,0:T(8,128)(2,1)S(1)}, bf16[32,704]{1,0:T(8,128)(2,1)}, u32[]{:S(2)}) copy-start(bf16[32,704]{1,0:T(8,128)(2,1)} %param.32) | copy-start | bytes 135172
  61.6 13.2 %copy-start.14 = (bf16[704,32]{0,1:T(8,128)(2,1)S(1)}, bf16[704,32]{0,1:T(8,128)(2,1)}, u32[]{:S(2)}) copy-start(bf16[704,32]{0,1:T(8,128)(2,1)} %param.33) | copy-start | bytes 135172
  63.0 39.7 %all-to-all-start.2 = ((bf16[64,16,512]{2,1,0:T(8,128)(2,1)}), bf16[64,16,512]{2,1,0:T(8,128)(2,1)S(1)}, u32[]{:S(2)}, u32[]{:S(2)}) async-start(bf16[64,16,512]{2,1,0:T(8,128)(2,1)} %bitcast.18), calls=%async_computation.2 | async-start | bytes 2097152 | tf_op jit(solution)/shard_map/all_to_all | solution.py:188
  74.8 110.2 %all-gather.2.cloned.1.call-start = ((), (), s32[]{:S(2)}) async-start(), calls=%async_computation.5 | async-start | bytes 9052160 | tf_op jit(solution)/shard_map/all_gather | solution.py:114
  102.7 25.4 %collective-permute-start = (bf16[1024,512]{1,0:T(8,128)(2,1)S(1)}, bf16[1024,512]{1,0:T(8,128)(2,1)S(1)}, u32[]{:S(2)}, u32[]{:S(2)}) collective-permute-start(bf16[1024,512]{1,0:T(8,128)(2,1)S(1)} %bitcast.135), channel_id=1, source_target_pairs={{0,3},{1,0},{2,1},{3,2},{4,7},{5,4},{6,5},{7,6},{8,11},{9,8},{10,9... | collective-permute-start | bytes 3145736 | tf_op jit(solution)/shard_map/ppermute | solution.py:73
  104.0 26.6 %collective-permute-start.2 = (bf16[1024,512]{1,0:T(8,128)(2,1)S(1)}, bf16[1024,512]{1,0:T(8,128)(2,1)}, u32[]{:S(2)}, u32[]{:S(2)}) collective-permute-start(bf16[1024,512]{1,0:T(8,128)(2,1)S(1)} %bitcast.136), channel_id=1, source_target_pairs={{0,1},{1,2},{2,3},{3,0},{4,5},{5,6},{6,7},{7,4},{8,9},{9,10},{10,1... | collective-permute-start | bytes 3145736 | tf_op jit(solution)/shard_map/ppermute | solution.py:72
  104.8 1.7 copy-start.1
  128.2 13.4 %collective-permute-start.1 = (bf16[512,512]{1,0:T(8,128)(2,1)S(1)}, bf16[512,512]{1,0:T(8,128)(2,1)S(1)}, u32[]{:S(2)}, u32[]{:S(2)}) collective-permute-start(bf16[512,512]{1,0:T(8,128)(2,1)S(1)} %slice.58), channel_id=1, source_target_pairs={{0,3},{1,0},{2,1},{3,2},{4,7},{5,4},{6,5},{7,6},{8,11},{9,8},{10,9... | collective-permute-start | bytes 1572872 | tf_op jit(solution)/shard_map/ppermute | solution.py:74
  131.7 2.0 copy-start.7
  131.7 14.4 %collective-permute-start.3 = (bf16[512,512]{1,0:T(8,128)(2,1)S(1)}, bf16[512,512]{1,0:T(8,128)(2,1)S(1)}, u32[]{:S(2)}, u32[]{:S(2)}) collective-permute-start(bf16[512,512]{1,0:T(8,128)(2,1)S(1)} %slice.59), channel_id=1, source_target_pairs={{0,1},{1,2},{2,3},{3,0},{4,5},{5,6},{6,7},{7,4},{8,9},{9,10},{10,1... | collective-permute-start | bytes 1572872 | tf_op jit(solution)/shard_map/ppermute | solution.py:75
  148.4 16.6 %collective-permute-start.4 = (bf16[1024,352]{0,1:T(8,128)(2,1)}, bf16[1024,352]{0,1:T(8,128)(2,1)S(1)}, u32[]{:S(2)}, u32[]{:S(2)}) collective-permute-start(bf16[1024,352]{0,1:T(8,128)(2,1)} %multiply_convert_fusion), channel_id=1, source_target_pairs={{0,3},{1,0},{2,1},{3,2},{4,7},{5,4},{6,5},{7,6},{8,11},{9,8},{10,9... | collective-permute-start | bytes 2162696 | tf_op jit(solution)/shard_map/ppermute | solution.py:73
  148.4 18.2 %collective-permute-start.6 = (bf16[1024,352]{0,1:T(8,128)(2,1)}, bf16[1024,352]{0,1:T(8,128)(2,1)S(1)}, u32[]{:S(2)}, u32[]{:S(2)}) collective-permute-start(bf16[1024,352]{0,1:T(8,128)(2,1)} %multiply_convert_fusion), channel_id=1, source_target_pairs={{0,1},{1,2},{2,3},{3,0},{4,5},{5,6},{6,7},{7,4},{8,9},{9,10},{10,1... | collective-permute-start | bytes 2162696 | tf_op jit(solution)/shard_map/ppermute | solution.py:72
  165.0 7.9 %collective-permute-start.5 = (bf16[512,352]{0,1:T(8,128)(2,1)S(1)}, bf16[512,352]{0,1:T(8,128)(2,1)S(1)}, u32[]{:S(2)}, u32[]{:S(2)}) collective-permute-start(bf16[512,352]{0,1:T(8,128)(2,1)S(1)} %slice.60), channel_id=1, source_target_pairs={{0,3},{1,0},{2,1},{3,2},{4,7},{5,4},{6,5},{7,6},{8,11},{9,8},{10,9... | collective-permute-start | bytes 1081352 | tf_op jit(solution)/shard_map/ppermute | solution.py:74
  166.6 9.3 %collective-permute-start.7 = (bf16[512,352]{0,1:T(8,128)(2,1)S(1)}, bf16[512,352]{0,1:T(8,128)(2,1)S(1)}, u32[]{:S(2)}, u32[]{:S(2)}) collective-permute-start(bf16[512,352]{0,1:T(8,128)(2,1)S(1)} %slice.61), channel_id=1, source_target_pairs={{0,1},{1,2},{2,3},{3,0},{4,5},{5,6},{6,7},{7,4},{8,9},{9,10},{10,1... | collective-permute-start | bytes 1081352 | tf_op jit(solution)/shard_map/ppermute | solution.py:75
  178.4 6.3 %copy-start.9 = (s32[128,6]{1,0:T(8,128)S(1)}, s32[128,6]{1,0:T(8,128)}, u32[]{:S(2)}) copy-start(s32[128,6]{1,0:T(8,128)} %get-tuple-element.9) | copy-start | bytes 9220
  178.4 6.5 %copy-start.6 = (bf16[128,2048]{0,1:T(8,128)(2,1)S(1)}, bf16[128,2048]{0,1:T(8,128)(2,1)}, u32[]{:S(2)}) copy-start(bf16[128,2048]{0,1:T(8,128)(2,1)} %copy-done.5) | copy-start | bytes 1572868
  178.5 34.3 %all-to-all-start.4 = ((bf16[64,16,512]{2,1,0:T(8,128)(2,1)}), bf16[64,16,512]{2,1,0:T(8,128)(2,1)S(1)}, u32[]{:S(2)}, u32[]{:S(2)}) async-start(bf16[64,16,512]{2,1,0:T(8,128)(2,1)} %bitcast.33), calls=%async_computation.4 | async-start | bytes 2097152 | tf_op jit(solution)/shard_map/all_to_all | solution.py:107
  196.3 20.6 %copy-start.17 = (f32[128,6]{0,1:T(8,128)S(1)}, f32[128,6]{0,1:T(8,128)}, u32[]{:S(2)}) copy-start(f32[128,6]{0,1:T(8,128)} %param.27) | copy-start | bytes 9220
  212.7 14.4 %all-to-all-start.3 = ((bf16[4,128,512]{2,1,0:T(8,128)(2,1)}), bf16[4,128,512]{2,1,0:T(8,128)(2,1)}, u32[]{:S(2)}, u32[]{:S(2)}) async-start(bf16[4,128,512]{2,1,0:T(8,128)(2,1)} %bitcast.132), calls=%async_computation.3 | async-start | bytes 1048576 | tf_op jit(solution)/shard_map/all_to_all | solution.py:97
  220.0 8.3 %copy-start.4 = (bf16[128,512]{1,0:T(8,128)(2,1)S(1)}, bf16[128,512]{1,0:T(8,128)(2,1)}, u32[]{:S(2)}) copy-start(bf16[128,512]{1,0:T(8,128)(2,1)} %copy-done.3) | copy-start | bytes 393220
Sparse Core Ops, SparseCore 0:
  102.8 79.5 all-gather.1

commit v10 on v9

--- a/solution.py
+++ b/solution.py
@@ -125,7 +125,7 @@
         gathered[:, 2 * hidden_width :],
         preferred_element_type=jnp.float32,
     )
-    return scatter_sum_mp(terms.astype(jnp.bfloat16))
+    return lax.psum_scatter(terms.astype(jnp.bfloat16), "mp", scatter_dimension=1, tiled=True)
 
 
 def on_device(

time: 237 us -> 228 us (0.962)
  starting transfers between devices: 39.2 us -> 35.2 us
  waiting for transfers between devices: 119 us -> 116 us
    all_to_all x2 -> x1, waiting for transfers between devices: 18.7 us -> 12.6 us  [scatter_sum_mp(): lax.all_to_all(blocks, 'mp', split_axis=0, concat_axis=0, tiled=True)]
    all_to_all x2 -> x1, starting transfers between devices: 8.55 us -> 4.43 us  [scatter_sum_mp(): lax.all_to_all(blocks, 'mp', split_axis=0, concat_axis=0, tiled=True)]
where the time goes in v10:
time: 228 us; the launch traced here: 227 us
  waiting for transfers between devices  116 us (51%)
  matrix products  35.9 us (16%)
  starting transfers between devices  35.2 us (15%)
  local copies, waits for them, and re-layouts  15.2 us (7%)
  between operations  13.9 us (6%)
  other arithmetic  11 us (5%)
    ppermute x2, waiting for transfers between devices, ring_blocks_mp(): from_right = lax.ppermute(block, 'mp', to_left)  35.6 us
    all_to_all x1, waiting for transfers between devices, on_device(): lax.all_to_all(buffer, 'dp', split_axis=0, concat_axis=0, tiled=True)  27.1 us
    all_to_all x1, waiting for transfers between devices, run_experts(): lax.all_to_all(outputs, 'dp', split_axis=0, concat_axis=0, tiled=True)  16.2 us
    dot_general x12, matrix products, blockwise_dot(): term = jnp.dot(piece, rows, preferred_element_type=jnp.float32)  14.4 us
    all_to_all x1, waiting for transfers between devices, scatter_sum_mp(): lax.all_to_all(blocks, 'mp', split_axis=0, concat_axis=0, tiled=True)  12.6 us
    all_to_all x1, starting transfers between devices, on_device(): lax.all_to_all(buffer, 'dp', split_axis=0, concat_axis=0, tiled=True)  11.8 us
    dot_general x1, matrix products, shared_experts(): jnp.einsum('th,dh->td', shared_hidden, gathered[:, 2 * hidden_width:], pr...  8.05 us
    ppermute x2, waiting for transfers between devices, ring_blocks_mp(): far_top = lax.ppermute(from_right[:half], 'mp', to_left)  7.73 us
  transfers between devices with their start and end apart: 14, of which 11 were waited for; matrix products, arithmetic and copies ran while one was open for 16% of the time, Pallas kernels for 0%

profile of v10, /device:TPU:32, one launch (start us, length us, event | category | flops | bytes accessed | tf_op | source)
XLA Modules:
  0.0 227.3 jit_solution(18377638447491404489)
XLA Ops:
  6.5 0.8 compare_select_fusion.1
  7.4 0.8 select_reduce_fusion
  8.2 3.1 %fusion.108 = (bf16[40,1,128,128]{3,2,1,0:T(8,128)(2,1)S(1)}, bf16[40,1,128,128]{3,2,1,0:T(8,128)(2,1)}) fusion(bf16[40,2,128,128]{3,2,1,0:T(8,128)(2,1)} %param.19), kind=kLoop, calls=%fused_computation.133 | loop fusion | bytes 5242880 | tf_op jit(solution)/shard_map/slice | solution.py:20
  11.6 0.2 eq.79
  11.9 1.8 fusion
  13.8 0.2 fusion.110
  14.0 2.9 %fusion.1 = f32[2,256]{1,0:T(2,128)S(1)} fusion(f32[2,256,5120]{2,1,0:T(8,128)S(1)} %get-tuple-element.14, f32[2,256]{1,0:T(2,128)S(1)} %max.7, pred[2,5120]{1,0:T(4,128)(4,1)S(1)} %bitcast_compare_fusion), kind=kLoop, calls=%fused_computation.4 | loop fusion | flops 13106688 | bytes 10500096 | tf_op jit(solution)/shard_map/reduce_sum | solution.py:45
  16.9 3.0 %fusion.3 = f32[2,256,128]{2,1,0:T(8,128)S(1)} fusion(bf16[5120,128,1]{1,0,2:T(8,128)(2,1)S(1)} %bitcast.135, f32[2,256,5120]{2,1,0:T(8,128)S(1)} %get-tuple-element.14, f32[2,256]{1,0:T(2,128)S(1)} %max.7, pred[2,5120]{1,0:T(4,128)(4,1)S(1)} %bitcast_compare_fusion), kind=kOutput, calls=%fused_computation.6 | convolution fusion | flops 684195840 | bytes 12070912 | tf_op jit(solution)/shard_map/rqk,kd->rqd/dot_general | solution.py:46
  19.9 0.2 fusion.27
  20.3 0.7 reshape.195
  21.0 2.9 %copy.48 = bf16[2048,512]{1,0:T(8,128)(2,1)S(1)} copy(bf16[2048,512]{0,1:T(8,128)(2,1)} %bitcast.134) | data formatting | bytes 4194304 | tf_op jit(solution)/shard_map/dot_general | solution.py:166
  23.9 2.7 %convolution_bitcast_fusion = f32[4,128,512]{2,1,0:T(8,128)} fusion(bf16[128,512,1]{1,0,2:T(8,128)(2,1)} %reshape.195, bf16[4,512,512]{2,1,0:T(8,128)(2,1)S(1)} %bitcast.132), kind=kOutput, calls=%fused_computation.26 | convolution fusion | flops 268435456 | bytes 3276800 | tf_op jit(solution)/shard_map/dot_general | solution.py:166
  26.6 4.4 %all-to-all-start = ((f32[4,128,512]{2,1,0:T(8,128)}), f32[4,128,512]{2,1,0:T(8,128)S(1)}, u32[]{:S(2)}, u32[]{:S(2)}) async-start(f32[4,128,512]{2,1,0:T(8,128)} %convolution_bitcast_fusion), calls=%async_computation | async-start | bytes 2097152 | tf_op jit(solution)/shard_map/all_to_all | solution.py:97
  31.4 1.8 reduce-window.6
  33.2 0.3 slice_reduce_fusion
  33.5 12.6 %all-to-all-done = f32[4,128,512]{2,1,0:T(8,128)S(1)} async-done(((f32[4,128,512]{2,1,0:T(8,128)}), f32[4,128,512]{2,1,0:T(8,128)S(1)}, u32[]{:S(2)}, u32[]{:S(2)}) %all-to-all-start) | async-done | bytes 1048608 | tf_op jit(solution)/shard_map/all_to_all | solution.py:97
  46.2 0.9 add_convert_fusion.1
  47.3 0.9 broadcast_in_dim.66
  48.1 3.5 %all-to-all-start.1 = ((bf16[4,128,512]{1,2,0:T(8,128)(2,1)}), bf16[4,128,512]{1,2,0:T(8,128)(2,1)S(1)}, u32[]{:S(2)}, u32[]{:S(2)}) async-start(bf16[4,128,512]{1,2,0:T(8,128)(2,1)} %broadcast_in_dim.66), calls=%async_computation.1 | async-start | bytes 1048576 | tf_op jit(solution)/shard_map/all_to_all | solution.py:60
  51.9 0.6 broadcast_multiply_fusion
  52.6 0.5 fusion.12
  53.1 7.0 %all-to-all-done.1 = bf16[4,128,512]{1,2,0:T(8,128)(2,1)S(1)} async-done(((bf16[4,128,512]{1,2,0:T(8,128)(2,1)}), bf16[4,128,512]{1,2,0:T(8,128)(2,1)S(1)}, u32[]{:S(2)}, u32[]{:S(2)}) %all-to-all-start.1) | async-done | bytes 524320 | tf_op jit(solution)/shard_map/all_to_all | solution.py:60
  60.1 0.3 multiply_reduce_fusion
  60.4 0.3 fusion.30
  60.8 0.8 copy-done.5
  61.6 1.4 convolution_convert_fusion
  63.0 11.8 %all-to-all-start.2 = ((bf16[64,16,512]{2,1,0:T(8,128)(2,1)}), bf16[64,16,512]{2,1,0:T(8,128)(2,1)S(1)}, u32[]{:S(2)}, u32[]{:S(2)}) async-start(bf16[64,16,512]{2,1,0:T(8,128)(2,1)} %bitcast.18), calls=%async_computation.2 | async-start | bytes 2097152 | tf_op jit(solution)/shard_map/all_to_all | solution.py:188
  74.8 0.8 concatenate.9
  75.6 27.1 %all-to-all-done.2 = bf16[64,16,512]{2,1,0:T(8,128)(2,1)S(1)} async-done(((bf16[64,16,512]{2,1,0:T(8,128)(2,1)}), bf16[64,16,512]{2,1,0:T(8,128)(2,1)S(1)}, u32[]{:S(2)}, u32[]{:S(2)}) %all-to-all-start.2) | async-done | bytes 1048608 | tf_op jit(solution)/shard_map/all_to_all | solution.py:188
  102.7 1.3 collective-permute-start
  104.0 0.8 collective-permute-start.2
  104.8 1.7 fusion.50
  106.5 0.6 fusion.56
  107.1 21.0 %collective-permute-done = bf16[1024,512]{1,0:T(8,128)(2,1)S(1)} collective-permute-done((bf16[1024,512]{1,0:T(8,128)(2,1)S(1)}, bf16[1024,512]{1,0:T(8,128)(2,1)S(1)}, u32[]{:S(2)}, u32[]{:S(2)}) %collective-permute-start) | collective-permute-done | bytes 1048608 | tf_op jit(solution)/shard_map/ppermute | solution.py:73
  128.1 2.5 %collective-permute-start.1 = (bf16[512,512]{1,0:T(8,128)(2,1)S(1)}, bf16[512,512]{1,0:T(8,128)(2,1)S(1)}, u32[]{:S(2)}, u32[]{:S(2)}) collective-permute-start(bf16[512,512]{1,0:T(8,128)(2,1)S(1)} %slice.58), channel_id=1, source_target_pairs={{0,3},{1,0},{2,1},{3,2},{4,7},{5,4},{6,5},{7,6},{8,11},{9,8},{10,9... | collective-permute-start | bytes 1572872 | tf_op jit(solution)/shard_map/ppermute | solution.py:74
  130.6 1.1 slice.59
  131.8 1.9 fusion.52
  133.7 0.6 convolution_add_fusion.1
  134.3 1.8 fusion.44
  136.1 0.6 convolution_add_fusion.3
  136.7 4.9 %collective-permute-done.1 = bf16[512,512]{1,0:T(8,128)(2,1)S(1)} collective-permute-done((bf16[512,512]{1,0:T(8,128)(2,1)S(1)}, bf16[512,512]{1,0:T(8,128)(2,1)S(1)}, u32[]{:S(2)}, u32[]{:S(2)}) %collective-permute-start.1) | collective-permute-done | bytes 524320 | tf_op jit(solution)/shard_map/ppermute | solution.py:74
  141.6 4.5 %collective-permute-done.3 = bf16[512,512]{1,0:T(8,128)(2,1)S(1)} collective-permute-done((bf16[512,512]{1,0:T(8,128)(2,1)S(1)}, bf16[512,512]{1,0:T(8,128)(2,1)S(1)}, u32[]{:S(2)}, u32[]{:S(2)}) %collective-permute-start.3) | collective-permute-done | bytes 524320 | tf_op jit(solution)/shard_map/ppermute | solution.py:75
  146.2 0.6 fusion.17
  146.7 1.6 multiply_convert_fusion
  148.4 2.0 collective-permute-start.6
  150.4 14.6 %collective-permute-done.4 = bf16[1024,352]{0,1:T(8,128)(2,1)S(1)} collective-permute-done((bf16[1024,352]{0,1:T(8,128)(2,1)}, bf16[1024,352]{0,1:T(8,128)(2,1)S(1)}, u32[]{:S(2)}, u32[]{:S(2)}) %collective-permute-start.4) | collective-permute-done | bytes 720928 | tf_op jit(solution)/shard_map/ppermute | solution.py:73
  165.0 1.6 collective-permute-start.5
  166.6 0.8 collective-permute-start.7
  167.4 1.9 fusion.42
  169.3 0.7 fusion.40
  170.0 2.9 %collective-permute-done.5 = bf16[512,352]{0,1:T(8,128)(2,1)S(1)} collective-permute-done((bf16[512,352]{0,1:T(8,128)(2,1)S(1)}, bf16[512,352]{0,1:T(8,128)(2,1)S(1)}, u32[]{:S(2)}, u32[]{:S(2)}) %collective-permute-start.5) | collective-permute-done | bytes 360480 | tf_op jit(solution)/shard_map/ppermute | solution.py:74
  172.9 3.0 %collective-permute-done.7 = bf16[512,352]{0,1:T(8,128)(2,1)S(1)} collective-permute-done((bf16[512,352]{0,1:T(8,128)(2,1)S(1)}, bf16[512,352]{0,1:T(8,128)(2,1)S(1)}, u32[]{:S(2)}, u32[]{:S(2)}) %collective-permute-start.7) | collective-permute-done | bytes 360480 | tf_op jit(solution)/shard_map/ppermute | solution.py:75
  175.9 0.7 fusion.31
  176.7 1.8 add_convert_fusion
  178.4 6.3 %all-to-all-start.3 = ((bf16[64,16,512]{2,1,0:T(8,128)(2,1)}), bf16[64,16,512]{2,1,0:T(8,128)(2,1)S(1)}, u32[]{:S(2)}, u32[]{:S(2)}) async-start(bf16[64,16,512]{2,1,0:T(8,128)(2,1)} %bitcast.32), calls=%async_computation.4 | async-start | bytes 2097152 | tf_op jit(solution)/shard_map/all_to_all | solution.py:107
  184.9 3.2 %fusion.10 = f32[128,704]{0,1:T(8,128)S(1)} fusion(bf16[128,2048]{0,1:T(8,128)(2,1)S(1)} %copy-done.6, bf16[2048,2112]{1,0:T(8,128)(2,1)} %all-gather.2.cloned.1.call-done), kind=kOutput, calls=%fused_computation.12 | convolution fusion | flops 369098752 | bytes 4030464 | tf_op jit(solution)/shard_map/dot_general | solution.py:115
  188.1 8.1 %fusion.13 = bf16[128,2048]{1,0:T(8,128)(2,1)} fusion(bf16[2048,2112]{1,0:T(8,128)(2,1)} %all-gather.2.cloned.1.call-done, bf16[128,2048]{0,1:T(8,128)(2,1)S(1)} %copy-done.6, f32[128,704]{0,1:T(8,128)S(1)} %fusion.10), kind=kOutput, calls=%fused_computation.16 | convolution fusion | flops 739000320 | bytes 7700480 | tf_op jit(solution)/shard_map/th,dh->td/dot_general | solution.py:122
  196.2 0.1 mul.133
  196.5 16.2 %all-to-all-done.3 = bf16[64,16,512]{2,1,0:T(8,128)(2,1)S(1)} async-done(((bf16[64,16,512]{2,1,0:T(8,128)(2,1)}), bf16[64,16,512]{2,1,0:T(8,128)(2,1)S(1)}, u32[]{:S(2)}, u32[]{:S(2)}) %all-to-all-start.3) | async-done | bytes 1048608 | tf_op jit(solution)/shard_map/all_to_all | solution.py:107
  212.7 2.7 %gather_fusion = bf16[768,512]{1,0:T(8,128)(2,1)S(1)} fusion(bf16[1024,512]{1,0:T(8,128)(2,1)S(1)} %bitcast.127, s32[1024]{0:T(1024)S(1)} %pad_clamp_fusion), kind=kCustom, calls=%fused_computation | custom fusion | bytes 1575936 | tf_op jit(solution)/shard_map/gather | solution.py:200
  215.4 0.3 reshape.183
  215.7 1.0 fusion.111
  216.6 2.2 reduce-scatter.2.cloned.1.call-done
  218.9 1.6 fusion.75
  (79 shorter events, 2.2 us)
Async XLA Ops:
  6.5 160.9 %copy-start = (bf16[1,1408,512]{2,1,0:T(8,128)(2,1)S(1)}, bf16[1,1408,512]{2,1,0:T(8,128)(2,1)}, u32[]{:S(2)}) copy-start(bf16[1,1408,512]{2,1,0:T(8,128)(2,1)} %param.30) | copy-start | bytes 4325380
  8.2 3.1 %copy-start.10 = (bf16[128,512]{1,0:T(8,128)(2,1)S(1)}, bf16[128,512]{1,0:T(8,128)(2,1)}, u32[]{:S(2)}) copy-start(bf16[128,512]{1,0:T(8,128)(2,1)} %param.17) | copy-start | bytes 393220
  8.2 3.2 %copy-start.11 = (s32[2,64,64]{2,1,0:T(8,128)S(1)}, s32[2,64,64]{2,1,0:T(8,128)}, u32[]{:S(2)}) copy-start(s32[2,64,64]{2,1,0:T(8,128)} %param.22) | copy-start | bytes 98308
  8.2 3.5 %copy-start.8 = (bf16[128,2,128]{2,1,0:T(2,128)(2,1)S(1)}, bf16[128,2,128]{2,1,0:T(2,128)(2,1)}, u32[]{:S(2)}) copy-start(bf16[128,2,128]{2,1,0:T(2,128)(2,1)} %param.18) | copy-start | bytes 196612
  14.0 3.0 %copy-start.2 = (bf16[40,1,128,128]{3,2,1,0:T(8,128)(2,1)S(1)}, bf16[40,1,128,128]{3,2,1,0:T(8,128)(2,1)}, u32[]{:S(2)}) copy-start(bf16[40,1,128,128]{3,2,1,0:T(8,128)(2,1)} %get-tuple-element.8) | copy-start | bytes 3932164
  26.6 4.4 %copy-start.16 = (s32[128,6]{0,1:T(8,128)S(1)}, s32[128,6]{0,1:T(8,128)}, u32[]{:S(2)}) copy-start(s32[128,6]{0,1:T(8,128)} %param.26) | copy-start | bytes 9220
  26.6 19.5 %all-to-all-start = ((f32[4,128,512]{2,1,0:T(8,128)}), f32[4,128,512]{2,1,0:T(8,128)S(1)}, u32[]{:S(2)}, u32[]{:S(2)}) async-start(f32[4,128,512]{2,1,0:T(8,128)} %convolution_bitcast_fusion), calls=%async_computation | async-start | bytes 2097152 | tf_op jit(solution)/shard_map/all_to_all | solution.py:97
  47.1 1.0 copy-start.3
  47.3 13.2 %copy-start.15 = (f32[2048]{0:T(1024)S(1)}, f32[2048]{0:T(1024)}, u32[]{:S(2)}) copy-start(f32[2048]{0:T(1024)} %param.25) | copy-start | bytes 24580
  48.1 12.0 %all-to-all-start.1 = ((bf16[4,128,512]{1,2,0:T(8,128)(2,1)}), bf16[4,128,512]{1,2,0:T(8,128)(2,1)S(1)}, u32[]{:S(2)}, u32[]{:S(2)}) async-start(bf16[4,128,512]{1,2,0:T(8,128)(2,1)} %broadcast_in_dim.66), calls=%async_computation.1 | async-start | bytes 1048576 | tf_op jit(solution)/shard_map/all_to_all | solution.py:60
  60.8 0.8 copy-start.5
  61.6 13.2 %copy-start.12 = (bf16[32,704]{1,0:T(8,128)(2,1)S(1)}, bf16[32,704]{1,0:T(8,128)(2,1)}, u32[]{:S(2)}) copy-start(bf16[32,704]{1,0:T(8,128)(2,1)} %param.31) | copy-start | bytes 135172
  61.6 13.3 %copy-start.13 = (bf16[32,704]{1,0:T(8,128)(2,1)S(1)}, bf16[32,704]{1,0:T(8,128)(2,1)}, u32[]{:S(2)}) copy-start(bf16[32,704]{1,0:T(8,128)(2,1)} %param.32) | copy-start | bytes 135172
  61.6 13.3 %copy-start.14 = (bf16[704,32]{0,1:T(8,128)(2,1)S(1)}, bf16[704,32]{0,1:T(8,128)(2,1)}, u32[]{:S(2)}) copy-start(bf16[704,32]{0,1:T(8,128)(2,1)} %param.33) | copy-start | bytes 135172
  63.0 39.7 %all-to-all-start.2 = ((bf16[64,16,512]{2,1,0:T(8,128)(2,1)}), bf16[64,16,512]{2,1,0:T(8,128)(2,1)S(1)}, u32[]{:S(2)}, u32[]{:S(2)}) async-start(bf16[64,16,512]{2,1,0:T(8,128)(2,1)} %bitcast.18), calls=%async_computation.2 | async-start | bytes 2097152 | tf_op jit(solution)/shard_map/all_to_all | solution.py:188
  74.8 110.1 %all-gather.2.cloned.1.call-start = ((), (), s32[]{:S(2)}) async-start(), calls=%async_computation.5 | async-start | bytes 9052160 | tf_op jit(solution)/shard_map/all_gather | solution.py:114
  102.7 25.4 %collective-permute-start = (bf16[1024,512]{1,0:T(8,128)(2,1)S(1)}, bf16[1024,512]{1,0:T(8,128)(2,1)S(1)}, u32[]{:S(2)}, u32[]{:S(2)}) collective-permute-start(bf16[1024,512]{1,0:T(8,128)(2,1)S(1)} %bitcast.128), channel_id=1, source_target_pairs={{0,3},{1,0},{2,1},{3,2},{4,7},{5,4},{6,5},{7,6},{8,11},{9,8},{10,9... | collective-permute-start | bytes 3145736 | tf_op jit(solution)/shard_map/ppermute | solution.py:73
  104.0 26.6 %collective-permute-start.2 = (bf16[1024,512]{1,0:T(8,128)(2,1)S(1)}, bf16[1024,512]{1,0:T(8,128)(2,1)}, u32[]{:S(2)}, u32[]{:S(2)}) collective-permute-start(bf16[1024,512]{1,0:T(8,128)(2,1)S(1)} %bitcast.129), channel_id=1, source_target_pairs={{0,1},{1,2},{2,3},{3,0},{4,5},{5,6},{6,7},{7,4},{8,9},{9,10},{10,1... | collective-permute-start | bytes 3145736 | tf_op jit(solution)/shard_map/ppermute | solution.py:72
  104.8 1.7 copy-start.1
  128.1 13.4 %collective-permute-start.1 = (bf16[512,512]{1,0:T(8,128)(2,1)S(1)}, bf16[512,512]{1,0:T(8,128)(2,1)S(1)}, u32[]{:S(2)}, u32[]{:S(2)}) collective-permute-start(bf16[512,512]{1,0:T(8,128)(2,1)S(1)} %slice.58), channel_id=1, source_target_pairs={{0,3},{1,0},{2,1},{3,2},{4,7},{5,4},{6,5},{7,6},{8,11},{9,8},{10,9... | collective-permute-start | bytes 1572872 | tf_op jit(solution)/shard_map/ppermute | solution.py:74
  131.7 2.0 copy-start.7
  131.7 14.4 %collective-permute-start.3 = (bf16[512,512]{1,0:T(8,128)(2,1)S(1)}, bf16[512,512]{1,0:T(8,128)(2,1)S(1)}, u32[]{:S(2)}, u32[]{:S(2)}) collective-permute-start(bf16[512,512]{1,0:T(8,128)(2,1)S(1)} %slice.59), channel_id=1, source_target_pairs={{0,1},{1,2},{2,3},{3,0},{4,5},{5,6},{6,7},{7,4},{8,9},{9,10},{10,1... | collective-permute-start | bytes 1572872 | tf_op jit(solution)/shard_map/ppermute | solution.py:75
  148.4 16.6 %collective-permute-start.4 = (bf16[1024,352]{0,1:T(8,128)(2,1)}, bf16[1024,352]{0,1:T(8,128)(2,1)S(1)}, u32[]{:S(2)}, u32[]{:S(2)}) collective-permute-start(bf16[1024,352]{0,1:T(8,128)(2,1)} %multiply_convert_fusion), channel_id=1, source_target_pairs={{0,3},{1,0},{2,1},{3,2},{4,7},{5,4},{6,5},{7,6},{8,11},{9,8},{10,9... | collective-permute-start | bytes 2162696 | tf_op jit(solution)/shard_map/ppermute | solution.py:73
  148.4 18.2 %collective-permute-start.6 = (bf16[1024,352]{0,1:T(8,128)(2,1)}, bf16[1024,352]{0,1:T(8,128)(2,1)S(1)}, u32[]{:S(2)}, u32[]{:S(2)}) collective-permute-start(bf16[1024,352]{0,1:T(8,128)(2,1)} %multiply_convert_fusion), channel_id=1, source_target_pairs={{0,1},{1,2},{2,3},{3,0},{4,5},{5,6},{6,7},{7,4},{8,9},{9,10},{10,1... | collective-permute-start | bytes 2162696 | tf_op jit(solution)/shard_map/ppermute | solution.py:72
  165.0 7.9 %collective-permute-start.5 = (bf16[512,352]{0,1:T(8,128)(2,1)S(1)}, bf16[512,352]{0,1:T(8,128)(2,1)S(1)}, u32[]{:S(2)}, u32[]{:S(2)}) collective-permute-start(bf16[512,352]{0,1:T(8,128)(2,1)S(1)} %slice.60), channel_id=1, source_target_pairs={{0,3},{1,0},{2,1},{3,2},{4,7},{5,4},{6,5},{7,6},{8,11},{9,8},{10,9... | collective-permute-start | bytes 1081352 | tf_op jit(solution)/shard_map/ppermute | solution.py:74
  166.6 9.3 %collective-permute-start.7 = (bf16[512,352]{0,1:T(8,128)(2,1)S(1)}, bf16[512,352]{0,1:T(8,128)(2,1)S(1)}, u32[]{:S(2)}, u32[]{:S(2)}) collective-permute-start(bf16[512,352]{0,1:T(8,128)(2,1)S(1)} %slice.61), channel_id=1, source_target_pairs={{0,1},{1,2},{2,3},{3,0},{4,5},{5,6},{6,7},{7,4},{8,9},{9,10},{10,1... | collective-permute-start | bytes 1081352 | tf_op jit(solution)/shard_map/ppermute | solution.py:75
  178.4 6.4 %copy-start.6 = (bf16[128,2048]{0,1:T(8,128)(2,1)S(1)}, bf16[128,2048]{0,1:T(8,128)(2,1)}, u32[]{:S(2)}) copy-start(bf16[128,2048]{0,1:T(8,128)(2,1)} %copy-done.5) | copy-start | bytes 1572868
  178.4 34.3 %all-to-all-start.3 = ((bf16[64,16,512]{2,1,0:T(8,128)(2,1)}), bf16[64,16,512]{2,1,0:T(8,128)(2,1)S(1)}, u32[]{:S(2)}, u32[]{:S(2)}) async-start(bf16[64,16,512]{2,1,0:T(8,128)(2,1)} %bitcast.32), calls=%async_computation.4 | async-start | bytes 2097152 | tf_op jit(solution)/shard_map/all_to_all | solution.py:107
  184.8 34.1 %reduce-scatter.2.cloned.1.call-start = ((), (), s32[]{:S(2)}) async-start(), calls=%async_computation.6 | async-start | bytes 655360 | tf_op jit(solution)/shard_map/reduce_scatter | solution.py:128
  188.1 8.1 %copy-start.9 = (s32[128,6]{1,0:T(8,128)S(1)}, s32[128,6]{1,0:T(8,128)}, u32[]{:S(2)}) copy-start(s32[128,6]{1,0:T(8,128)} %get-tuple-element.9) | copy-start | bytes 9220
  188.1 8.2 %copy-start.17 = (f32[128,6]{0,1:T(8,128)S(1)}, f32[128,6]{0,1:T(8,128)}, u32[]{:S(2)}) copy-start(f32[128,6]{0,1:T(8,128)} %param.27) | copy-start | bytes 9220
  215.4 3.5 %copy-start.4 = (bf16[128,512]{1,0:T(8,128)(2,1)S(1)}, bf16[128,512]{1,0:T(8,128)(2,1)}, u32[]{:S(2)}) copy-start(bf16[128,512]{1,0:T(8,128)(2,1)} %copy-done.3) | copy-start | bytes 393220
Sparse Core Ops, SparseCore 0:
  102.8 79.5 all-gather.1
  196.3 22.5 reduce-scatter.1

commit v11 on v10

--- a/solution.py
+++ b/solution.py
@@ -176,7 +176,7 @@
     )
     slot_index = jnp.sum((jnp.cumsum(onehot, axis=0) - onehot) * onehot, axis=1)
     own_residual = lax.dynamic_slice_in_dim(residual_in, col_start, quarter, 1)
-    own_stream = (own_residual.astype(jnp.float32) + scatter_sum_mp(partial_value)).astype(jnp.bfloat16)
+    own_stream = (own_residual.astype(jnp.float32) + scatter_sum_mp(partial_value.astype(jnp.bfloat16))).astype(jnp.bfloat16)
     stream = gather_mp(own_stream, 1)
     normed_rows = normalize(stream, norm_gain)
     codes = (expert_ids * capacity + slot_index).reshape(tok_rows, route_count)

time: 228 us -> 226 us (level)
  waiting for transfers between devices: 116 us -> 109 us
  local copies, waits for them, and re-layouts: 15.2 us -> 20.3 us
  matrix products: 35.9 us -> 32.1 us
    all_to_all x1, waiting for transfers between devices: 12.6 us -> 6.95 us  [scatter_sum_mp(): lax.all_to_all(blocks, 'mp', split_axis=0, concat_axis=0, tiled=True)]
    ppermute x2, waiting for transfers between devices: 7.73 us -> 10.8 us  [ring_blocks_mp(): far_top = lax.ppermute(from_right[:half], 'mp', to_left)]
    dot_general x1 -> x0, local copies, waits for them, and re-layouts: 2.86 us -> none  [on_device(): jnp.dot(attended, out_weight, preferred_element_type=jnp.float32)]
    dot_general x12, matrix products: 14.4 us -> 11.9 us  [blockwise_dot(): term = jnp.dot(piece, rows, preferred_element_type=jnp.float32)]
  transfers between devices with their start and end apart: 14 -> 14, of which waited for: 11 -> 10; matrix products, arithmetic and copies ran while one was open for 16% -> 16% of each run, Pallas kernels for 0% -> 0%
where the time goes in v11:
time: 226 us; the launch traced here: 224 us
  waiting for transfers between devices  109 us (48%)
  starting transfers between devices  35.1 us (16%)
  matrix products  32.1 us (14%)
  local copies, waits for them, and re-layouts  20.3 us (9%)
  between operations  13.9 us (6%)
  other arithmetic  13.1 us (6%)
    ppermute x2, waiting for transfers between devices, ring_blocks_mp(): from_right = lax.ppermute(block, 'mp', to_left)  35.6 us
    all_to_all x1, waiting for transfers between devices, on_device(): lax.all_to_all(buffer, 'dp', split_axis=0, concat_axis=0, tiled=True)  27.1 us
    all_to_all x1, waiting for transfers between devices, run_experts(): lax.all_to_all(outputs, 'dp', split_axis=0, concat_axis=0, tiled=True)  15.6 us
    dot_general x12, matrix products, blockwise_dot(): term = jnp.dot(piece, rows, preferred_element_type=jnp.float32)  11.9 us
    all_to_all x1, starting transfers between devices, on_device(): lax.all_to_all(buffer, 'dp', split_axis=0, concat_axis=0, tiled=True)  11.8 us
    ppermute x2, waiting for transfers between devices, ring_blocks_mp(): far_top = lax.ppermute(from_right[:half], 'mp', to_left)  10.8 us
    dot_general x1, matrix products, shared_experts(): jnp.einsum('th,dh->td', shared_hidden, gathered[:, 2 * hidden_width:], pr...  8.07 us
    all_to_all x1, waiting for transfers between devices, scatter_sum_mp(): lax.all_to_all(blocks, 'mp', split_axis=0, concat_axis=0, tiled=True)  6.95 us
  transfers between devices with their start and end apart: 14, of which 10 were waited for; matrix products, arithmetic and copies ran while one was open for 16% of the time, Pallas kernels for 0%

profile of v11, /device:TPU:32, one launch (start us, length us, event | category | flops | bytes accessed | tf_op | source)
XLA Modules:
  0.0 224.0 jit_solution(2473010214371078458)
XLA Ops:
  6.5 0.6 iota_bitcast_fusion
  7.1 0.8 compare_select_fusion.1
  7.9 0.8 select_reduce_fusion
  8.7 0.7 broadcast_bitcast_fusion
  9.4 3.1 %fusion.110 = (bf16[40,1,128,128]{3,2,1,0:T(8,128)(2,1)S(1)}, bf16[40,1,128,128]{3,2,1,0:T(8,128)(2,1)}) fusion(bf16[40,2,128,128]{3,2,1,0:T(8,128)(2,1)} %param.19), kind=kLoop, calls=%fused_computation.137 | loop fusion | bytes 5242880 | tf_op jit(solution)/shard_map/slice | solution.py:20
  12.5 0.7 reshape.175
  13.2 0.9 copy.42
  14.1 1.5 broadcast_compare_fusion
  15.5 0.8 copy.43
  16.4 0.7 tile.2
  17.1 1.6 eq.79
  18.7 1.0 fusion.111
  19.7 0.8 bitcast_compare_fusion
  20.5 1.8 fusion
  22.6 2.9 %fusion.1 = f32[2,256]{1,0:T(2,128)S(1)} fusion(f32[2,256,5120]{2,1,0:T(8,128)S(1)} %get-tuple-element.14, f32[2,256]{1,0:T(2,128)S(1)} %max.7, pred[2,5120]{1,0:T(4,128)(4,1)S(1)} %bitcast_compare_fusion), kind=kLoop, calls=%fused_computation.4 | loop fusion | flops 13106688 | bytes 10500096 | tf_op jit(solution)/shard_map/reduce_sum | solution.py:45
  25.5 3.0 %fusion.3 = f32[2,256,128]{2,1,0:T(8,128)S(1)} fusion(bf16[5120,128,1]{1,0,2:T(8,128)(2,1)S(1)} %bitcast.140, f32[2,256,5120]{2,1,0:T(8,128)S(1)} %get-tuple-element.14, f32[2,256]{1,0:T(2,128)S(1)} %max.7, pred[2,5120]{1,0:T(4,128)(4,1)S(1)} %bitcast_compare_fusion), kind=kOutput, calls=%fused_computation.6 | convolution fusion | flops 684195840 | bytes 12070912 | tf_op jit(solution)/shard_map/rqk,kd->rqd/dot_general | solution.py:46
  29.0 0.4 convolution_convert_fusion
  29.4 0.8 copy.70
  30.3 4.3 %all-to-all-start = ((bf16[4,128,512]{2,1,0:T(8,128)(2,1)}), bf16[4,128,512]{2,1,0:T(8,128)(2,1)S(1)}, u32[]{:S(2)}, u32[]{:S(2)}) async-start(bf16[4,128,512]{2,1,0:T(8,128)(2,1)} %bitcast.131), calls=%async_computation | async-start | bytes 1048576 | tf_op jit(solution)/shard_map/all_to_all | solution.py:97
  35.0 1.8 reduce-window.6
  37.1 7.0 %all-to-all-done = bf16[4,128,512]{2,1,0:T(8,128)(2,1)S(1)} async-done(((bf16[4,128,512]{2,1,0:T(8,128)(2,1)}), bf16[4,128,512]{2,1,0:T(8,128)(2,1)S(1)}, u32[]{:S(2)}, u32[]{:S(2)}) %all-to-all-start) | async-done | bytes 524320 | tf_op jit(solution)/shard_map/all_to_all | solution.py:97
  44.1 0.9 add_convert_fusion.1
  45.2 0.9 broadcast_in_dim.66
  46.1 3.5 %all-to-all-start.1 = ((bf16[4,128,512]{1,2,0:T(8,128)(2,1)}), bf16[4,128,512]{1,2,0:T(8,128)(2,1)S(1)}, u32[]{:S(2)}, u32[]{:S(2)}) async-start(bf16[4,128,512]{1,2,0:T(8,128)(2,1)} %broadcast_in_dim.66), calls=%async_computation.1 | async-start | bytes 1048576 | tf_op jit(solution)/shard_map/all_to_all | solution.py:60
  49.8 0.6 broadcast_multiply_fusion
  50.5 0.5 fusion.12
  51.0 6.8 %all-to-all-done.1 = bf16[4,128,512]{1,2,0:T(8,128)(2,1)S(1)} async-done(((bf16[4,128,512]{1,2,0:T(8,128)(2,1)}), bf16[4,128,512]{1,2,0:T(8,128)(2,1)S(1)}, u32[]{:S(2)}, u32[]{:S(2)}) %all-to-all-start.1) | async-done | bytes 524320 | tf_op jit(solution)/shard_map/all_to_all | solution.py:60
  58.5 1.4 convolution_convert_fusion.1
  59.9 11.8 %all-to-all-start.2 = ((bf16[64,16,512]{2,1,0:T(8,128)(2,1)}), bf16[64,16,512]{2,1,0:T(8,128)(2,1)S(1)}, u32[]{:S(2)}, u32[]{:S(2)}) async-start(bf16[64,16,512]{2,1,0:T(8,128)(2,1)} %bitcast.16), calls=%async_computation.2 | async-start | bytes 2097152 | tf_op jit(solution)/shard_map/all_to_all | solution.py:188
  71.8 0.8 concatenate.9
  72.5 27.1 %all-to-all-done.2 = bf16[64,16,512]{2,1,0:T(8,128)(2,1)S(1)} async-done(((bf16[64,16,512]{2,1,0:T(8,128)(2,1)}), bf16[64,16,512]{2,1,0:T(8,128)(2,1)S(1)}, u32[]{:S(2)}, u32[]{:S(2)}) %all-to-all-start.2) | async-done | bytes 1048608 | tf_op jit(solution)/shard_map/all_to_all | solution.py:188
  99.6 1.5 collective-permute-start
  101.1 0.8 collective-permute-start.2
  101.9 1.7 fusion.50
  103.6 0.6 fusion.56
  104.2 21.0 %collective-permute-done = bf16[1024,512]{1,0:T(8,128)(2,1)S(1)} collective-permute-done((bf16[1024,512]{1,0:T(8,128)(2,1)S(1)}, bf16[1024,512]{1,0:T(8,128)(2,1)S(1)}, u32[]{:S(2)}, u32[]{:S(2)}) %collective-permute-start) | collective-permute-done | bytes 1048608 | tf_op jit(solution)/shard_map/ppermute | solution.py:73
  125.2 2.5 %collective-permute-start.1 = (bf16[512,512]{1,0:T(8,128)(2,1)S(1)}, bf16[512,512]{1,0:T(8,128)(2,1)S(1)}, u32[]{:S(2)}, u32[]{:S(2)}) collective-permute-start(bf16[512,512]{1,0:T(8,128)(2,1)S(1)} %slice.58), channel_id=1, source_target_pairs={{0,3},{1,0},{2,1},{3,2},{4,7},{5,4},{6,5},{7,6},{8,11},{9,8},{10,9... | collective-permute-start | bytes 1572872 | tf_op jit(solution)/shard_map/ppermute | solution.py:74
  127.9 0.6 fusion.52
  128.5 0.7 copy-done.9
  129.2 0.6 convolution_add_fusion.1
  129.8 0.6 fusion.44
  130.3 0.6 convolution_add_fusion.3
  130.9 7.7 %collective-permute-done.1 = bf16[512,512]{1,0:T(8,128)(2,1)S(1)} collective-permute-done((bf16[512,512]{1,0:T(8,128)(2,1)S(1)}, bf16[512,512]{1,0:T(8,128)(2,1)S(1)}, u32[]{:S(2)}, u32[]{:S(2)}) %collective-permute-start.1) | collective-permute-done | bytes 524320 | tf_op jit(solution)/shard_map/ppermute | solution.py:74
  138.7 3.5 %collective-permute-done.3 = bf16[512,512]{1,0:T(8,128)(2,1)S(1)} collective-permute-done((bf16[512,512]{1,0:T(8,128)(2,1)S(1)}, bf16[512,512]{1,0:T(8,128)(2,1)S(1)}, u32[]{:S(2)}, u32[]{:S(2)}) %collective-permute-start.3) | collective-permute-done | bytes 524320 | tf_op jit(solution)/shard_map/ppermute | solution.py:75
  142.2 0.6 fusion.17
  142.8 1.7 multiply_convert_fusion
  144.7 1.8 collective-permute-start.6
  146.5 14.6 %collective-permute-done.4 = bf16[1024,352]{0,1:T(8,128)(2,1)S(1)} collective-permute-done((bf16[1024,352]{0,1:T(8,128)(2,1)}, bf16[1024,352]{0,1:T(8,128)(2,1)S(1)}, u32[]{:S(2)}, u32[]{:S(2)}) %collective-permute-start.4) | collective-permute-done | bytes 720928 | tf_op jit(solution)/shard_map/ppermute | solution.py:73
  161.1 1.8 collective-permute-start.5
  163.3 1.9 fusion.42
  165.2 0.7 fusion.40
  165.9 3.1 %collective-permute-done.5 = bf16[512,352]{0,1:T(8,128)(2,1)S(1)} collective-permute-done((bf16[512,352]{0,1:T(8,128)(2,1)S(1)}, bf16[512,352]{0,1:T(8,128)(2,1)S(1)}, u32[]{:S(2)}, u32[]{:S(2)}) %collective-permute-start.5) | collective-permute-done | bytes 360480 | tf_op jit(solution)/shard_map/ppermute | solution.py:74
  169.0 3.0 %collective-permute-done.7 = bf16[512,352]{0,1:T(8,128)(2,1)S(1)} collective-permute-done((bf16[512,352]{0,1:T(8,128)(2,1)S(1)}, bf16[512,352]{0,1:T(8,128)(2,1)S(1)}, u32[]{:S(2)}, u32[]{:S(2)}) %collective-permute-start.7) | collective-permute-done | bytes 360480 | tf_op jit(solution)/shard_map/ppermute | solution.py:75
  172.0 0.7 fusion.31
  172.8 1.7 add_convert_fusion
  174.5 6.4 %all-to-all-start.3 = ((bf16[64,16,512]{2,1,0:T(8,128)(2,1)}), bf16[64,16,512]{2,1,0:T(8,128)(2,1)S(1)}, u32[]{:S(2)}, u32[]{:S(2)}) async-start(bf16[64,16,512]{2,1,0:T(8,128)(2,1)} %bitcast.30), calls=%async_computation.4 | async-start | bytes 2097152 | tf_op jit(solution)/shard_map/all_to_all | solution.py:107
  181.0 3.2 %fusion.10 = f32[128,704]{0,1:T(8,128)S(1)} fusion(bf16[128,2048]{0,1:T(8,128)(2,1)S(1)} %copy-done.8, bf16[2048,2112]{1,0:T(8,128)(2,1)} %all-gather.2.cloned.1.call-done), kind=kOutput, calls=%fused_computation.12 | convolution fusion | flops 369098752 | bytes 4030464 | tf_op jit(solution)/shard_map/dot_general | solution.py:115
  184.2 8.1 %fusion.13 = bf16[128,2048]{1,0:T(8,128)(2,1)} fusion(bf16[2048,2112]{1,0:T(8,128)(2,1)} %all-gather.2.cloned.1.call-done, bf16[128,2048]{0,1:T(8,128)(2,1)S(1)} %copy-done.8, f32[128,704]{0,1:T(8,128)S(1)} %fusion.10), kind=kOutput, calls=%fused_computation.16 | convolution fusion | flops 739000320 | bytes 7700480 | tf_op jit(solution)/shard_map/th,dh->td/dot_general | solution.py:122
  192.5 0.7 copy.54
  193.2 15.6 %all-to-all-done.3 = bf16[64,16,512]{2,1,0:T(8,128)(2,1)S(1)} async-done(((bf16[64,16,512]{2,1,0:T(8,128)(2,1)}), bf16[64,16,512]{2,1,0:T(8,128)(2,1)S(1)}, u32[]{:S(2)}, u32[]{:S(2)}) %all-to-all-start.3) | async-done | bytes 1048608 | tf_op jit(solution)/shard_map/all_to_all | solution.py:107
  208.8 3.3 %gather_fusion = bf16[768,512]{1,0:T(8,128)(2,1)} fusion(bf16[1024,512]{1,0:T(8,128)(2,1)S(1)} %bitcast.133, s32[1024]{0:T(1024)S(1)} %pad_clamp_fusion), kind=kCustom, calls=%fused_computation | custom fusion | bytes 1575936 | tf_op jit(solution)/shard_map/gather | solution.py:200
  212.2 1.5 reshape.185
  213.7 1.8 fusion.113
  215.5 1.6 fusion.75
  (80 shorter events, 3.7 us)
Async XLA Ops:
  6.5 22.4 %copy-start = (bf16[512,2048]{1,0:T(8,128)(2,1)S(1)}, bf16[512,2048]{1,0:T(8,128)(2,1)}, u32[]{:S(2)}) copy-start(bf16[512,2048]{1,0:T(8,128)(2,1)} %param.23) | copy-start | bytes 6291460
  9.4 3.1 %copy-start.12 = (bf16[128,512]{1,0:T(8,128)(2,1)S(1)}, bf16[128,512]{1,0:T(8,128)(2,1)}, u32[]{:S(2)}) copy-start(bf16[128,512]{1,0:T(8,128)(2,1)} %param.17) | copy-start | bytes 393220
  20.5 1.8 copy-start.10
  22.6 3.0 %copy-start.4 = (bf16[40,1,128,128]{3,2,1,0:T(8,128)(2,1)S(1)}, bf16[40,1,128,128]{3,2,1,0:T(8,128)(2,1)}, u32[]{:S(2)}) copy-start(bf16[40,1,128,128]{3,2,1,0:T(8,128)(2,1)} %get-tuple-element.8) | copy-start | bytes 3932164
  29.4 5.1 %copy-start.17 = (s32[128,6]{0,1:T(8,128)S(1)}, s32[128,6]{0,1:T(8,128)}, u32[]{:S(2)}) copy-start(s32[128,6]{0,1:T(8,128)} %param.26) | copy-start | bytes 9220
  30.3 13.8 %all-to-all-start = ((bf16[4,128,512]{2,1,0:T(8,128)(2,1)}), bf16[4,128,512]{2,1,0:T(8,128)(2,1)S(1)}, u32[]{:S(2)}, u32[]{:S(2)}) async-start(bf16[4,128,512]{2,1,0:T(8,128)(2,1)} %bitcast.131), calls=%async_computation | async-start | bytes 1048576 | tf_op jit(solution)/shard_map/all_to_all | solution.py:97
  45.0 1.0 copy-start.5
  45.2 12.9 %copy-start.16 = (f32[2048]{0:T(1024)S(1)}, f32[2048]{0:T(1024)}, u32[]{:S(2)}) copy-start(f32[2048]{0:T(1024)} %param.25) | copy-start | bytes 24580
  46.1 11.7 %all-to-all-start.1 = ((bf16[4,128,512]{1,2,0:T(8,128)(2,1)}), bf16[4,128,512]{1,2,0:T(8,128)(2,1)S(1)}, u32[]{:S(2)}, u32[]{:S(2)}) async-start(bf16[4,128,512]{1,2,0:T(8,128)(2,1)} %broadcast_in_dim.66), calls=%async_computation.1 | async-start | bytes 1048576 | tf_op jit(solution)/shard_map/all_to_all | solution.py:60
  58.4 1.5 copy-start.7
  58.4 13.3 %copy-start.13 = (bf16[32,704]{1,0:T(8,128)(2,1)S(1)}, bf16[32,704]{1,0:T(8,128)(2,1)}, u32[]{:S(2)}) copy-start(bf16[32,704]{1,0:T(8,128)(2,1)} %param.31) | copy-start | bytes 135172
  58.4 13.3 %copy-start.14 = (bf16[32,704]{1,0:T(8,128)(2,1)S(1)}, bf16[32,704]{1,0:T(8,128)(2,1)}, u32[]{:S(2)}) copy-start(bf16[32,704]{1,0:T(8,128)(2,1)} %param.32) | copy-start | bytes 135172
  58.5 13.3 %copy-start.15 = (bf16[704,32]{0,1:T(8,128)(2,1)S(1)}, bf16[704,32]{0,1:T(8,128)(2,1)}, u32[]{:S(2)}) copy-start(bf16[704,32]{0,1:T(8,128)(2,1)} %param.33) | copy-start | bytes 135172
  59.9 39.7 %all-to-all-start.2 = ((bf16[64,16,512]{2,1,0:T(8,128)(2,1)}), bf16[64,16,512]{2,1,0:T(8,128)(2,1)S(1)}, u32[]{:S(2)}, u32[]{:S(2)}) async-start(bf16[64,16,512]{2,1,0:T(8,128)(2,1)} %bitcast.16), calls=%async_computation.2 | async-start | bytes 2097152 | tf_op jit(solution)/shard_map/all_to_all | solution.py:188
  71.7 109.3 %all-gather.2.cloned.1.call-start = ((), (), s32[]{:S(2)}) async-start(), calls=%async_computation.5 | async-start | bytes 9052160 | tf_op jit(solution)/shard_map/all_gather | solution.py:114
  99.6 25.6 %collective-permute-start = (bf16[1024,512]{1,0:T(8,128)(2,1)S(1)}, bf16[1024,512]{1,0:T(8,128)(2,1)S(1)}, u32[]{:S(2)}, u32[]{:S(2)}) collective-permute-start(bf16[1024,512]{1,0:T(8,128)(2,1)S(1)} %bitcast.134), channel_id=1, source_target_pairs={{0,3},{1,0},{2,1},{3,2},{4,7},{5,4},{6,5},{7,6},{8,11},{9,8},{10,9... | collective-permute-start | bytes 3145736 | tf_op jit(solution)/shard_map/ppermute | solution.py:73
  101.1 26.6 %collective-permute-start.2 = (bf16[1024,512]{1,0:T(8,128)(2,1)S(1)}, bf16[1024,512]{1,0:T(8,128)(2,1)S(1)}, u32[]{:S(2)}, u32[]{:S(2)}) collective-permute-start(bf16[1024,512]{1,0:T(8,128)(2,1)S(1)} %bitcast.135), channel_id=1, source_target_pairs={{0,1},{1,2},{2,3},{3,0},{4,5},{5,6},{6,7},{7,4},{8,9},{9,10},{10,1... | collective-permute-start | bytes 3145736 | tf_op jit(solution)/shard_map/ppermute | solution.py:72
  101.9 1.7 copy-start.2
  125.2 13.4 %collective-permute-start.1 = (bf16[512,512]{1,0:T(8,128)(2,1)S(1)}, bf16[512,512]{1,0:T(8,128)(2,1)S(1)}, u32[]{:S(2)}, u32[]{:S(2)}) collective-permute-start(bf16[512,512]{1,0:T(8,128)(2,1)S(1)} %slice.58), channel_id=1, source_target_pairs={{0,3},{1,0},{2,1},{3,2},{4,7},{5,4},{6,5},{7,6},{8,11},{9,8},{10,9... | collective-permute-start | bytes 1572872 | tf_op jit(solution)/shard_map/ppermute | solution.py:74
  127.8 1.4 copy-start.9
  127.8 14.4 %collective-permute-start.3 = (bf16[512,512]{1,0:T(8,128)(2,1)S(1)}, bf16[512,512]{1,0:T(8,128)(2,1)S(1)}, u32[]{:S(2)}, u32[]{:S(2)}) collective-permute-start(bf16[512,512]{1,0:T(8,128)(2,1)S(1)} %slice.59), channel_id=1, source_target_pairs={{0,1},{1,2},{2,3},{3,0},{4,5},{5,6},{6,7},{7,4},{8,9},{9,10},{10,1... | collective-permute-start | bytes 1572872 | tf_op jit(solution)/shard_map/ppermute | solution.py:75
  144.5 18.8 %copy-start.3 = (bf16[1,1408,512]{2,1,0:T(8,128)(2,1)S(1)}, bf16[1,1408,512]{2,1,0:T(8,128)(2,1)}, u32[]{:S(2)}) copy-start(bf16[1,1408,512]{2,1,0:T(8,128)(2,1)} %param.30) | copy-start | bytes 4325380
  144.5 16.6 %collective-permute-start.4 = (bf16[1024,352]{0,1:T(8,128)(2,1)}, bf16[1024,352]{0,1:T(8,128)(2,1)S(1)}, u32[]{:S(2)}, u32[]{:S(2)}) collective-permute-start(bf16[1024,352]{0,1:T(8,128)(2,1)} %multiply_convert_fusion), channel_id=1, source_target_pairs={{0,3},{1,0},{2,1},{3,2},{4,7},{5,4},{6,5},{7,6},{8,11},{9,8},{10,9... | collective-permute-start | bytes 2162696 | tf_op jit(solution)/shard_map/ppermute | solution.py:73
  144.7 18.2 %collective-permute-start.6 = (bf16[1024,352]{0,1:T(8,128)(2,1)}, bf16[1024,352]{0,1:T(8,128)(2,1)S(1)}, u32[]{:S(2)}, u32[]{:S(2)}) collective-permute-start(bf16[1024,352]{0,1:T(8,128)(2,1)} %multiply_convert_fusion), channel_id=1, source_target_pairs={{0,1},{1,2},{2,3},{3,0},{4,5},{5,6},{6,7},{7,4},{8,9},{9,10},{10,1... | collective-permute-start | bytes 2162696 | tf_op jit(solution)/shard_map/ppermute | solution.py:72
  161.1 7.9 %collective-permute-start.5 = (bf16[512,352]{0,1:T(8,128)(2,1)S(1)}, bf16[512,352]{0,1:T(8,128)(2,1)S(1)}, u32[]{:S(2)}, u32[]{:S(2)}) collective-permute-start(bf16[512,352]{0,1:T(8,128)(2,1)S(1)} %slice.60), channel_id=1, source_target_pairs={{0,3},{1,0},{2,1},{3,2},{4,7},{5,4},{6,5},{7,6},{8,11},{9,8},{10,9... | collective-permute-start | bytes 1081352 | tf_op jit(solution)/shard_map/ppermute | solution.py:74
  162.9 9.1 %collective-permute-start.7 = (bf16[512,352]{0,1:T(8,128)(2,1)S(1)}, bf16[512,352]{0,1:T(8,128)(2,1)S(1)}, u32[]{:S(2)}, u32[]{:S(2)}) collective-permute-start(bf16[512,352]{0,1:T(8,128)(2,1)S(1)} %slice.61), channel_id=1, source_target_pairs={{0,1},{1,2},{2,3},{3,0},{4,5},{5,6},{6,7},{7,4},{8,9},{9,10},{10,1... | collective-permute-start | bytes 1081352 | tf_op jit(solution)/shard_map/ppermute | solution.py:75
  174.5 6.5 %copy-start.8 = (bf16[128,2048]{0,1:T(8,128)(2,1)S(1)}, bf16[128,2048]{0,1:T(8,128)(2,1)}, u32[]{:S(2)}) copy-start(bf16[128,2048]{0,1:T(8,128)(2,1)} %copy-done.7) | copy-start | bytes 1572868
  174.5 34.3 %all-to-all-start.3 = ((bf16[64,16,512]{2,1,0:T(8,128)(2,1)}), bf16[64,16,512]{2,1,0:T(8,128)(2,1)S(1)}, u32[]{:S(2)}, u32[]{:S(2)}) async-start(bf16[64,16,512]{2,1,0:T(8,128)(2,1)} %bitcast.30), calls=%async_computation.4 | async-start | bytes 2097152 | tf_op jit(solution)/shard_map/all_to_all | solution.py:107
  180.9 34.6 %reduce-scatter.2.cloned.1.call-start = ((), (), s32[]{:S(2)}) async-start(), calls=%async_computation.6 | async-start | bytes 655360 | tf_op jit(solution)/shard_map/reduce_scatter | solution.py:128
  184.2 8.1 %copy-start.11 = (s32[128,6]{1,0:T(8,128)S(1)}, s32[128,6]{1,0:T(8,128)}, u32[]{:S(2)}) copy-start(s32[128,6]{1,0:T(8,128)} %get-tuple-element.9) | copy-start | bytes 9220
  184.2 8.3 %copy-start.18 = (f32[128,6]{0,1:T(8,128)S(1)}, f32[128,6]{0,1:T(8,128)}, u32[]{:S(2)}) copy-start(f32[128,6]{0,1:T(8,128)} %param.27) | copy-start | bytes 9220
  212.2 3.3 %copy-start.6 = (bf16[128,512]{1,0:T(8,128)(2,1)S(1)}, bf16[128,512]{1,0:T(8,128)(2,1)}, u32[]{:S(2)}) copy-start(bf16[128,512]{1,0:T(8,128)(2,1)} %copy-done.5) | copy-start | bytes 393220
  212.2 5.0 %copy-start.1 = (bf16[512,2048]{1,0:T(8,128)(2,1)S(1)}, bf16[512,2048]{1,0:T(8,128)(2,1)}, u32[]{:S(2)}) copy-start(bf16[512,2048]{1,0:T(8,128)(2,1)} %param.23) | copy-start | bytes 6291460
Sparse Core Ops, SparseCore 0:
  99.8 79.5 all-gather.1
  192.4 22.5 reduce-scatter.1

commit v12 on v10

--- a/solution.py
+++ b/solution.py
@@ -177,7 +177,9 @@
     slot_index = jnp.sum((jnp.cumsum(onehot, axis=0) - onehot) * onehot, axis=1)
     own_residual = lax.dynamic_slice_in_dim(residual_in, col_start, quarter, 1)
     own_stream = (own_residual.astype(jnp.float32) + scatter_sum_mp(partial_value)).astype(jnp.bfloat16)
-    stream = gather_mp(own_stream, 1)
+    stream = jnp.roll(
+        jnp.concatenate(ring_blocks_mp(own_stream), axis=1), lax.axis_index("mp") * quarter, axis=1
+    )
     normed_rows = normalize(stream, norm_gain)
     codes = (expert_ids * capacity + slot_index).reshape(tok_rows, route_count)
     slots = jnp.arange(experts * capacity, dtype=jnp.int32)

time: 228 us -> 229 us (level)
  starting transfers between devices: 35.2 us -> 38.1 us
    ppermute x2 -> x3, waiting for transfers between devices: 0.01 us -> 14.9 us  [ring_blocks_mp(): from_left = lax.ppermute(block, 'mp', to_right)]
    ppermute x2 -> x3, waiting for transfers between devices: 35.6 us -> 23.5 us  [ring_blocks_mp(): from_right = lax.ppermute(block, 'mp', to_left)]
    all_to_all x1 -> x0, waiting for transfers between devices: 7.04 us -> none  [gather_mp(): lax.all_to_all(copies, 'mp', split_axis=0, concat_axis=0, tiled=True)]
    all_to_all x1 -> x0, starting transfers between devices: 3.47 us -> none  [gather_mp(): lax.all_to_all(copies, 'mp', split_axis=0, concat_axis=0, tiled=True)]
    ppermute x2 -> x3, starting transfers between devices: 4.07 us -> 7.46 us  [ring_blocks_mp(): far_top = lax.ppermute(from_right[:half], 'mp', to_left)]
    ppermute x2 -> x3, starting transfers between devices: 1.29 us -> 4.56 us  [ring_blocks_mp(): from_right = lax.ppermute(block, 'mp', to_left)]
    ppermute x2 -> x3, waiting for transfers between devices: 7.52 us -> 10.6 us  [ring_blocks_mp(): far_bottom = lax.ppermute(from_left[half:], 'mp', to_right)]
    reduce_scatter x1, waiting for transfers between devices: 2.21 us -> 5.01 us  [shared_experts(): lax.psum_scatter(terms.astype(jnp.bfloat16), 'mp', scatter_dimension=1, t...]
  transfers between devices with their start and end apart: 14 -> 17, of which waited for: 11 -> 12; matrix products, arithmetic and copies ran while one was open for 16% -> 16% of each run, Pallas kernels for 0% -> 0%
where the time goes in v12:
time: 229 us; the launch traced here: 228 us
  waiting for transfers between devices  116 us (51%)
  starting transfers between devices  38.1 us (17%)
  matrix products  35.8 us (16%)
  between operations  14.1 us (6%)
  local copies, waits for them, and re-layouts  13.5 us (6%)
  other arithmetic  10.8 us (5%)
    all_to_all x1, waiting for transfers between devices, on_device(): lax.all_to_all(buffer, 'dp', split_axis=0, concat_axis=0, tiled=True)  27.1 us
    ppermute x3, waiting for transfers between devices, ring_blocks_mp(): from_right = lax.ppermute(block, 'mp', to_left)  23.5 us
    all_to_all x1, waiting for transfers between devices, run_experts(): lax.all_to_all(outputs, 'dp', split_axis=0, concat_axis=0, tiled=True)  16.2 us
    ppermute x3, waiting for transfers between devices, ring_blocks_mp(): from_left = lax.ppermute(block, 'mp', to_right)  14.9 us
    dot_general x12, matrix products, blockwise_dot(): term = jnp.dot(piece, rows, preferred_element_type=jnp.float32)  14.2 us
    all_to_all x1, starting transfers between devices, on_device(): lax.all_to_all(buffer, 'dp', split_axis=0, concat_axis=0, tiled=True)  11.8 us
    all_to_all x1, waiting for transfers between devices, scatter_sum_mp(): lax.all_to_all(blocks, 'mp', split_axis=0, concat_axis=0, tiled=True)  11.6 us
    ppermute x3, waiting for transfers between devices, ring_blocks_mp(): far_bottom = lax.ppermute(from_left[half:], 'mp', to_right)  10.6 us
  transfers between devices with their start and end apart: 17, of which 12 were waited for; matrix products, arithmetic and copies ran while one was open for 16% of the time, Pallas kernels for 0%

profile of v12, /device:TPU:32, one launch (start us, length us, event | category | flops | bytes accessed | tf_op | source)
XLA Modules:
  0.0 228.4 jit_solution(18251558839305720883)
XLA Ops:
  6.5 0.8 compare_select_fusion.1
  7.4 0.8 select_reduce_fusion
  8.2 3.1 %fusion.111 = (bf16[40,1,128,128]{3,2,1,0:T(8,128)(2,1)S(1)}, bf16[40,1,128,128]{3,2,1,0:T(8,128)(2,1)}) fusion(bf16[40,2,128,128]{3,2,1,0:T(8,128)(2,1)} %param.19), kind=kLoop, calls=%fused_computation.143 | loop fusion | bytes 5242880 | tf_op jit(solution)/shard_map/slice | solution.py:20
  11.6 0.2 eq.82
  12.0 1.8 fusion
  13.8 0.2 fusion.113
  14.0 2.9 %fusion.1 = f32[2,256]{1,0:T(2,128)S(1)} fusion(f32[2,256,5120]{2,1,0:T(8,128)S(1)} %get-tuple-element.16, f32[2,256]{1,0:T(2,128)S(1)} %max.7, pred[2,5120]{1,0:T(4,128)(4,1)S(1)} %bitcast_compare_fusion), kind=kLoop, calls=%fused_computation.4 | loop fusion | flops 13106688 | bytes 10500096 | tf_op jit(solution)/shard_map/reduce_sum | solution.py:45
  17.0 3.0 %fusion.3 = f32[2,256,128]{2,1,0:T(8,128)S(1)} fusion(bf16[5120,128,1]{1,0,2:T(8,128)(2,1)S(1)} %bitcast.127, f32[2,256,5120]{2,1,0:T(8,128)S(1)} %get-tuple-element.16, f32[2,256]{1,0:T(2,128)S(1)} %max.7, pred[2,5120]{1,0:T(4,128)(4,1)S(1)} %bitcast_compare_fusion), kind=kOutput, calls=%fused_computation.6 | convolution fusion | flops 684195840 | bytes 12070912 | tf_op jit(solution)/shard_map/rqk,kd->rqd/dot_general | solution.py:46
  20.0 0.2 fusion.27
  20.3 0.7 reshape.190
  21.0 2.9 %copy.46 = bf16[2048,512]{1,0:T(8,128)(2,1)S(1)} copy(bf16[2048,512]{0,1:T(8,128)(2,1)} %bitcast.126) | data formatting | bytes 4194304 | tf_op jit(solution)/shard_map/dot_general | solution.py:166
  23.9 2.7 %convolution_bitcast_fusion = f32[4,128,512]{2,1,0:T(8,128)} fusion(bf16[128,512,1]{1,0,2:T(8,128)(2,1)} %reshape.190, bf16[4,512,512]{2,1,0:T(8,128)(2,1)S(1)} %bitcast.124), kind=kOutput, calls=%fused_computation.26 | convolution fusion | flops 268435456 | bytes 3276800 | tf_op jit(solution)/shard_map/dot_general | solution.py:166
  26.6 4.4 %all-to-all-start = ((f32[4,128,512]{2,1,0:T(8,128)}), f32[4,128,512]{2,1,0:T(8,128)S(1)}, u32[]{:S(2)}, u32[]{:S(2)}) async-start(f32[4,128,512]{2,1,0:T(8,128)} %convolution_bitcast_fusion), calls=%async_computation | async-start | bytes 2097152 | tf_op jit(solution)/shard_map/all_to_all | solution.py:97
  31.5 1.8 reduce-window.6
  33.3 0.3 slice_reduce_fusion
  33.8 0.6 broadcast_multiply_fusion
  34.5 11.6 %all-to-all-done = f32[4,128,512]{2,1,0:T(8,128)S(1)} async-done(((f32[4,128,512]{2,1,0:T(8,128)}), f32[4,128,512]{2,1,0:T(8,128)S(1)}, u32[]{:S(2)}, u32[]{:S(2)}) %all-to-all-start) | async-done | bytes 1048608 | tf_op jit(solution)/shard_map/all_to_all | solution.py:97
  46.2 0.9 constant_dynamic-update-slice_fusion.5
  47.2 1.2 collective-permute-start
  48.4 0.9 collective-permute-start.2
  49.3 0.5 fusion.12
  49.8 2.4 %collective-permute-done = bf16[128,512]{1,0:T(8,128)(2,1)S(1)} collective-permute-done((bf16[128,512]{1,0:T(8,128)(2,1)S(1)}, bf16[128,512]{1,0:T(8,128)(2,1)S(1)}, u32[]{:S(2)}, u32[]{:S(2)}) %collective-permute-start) | collective-permute-done | bytes 131104 | tf_op jit(solution)/shard_map/ppermute | solution.py:73
  52.2 2.4 %collective-permute-start.1 = (bf16[64,512]{1,0:T(8,128)(2,1)S(1)}, bf16[64,512]{1,0:T(8,128)(2,1)S(1)}, u32[]{:S(2)}, u32[]{:S(2)}) collective-permute-start(bf16[64,512]{1,0:T(8,128)(2,1)S(1)} %slice.62), channel_id=1, source_target_pairs={{0,3},{1,0},{2,1},{3,2},{4,7},{5,4},{6,5},{7,6},{8,11},{9,8},{10,9... | collective-permute-start | bytes 196616 | tf_op jit(solution)/shard_map/ppermute | solution.py:74
  54.7 1.8 collective-permute-done.1
  56.5 3.7 %collective-permute-done.3 = bf16[64,512]{1,0:T(8,128)(2,1)S(1)} collective-permute-done((bf16[64,512]{1,0:T(8,128)(2,1)S(1)}, bf16[64,512]{1,0:T(8,128)(2,1)S(1)}, u32[]{:S(2)}, u32[]{:S(2)}) %collective-permute-start.3) | collective-permute-done | bytes 65568 | tf_op jit(solution)/shard_map/ppermute | solution.py:75
  60.3 0.2 fusion.29
  60.5 0.2 fusion.31
  60.7 1.4 convolution_convert_fusion
  62.2 11.8 %all-to-all-start.1 = ((bf16[64,16,512]{2,1,0:T(8,128)(2,1)}), bf16[64,16,512]{2,1,0:T(8,128)(2,1)S(1)}, u32[]{:S(2)}, u32[]{:S(2)}) async-start(bf16[64,16,512]{2,1,0:T(8,128)(2,1)} %bitcast.16), calls=%async_computation.1 | async-start | bytes 2097152 | tf_op jit(solution)/shard_map/all_to_all | solution.py:190
  74.0 0.8 concatenate.20
  74.8 27.1 %all-to-all-done.1 = bf16[64,16,512]{2,1,0:T(8,128)(2,1)S(1)} async-done(((bf16[64,16,512]{2,1,0:T(8,128)(2,1)}), bf16[64,16,512]{2,1,0:T(8,128)(2,1)S(1)}, u32[]{:S(2)}, u32[]{:S(2)}) %all-to-all-start.1) | async-done | bytes 1048608 | tf_op jit(solution)/shard_map/all_to_all | solution.py:190
  102.0 2.0 collective-permute-start.6
  104.0 1.7 fusion.51
  105.7 0.6 fusion.57
  106.3 21.0 %collective-permute-done.4 = bf16[1024,512]{1,0:T(8,128)(2,1)S(1)} collective-permute-done((bf16[1024,512]{1,0:T(8,128)(2,1)S(1)}, bf16[1024,512]{1,0:T(8,128)(2,1)S(1)}, u32[]{:S(2)}, u32[]{:S(2)}) %collective-permute-start.4) | collective-permute-done | bytes 1048608 | tf_op jit(solution)/shard_map/ppermute | solution.py:73
  127.3 1.6 collective-permute-start.5
  128.9 1.1 slice.69
  130.0 0.6 collective-permute-start.7
  130.6 1.8 fusion.53
  132.4 0.6 convolution_add_fusion.1
  133.0 1.8 fusion.45
  134.8 0.6 convolution_add_fusion.3
  135.4 5.4 %collective-permute-done.5 = bf16[512,512]{1,0:T(8,128)(2,1)S(1)} collective-permute-done((bf16[512,512]{1,0:T(8,128)(2,1)S(1)}, bf16[512,512]{1,0:T(8,128)(2,1)S(1)}, u32[]{:S(2)}, u32[]{:S(2)}) %collective-permute-start.5) | collective-permute-done | bytes 524320 | tf_op jit(solution)/shard_map/ppermute | solution.py:74
  140.8 3.9 %collective-permute-done.7 = bf16[512,512]{1,0:T(8,128)(2,1)S(1)} collective-permute-done((bf16[512,512]{1,0:T(8,128)(2,1)S(1)}, bf16[512,512]{1,0:T(8,128)(2,1)S(1)}, u32[]{:S(2)}, u32[]{:S(2)}) %collective-permute-start.7) | collective-permute-done | bytes 524320 | tf_op jit(solution)/shard_map/ppermute | solution.py:75
  144.7 0.6 fusion.17
  145.3 1.6 multiply_convert_fusion
  146.9 3.2 %collective-permute-start.8 = (bf16[1024,352]{0,1:T(8,128)(2,1)}, bf16[1024,352]{0,1:T(8,128)(2,1)S(1)}, u32[]{:S(2)}, u32[]{:S(2)}) collective-permute-start(bf16[1024,352]{0,1:T(8,128)(2,1)} %multiply_convert_fusion), channel_id=1, source_target_pairs={{0,3},{1,0},{2,1},{3,2},{4,7},{5,4},{6,5},{7,6},{8,11},{9,8},{10,9... | collective-permute-start | bytes 2162696 | tf_op jit(solution)/shard_map/ppermute | solution.py:73
  150.1 14.9 %collective-permute-done.10 = bf16[1024,352]{0,1:T(8,128)(2,1)S(1)} collective-permute-done((bf16[1024,352]{0,1:T(8,128)(2,1)}, bf16[1024,352]{0,1:T(8,128)(2,1)S(1)}, u32[]{:S(2)}, u32[]{:S(2)}) %collective-permute-start.10) | collective-permute-done | bytes 720928 | tf_op jit(solution)/shard_map/ppermute | solution.py:72
  165.2 3.5 %collective-permute-start.9 = (bf16[512,352]{0,1:T(8,128)(2,1)S(1)}, bf16[512,352]{0,1:T(8,128)(2,1)S(1)}, u32[]{:S(2)}, u32[]{:S(2)}) collective-permute-start(bf16[512,352]{0,1:T(8,128)(2,1)S(1)} %slice.70), channel_id=1, source_target_pairs={{0,3},{1,0},{2,1},{3,2},{4,7},{5,4},{6,5},{7,6},{8,11},{9,8},{10,9... | collective-permute-start | bytes 1081352 | tf_op jit(solution)/shard_map/ppermute | solution.py:74
  168.7 1.8 fusion.43
  170.6 0.7 fusion.41
  171.3 3.1 %collective-permute-done.11 = bf16[512,352]{0,1:T(8,128)(2,1)S(1)} collective-permute-done((bf16[512,352]{0,1:T(8,128)(2,1)S(1)}, bf16[512,352]{0,1:T(8,128)(2,1)S(1)}, u32[]{:S(2)}, u32[]{:S(2)}) %collective-permute-start.11) | collective-permute-done | bytes 360480 | tf_op jit(solution)/shard_map/ppermute | solution.py:75
  174.4 0.7 fusion.32
  175.1 1.8 add_convert_fusion
  176.9 6.1 %all-to-all-start.2 = ((bf16[64,16,512]{2,1,0:T(8,128)(2,1)}), bf16[64,16,512]{2,1,0:T(8,128)(2,1)S(1)}, u32[]{:S(2)}, u32[]{:S(2)}) async-start(bf16[64,16,512]{2,1,0:T(8,128)(2,1)} %bitcast.30), calls=%async_computation.3 | async-start | bytes 2097152 | tf_op jit(solution)/shard_map/all_to_all | solution.py:107
  183.1 3.2 %fusion.10 = f32[128,704]{0,1:T(8,128)S(1)} fusion(bf16[128,2048]{1,0:T(8,128)(2,1)S(1)} %copy-done.6, bf16[2048,2112]{1,0:T(8,128)(2,1)} %all-gather.2.cloned.1.call-done), kind=kOutput, calls=%fused_computation.12 | convolution fusion | flops 369098752 | bytes 4030464 | tf_op jit(solution)/shard_map/dot_general | solution.py:115
  186.3 8.1 %fusion.13 = bf16[128,2048]{1,0:T(8,128)(2,1)} fusion(bf16[2048,2112]{1,0:T(8,128)(2,1)} %all-gather.2.cloned.1.call-done, bf16[128,2048]{1,0:T(8,128)(2,1)S(1)} %copy-done.6, f32[128,704]{0,1:T(8,128)S(1)} %fusion.10), kind=kOutput, calls=%fused_computation.16 | convolution fusion | flops 739000320 | bytes 7700480 | tf_op jit(solution)/shard_map/th,dh->td/dot_general | solution.py:122
  194.4 0.1 mul.132
  194.7 16.2 %all-to-all-done.2 = bf16[64,16,512]{2,1,0:T(8,128)(2,1)S(1)} async-done(((bf16[64,16,512]{2,1,0:T(8,128)(2,1)}), bf16[64,16,512]{2,1,0:T(8,128)(2,1)S(1)}, u32[]{:S(2)}, u32[]{:S(2)}) %all-to-all-start.2) | async-done | bytes 1048608 | tf_op jit(solution)/shard_map/all_to_all | solution.py:107
  211.0 2.7 %gather_fusion = bf16[768,512]{1,0:T(8,128)(2,1)S(1)} fusion(bf16[1024,512]{1,0:T(8,128)(2,1)S(1)} %bitcast.119, s32[1024]{0:T(1024)S(1)} %pad_clamp_fusion), kind=kCustom, calls=%fused_computation | custom fusion | bytes 1575936 | tf_op jit(solution)/shard_map/gather | solution.py:202
  213.7 0.3 reshape.179
  213.9 1.0 fusion.114
  214.9 5.0 %reduce-scatter.2.cloned.1.call-done = bf16[128,512]{1,0:T(8,128)(2,1)} async-done(((bf16[128,2048]{1,0:T(8,128)(2,1)}), bf16[128,512]{1,0:T(8,128)(2,1)}) %reduce-scatter.2.cloned.1.call-update) | async-done | bytes 131088 | tf_op jit(solution)/shard_map/reduce_scatter | solution.py:128
  219.9 1.6 fusion.76
  (92 shorter events, 2.3 us)
Async XLA Ops:
  6.5 162.2 %copy-start = (bf16[1,1408,512]{2,1,0:T(8,128)(2,1)S(1)}, bf16[1,1408,512]{2,1,0:T(8,128)(2,1)}, u32[]{:S(2)}) copy-start(bf16[1,1408,512]{2,1,0:T(8,128)(2,1)} %param.30) | copy-start | bytes 4325380
  8.2 3.1 %copy-start.10 = (bf16[128,512]{1,0:T(8,128)(2,1)S(1)}, bf16[128,512]{1,0:T(8,128)(2,1)}, u32[]{:S(2)}) copy-start(bf16[128,512]{1,0:T(8,128)(2,1)} %param.17) | copy-start | bytes 393220
  8.2 3.2 %copy-start.11 = (s32[2,64,64]{2,1,0:T(8,128)S(1)}, s32[2,64,64]{2,1,0:T(8,128)}, u32[]{:S(2)}) copy-start(s32[2,64,64]{2,1,0:T(8,128)} %param.22) | copy-start | bytes 98308
  8.2 3.6 %copy-start.8 = (bf16[128,2,128]{2,1,0:T(2,128)(2,1)S(1)}, bf16[128,2,128]{2,1,0:T(2,128)(2,1)}, u32[]{:S(2)}) copy-start(bf16[128,2,128]{2,1,0:T(2,128)(2,1)} %param.18) | copy-start | bytes 196612
  14.0 3.0 %copy-start.2 = (bf16[40,1,128,128]{3,2,1,0:T(8,128)(2,1)S(1)}, bf16[40,1,128,128]{3,2,1,0:T(8,128)(2,1)}, u32[]{:S(2)}) copy-start(bf16[40,1,128,128]{3,2,1,0:T(8,128)(2,1)} %get-tuple-element.10) | copy-start | bytes 3932164
  26.6 4.4 %copy-start.16 = (s32[128,6]{0,1:T(8,128)S(1)}, s32[128,6]{0,1:T(8,128)}, u32[]{:S(2)}) copy-start(s32[128,6]{0,1:T(8,128)} %param.26) | copy-start | bytes 9220
  26.6 19.5 %all-to-all-start = ((f32[4,128,512]{2,1,0:T(8,128)}), f32[4,128,512]{2,1,0:T(8,128)S(1)}, u32[]{:S(2)}, u32[]{:S(2)}) async-start(f32[4,128,512]{2,1,0:T(8,128)} %convolution_bitcast_fusion), calls=%async_computation | async-start | bytes 2097152 | tf_op jit(solution)/shard_map/all_to_all | solution.py:97
  47.1 13.5 %copy-start.3 = (bf16[128,512]{1,0:T(8,128)(2,1)}, bf16[128,512]{1,0:T(8,128)(2,1)S(1)}, u32[]{:S(2)}) copy-start(bf16[128,512]{1,0:T(8,128)(2,1)S(1)} %get-tuple-element.8) | copy-start | bytes 393220
  47.2 13.3 %copy-start.15 = (f32[2048]{0:T(1024)S(1)}, f32[2048]{0:T(1024)}, u32[]{:S(2)}) copy-start(f32[2048]{0:T(1024)} %param.25) | copy-start | bytes 24580
  47.2 5.0 %collective-permute-start = (bf16[128,512]{1,0:T(8,128)(2,1)S(1)}, bf16[128,512]{1,0:T(8,128)(2,1)S(1)}, u32[]{:S(2)}, u32[]{:S(2)}) collective-permute-start(bf16[128,512]{1,0:T(8,128)(2,1)S(1)} %get-tuple-element.8), channel_id=1, source_target_pairs={{0,3},{1,0},{2,1},{3,2},{4,7},{5,4},{6,5},{7,6},{8,11},{9,8},{10,9... | collective-permute-start | bytes 393224 | tf_op jit(solution)/shard_map/ppermute | solution.py:73
  48.4 6.2 %collective-permute-start.2 = (bf16[128,512]{1,0:T(8,128)(2,1)S(1)}, bf16[128,512]{1,0:T(8,128)(2,1)S(1)}, u32[]{:S(2)}, u32[]{:S(2)}) collective-permute-start(bf16[128,512]{1,0:T(8,128)(2,1)S(1)} %get-tuple-element.8), channel_id=1, source_target_pairs={{0,1},{1,2},{2,3},{3,0},{4,5},{5,6},{6,7},{7,4},{8,9},{9,10},{10,1... | collective-permute-start | bytes 393224 | tf_op jit(solution)/shard_map/ppermute | solution.py:72
  52.2 4.3 %collective-permute-start.1 = (bf16[64,512]{1,0:T(8,128)(2,1)S(1)}, bf16[64,512]{1,0:T(8,128)(2,1)S(1)}, u32[]{:S(2)}, u32[]{:S(2)}) collective-permute-start(bf16[64,512]{1,0:T(8,128)(2,1)S(1)} %slice.62), channel_id=1, source_target_pairs={{0,3},{1,0},{2,1},{3,2},{4,7},{5,4},{6,5},{7,6},{8,11},{9,8},{10,9... | collective-permute-start | bytes 196616 | tf_op jit(solution)/shard_map/ppermute | solution.py:74
  54.6 5.6 %collective-permute-start.3 = (bf16[64,512]{1,0:T(8,128)(2,1)S(1)}, bf16[64,512]{1,0:T(8,128)(2,1)S(1)}, u32[]{:S(2)}, u32[]{:S(2)}) collective-permute-start(bf16[64,512]{1,0:T(8,128)(2,1)S(1)} %slice.63), channel_id=1, source_target_pairs={{0,1},{1,2},{2,3},{3,0},{4,5},{5,6},{6,7},{7,4},{8,9},{9,10},{10,1... | collective-permute-start | bytes 196616 | tf_op jit(solution)/shard_map/ppermute | solution.py:75
  60.7 1.5 copy-start.5
  60.7 13.3 %copy-start.12 = (bf16[32,704]{1,0:T(8,128)(2,1)S(1)}, bf16[32,704]{1,0:T(8,128)(2,1)}, u32[]{:S(2)}) copy-start(bf16[32,704]{1,0:T(8,128)(2,1)} %param.31) | copy-start | bytes 135172
  60.7 13.3 %copy-start.13 = (bf16[32,704]{1,0:T(8,128)(2,1)S(1)}, bf16[32,704]{1,0:T(8,128)(2,1)}, u32[]{:S(2)}) copy-start(bf16[32,704]{1,0:T(8,128)(2,1)} %param.32) | copy-start | bytes 135172
  60.7 13.3 %copy-start.14 = (bf16[704,32]{0,1:T(8,128)(2,1)S(1)}, bf16[704,32]{0,1:T(8,128)(2,1)}, u32[]{:S(2)}) copy-start(bf16[704,32]{0,1:T(8,128)(2,1)} %param.33) | copy-start | bytes 135172
  62.2 39.7 %all-to-all-start.1 = ((bf16[64,16,512]{2,1,0:T(8,128)(2,1)}), bf16[64,16,512]{2,1,0:T(8,128)(2,1)S(1)}, u32[]{:S(2)}, u32[]{:S(2)}) async-start(bf16[64,16,512]{2,1,0:T(8,128)(2,1)} %bitcast.16), calls=%async_computation.1 | async-start | bytes 2097152 | tf_op jit(solution)/shard_map/all_to_all | solution.py:190
  73.9 109.2 %all-gather.2.cloned.1.call-start = ((), (), s32[]{:S(2)}) async-start(), calls=%async_computation.4 | async-start | bytes 9052160 | tf_op jit(solution)/shard_map/all_gather | solution.py:114
  101.9 25.4 %collective-permute-start.4 = (bf16[1024,512]{1,0:T(8,128)(2,1)S(1)}, bf16[1024,512]{1,0:T(8,128)(2,1)S(1)}, u32[]{:S(2)}, u32[]{:S(2)}) collective-permute-start(bf16[1024,512]{1,0:T(8,128)(2,1)S(1)} %bitcast.120), channel_id=1, source_target_pairs={{0,3},{1,0},{2,1},{3,2},{4,7},{5,4},{6,5},{7,6},{8,11},{9,8},{10,9... | collective-permute-start | bytes 3145736 | tf_op jit(solution)/shard_map/ppermute | solution.py:73
  102.0 26.9 %collective-permute-start.6 = (bf16[1024,512]{1,0:T(8,128)(2,1)S(1)}, bf16[1024,512]{1,0:T(8,128)(2,1)}, u32[]{:S(2)}, u32[]{:S(2)}) collective-permute-start(bf16[1024,512]{1,0:T(8,128)(2,1)S(1)} %bitcast.121), channel_id=1, source_target_pairs={{0,1},{1,2},{2,3},{3,0},{4,5},{5,6},{6,7},{7,4},{8,9},{9,10},{10,1... | collective-permute-start | bytes 3145736 | tf_op jit(solution)/shard_map/ppermute | solution.py:72
  104.0 1.7 copy-start.1
  127.3 13.4 %collective-permute-start.5 = (bf16[512,512]{1,0:T(8,128)(2,1)S(1)}, bf16[512,512]{1,0:T(8,128)(2,1)S(1)}, u32[]{:S(2)}, u32[]{:S(2)}) collective-permute-start(bf16[512,512]{1,0:T(8,128)(2,1)S(1)} %slice.68), channel_id=1, source_target_pairs={{0,3},{1,0},{2,1},{3,2},{4,7},{5,4},{6,5},{7,6},{8,11},{9,8},{10,9... | collective-permute-start | bytes 1572872 | tf_op jit(solution)/shard_map/ppermute | solution.py:74
  130.0 2.4 %copy-start.7 = (bf16[1,2048,352]{1,2,0:T(8,128)(2,1)S(1)}, bf16[1,2048,352]{1,2,0:T(8,128)(2,1)}, u32[]{:S(2)}) copy-start(bf16[1,2048,352]{1,2,0:T(8,128)(2,1)} %param.29) | copy-start | bytes 4325380
  130.0 14.7 %collective-permute-start.7 = (bf16[512,512]{1,0:T(8,128)(2,1)S(1)}, bf16[512,512]{1,0:T(8,128)(2,1)S(1)}, u32[]{:S(2)}, u32[]{:S(2)}) collective-permute-start(bf16[512,512]{1,0:T(8,128)(2,1)S(1)} %slice.69), channel_id=1, source_target_pairs={{0,1},{1,2},{2,3},{3,0},{4,5},{5,6},{6,7},{7,4},{8,9},{9,10},{10,1... | collective-permute-start | bytes 1572872 | tf_op jit(solution)/shard_map/ppermute | solution.py:75
  146.9 18.1 %collective-permute-start.10 = (bf16[1024,352]{0,1:T(8,128)(2,1)}, bf16[1024,352]{0,1:T(8,128)(2,1)S(1)}, u32[]{:S(2)}, u32[]{:S(2)}) collective-permute-start(bf16[1024,352]{0,1:T(8,128)(2,1)} %multiply_convert_fusion), channel_id=1, source_target_pairs={{0,1},{1,2},{2,3},{3,0},{4,5},{5,6},{6,7},{7,4},{8,9},{9,10},{10,1... | collective-permute-start | bytes 2162696 | tf_op jit(solution)/shard_map/ppermute | solution.py:72
  146.9 18.2 %collective-permute-start.8 = (bf16[1024,352]{0,1:T(8,128)(2,1)}, bf16[1024,352]{0,1:T(8,128)(2,1)S(1)}, u32[]{:S(2)}, u32[]{:S(2)}) collective-permute-start(bf16[1024,352]{0,1:T(8,128)(2,1)} %multiply_convert_fusion), channel_id=1, source_target_pairs={{0,3},{1,0},{2,1},{3,2},{4,7},{5,4},{6,5},{7,6},{8,11},{9,8},{10,9... | collective-permute-start | bytes 2162696 | tf_op jit(solution)/shard_map/ppermute | solution.py:73
  165.1 9.3 %collective-permute-start.11 = (bf16[512,352]{0,1:T(8,128)(2,1)S(1)}, bf16[512,352]{0,1:T(8,128)(2,1)S(1)}, u32[]{:S(2)}, u32[]{:S(2)}) collective-permute-start(bf16[512,352]{0,1:T(8,128)(2,1)S(1)} %slice.71), channel_id=1, source_target_pairs={{0,1},{1,2},{2,3},{3,0},{4,5},{5,6},{6,7},{7,4},{8,9},{9,10},{10,1... | collective-permute-start | bytes 1081352 | tf_op jit(solution)/shard_map/ppermute | solution.py:75
  165.2 9.2 %collective-permute-start.9 = (bf16[512,352]{0,1:T(8,128)(2,1)S(1)}, bf16[512,352]{0,1:T(8,128)(2,1)S(1)}, u32[]{:S(2)}, u32[]{:S(2)}) collective-permute-start(bf16[512,352]{0,1:T(8,128)(2,1)S(1)} %slice.70), channel_id=1, source_target_pairs={{0,3},{1,0},{2,1},{3,2},{4,7},{5,4},{6,5},{7,6},{8,11},{9,8},{10,9... | collective-permute-start | bytes 1081352 | tf_op jit(solution)/shard_map/ppermute | solution.py:74
  176.9 6.2 %copy-start.6 = (bf16[128,2048]{1,0:T(8,128)(2,1)S(1)}, bf16[128,2048]{1,0:T(8,128)(2,1)}, u32[]{:S(2)}) copy-start(bf16[128,2048]{1,0:T(8,128)(2,1)} %copy-done.5) | copy-start | bytes 1572868
  176.9 34.1 %all-to-all-start.2 = ((bf16[64,16,512]{2,1,0:T(8,128)(2,1)}), bf16[64,16,512]{2,1,0:T(8,128)(2,1)S(1)}, u32[]{:S(2)}, u32[]{:S(2)}) async-start(bf16[64,16,512]{2,1,0:T(8,128)(2,1)} %bitcast.30), calls=%async_computation.3 | async-start | bytes 2097152 | tf_op jit(solution)/shard_map/all_to_all | solution.py:107
  183.0 36.9 %reduce-scatter.2.cloned.1.call-start = ((), (), s32[]{:S(2)}) async-start(), calls=%async_computation.5 | async-start | bytes 655360 | tf_op jit(solution)/shard_map/reduce_scatter | solution.py:128
  186.3 8.1 %copy-start.9 = (s32[128,6]{1,0:T(8,128)S(1)}, s32[128,6]{1,0:T(8,128)}, u32[]{:S(2)}) copy-start(s32[128,6]{1,0:T(8,128)} %get-tuple-element.11) | copy-start | bytes 9220
  186.3 8.2 %copy-start.17 = (f32[128,6]{0,1:T(8,128)S(1)}, f32[128,6]{0,1:T(8,128)}, u32[]{:S(2)}) copy-start(f32[128,6]{0,1:T(8,128)} %param.27) | copy-start | bytes 9220
  213.7 6.3 %copy-start.4 = (bf16[128,512]{1,0:T(8,128)(2,1)S(1)}, bf16[128,512]{1,0:T(8,128)(2,1)}, u32[]{:S(2)}) copy-start(bf16[128,512]{1,0:T(8,128)(2,1)} %copy-done.3) | copy-start | bytes 393220
Sparse Core Ops, SparseCore 0:
  102.0 78.9 all-gather.1
  194.5 25.3 reduce-scatter.1

commit v13 on v10

--- a/solution.py
+++ b/solution.py
@@ -196,12 +196,13 @@
     )
     shared_out = shared_experts(normed_rows, shared_gate, shared_up, shared_down, received)
     result_rows = results.reshape(experts * capacity, quarter)
-    picked = (
-        result_rows[expert_ids * capacity + slot_index]
-        .reshape(tok_rows, route_count, quarter)
-        .astype(jnp.float32)
-    )
-    mixture = jnp.einsum("tk,tkc->tc", route_weight, picked, precision=lax.Precision.HIGHEST)
+    mixing = jnp.sum(
+        jnp.where(codes[:, :, None] == slots[None, None, :], route_weight[:, :, None], 0.0), axis=1
+    )
+    mixture = jnp.dot(
+        mixing, result_rows.astype(jnp.float32), precision=lax.Precision.HIGHEST,
+        preferred_element_type=jnp.float32,
+    )
     return (own_stream.astype(jnp.float32) + shared_out.astype(jnp.float32) + mixture).astype(
         jnp.bfloat16
     )

time: 228 us -> 229 us (level)
  waiting for transfers between devices: 116 us -> 120 us
  local copies, waits for them, and re-layouts: 15.2 us -> 12 us
    reduce_scatter x1, waiting for transfers between devices: 2.21 us -> 6.15 us  [shared_experts(): lax.psum_scatter(terms.astype(jnp.bfloat16), 'mp', scatter_dimension=1, t...]
    gather x1 -> x0, local copies, waits for them, and re-layouts: 2.67 us -> none  [on_device(): result_rows[expert_ids * capacity + slot_index]]
  transfers between devices with their start and end apart: 14 -> 14, of which waited for: 11 -> 11; matrix products, arithmetic and copies ran while one was open for 16% -> 14% of each run, Pallas kernels for 0% -> 0%
where the time goes in v13:
time: 229 us; the launch traced here: 228 us
  waiting for transfers between devices  120 us (52%)
  matrix products  37.3 us (16%)
  starting transfers between devices  35.2 us (15%)
  between operations  13.9 us (6%)
  local copies, waits for them, and re-layouts  12 us (5%)
  other arithmetic  9.18 us (4%)
    ppermute x2, waiting for transfers between devices, ring_blocks_mp(): from_right = lax.ppermute(block, 'mp', to_left)  35.6 us
    all_to_all x1, waiting for transfers between devices, on_device(): lax.all_to_all(buffer, 'dp', split_axis=0, concat_axis=0, tiled=True)  27.1 us
    all_to_all x1, waiting for transfers between devices, run_experts(): lax.all_to_all(outputs, 'dp', split_axis=0, concat_axis=0, tiled=True)  16.1 us
    dot_general x12, matrix products, blockwise_dot(): term = jnp.dot(piece, rows, preferred_element_type=jnp.float32)  14.5 us
    all_to_all x1, waiting for transfers between devices, scatter_sum_mp(): lax.all_to_all(blocks, 'mp', split_axis=0, concat_axis=0, tiled=True)  12.6 us
    all_to_all x1, starting transfers between devices, on_device(): lax.all_to_all(buffer, 'dp', split_axis=0, concat_axis=0, tiled=True)  11.8 us
    dot_general x1, matrix products, shared_experts(): jnp.einsum('th,dh->td', shared_hidden, gathered[:, 2 * hidden_width:], pr...  8.06 us
    ppermute x2, waiting for transfers between devices, ring_blocks_mp(): far_top = lax.ppermute(from_right[:half], 'mp', to_left)  7.71 us
  transfers between devices with their start and end apart: 14, of which 11 were waited for; matrix products, arithmetic and copies ran while one was open for 14% of the time, Pallas kernels for 0%

profile of v13, /device:TPU:32, one launch (start us, length us, event | category | flops | bytes accessed | tf_op | source)
XLA Modules:
  0.0 228.0 jit_solution(9848506382997384048)
XLA Ops:
  6.5 0.8 compare_select_fusion
  7.4 0.8 select_reduce_fusion.1
  8.2 3.1 %fusion.106 = (bf16[40,1,128,128]{3,2,1,0:T(8,128)(2,1)S(1)}, bf16[40,1,128,128]{3,2,1,0:T(8,128)(2,1)}) fusion(bf16[40,2,128,128]{3,2,1,0:T(8,128)(2,1)} %param.19), kind=kLoop, calls=%fused_computation.130 | loop fusion | bytes 5242880 | tf_op jit(solution)/shard_map/slice | solution.py:20
  11.6 0.2 eq.92
  12.0 1.8 fusion
  13.8 0.2 fusion.108
  14.0 2.9 %fusion.1 = f32[2,256]{1,0:T(2,128)S(1)} fusion(f32[2,256,5120]{2,1,0:T(8,128)S(1)} %get-tuple-element.12, f32[2,256]{1,0:T(2,128)S(1)} %max.7, pred[2,5120]{1,0:T(4,128)(4,1)S(1)} %bitcast_compare_fusion), kind=kLoop, calls=%fused_computation.3 | loop fusion | flops 13106688 | bytes 10500096 | tf_op jit(solution)/shard_map/reduce_sum | solution.py:45
  17.0 3.0 %fusion.3 = f32[2,256,128]{2,1,0:T(8,128)S(1)} fusion(bf16[5120,128,1]{1,0,2:T(8,128)(2,1)S(1)} %bitcast.130, f32[2,256,5120]{2,1,0:T(8,128)S(1)} %get-tuple-element.12, f32[2,256]{1,0:T(2,128)S(1)} %max.7, pred[2,5120]{1,0:T(4,128)(4,1)S(1)} %bitcast_compare_fusion), kind=kOutput, calls=%fused_computation.5 | convolution fusion | flops 684195840 | bytes 12070912 | tf_op jit(solution)/shard_map/rqk,kd->rqd/dot_general | solution.py:46
  20.0 0.2 fusion.27
  20.3 0.7 reshape.162
  21.0 2.9 %copy.63 = bf16[2048,512]{1,0:T(8,128)(2,1)S(1)} copy(bf16[2048,512]{0,1:T(8,128)(2,1)} %bitcast.129) | data formatting | bytes 4194304 | tf_op jit(solution)/shard_map/dot_general | solution.py:166
  23.9 2.7 %convolution_bitcast_fusion = f32[4,128,512]{2,1,0:T(8,128)} fusion(bf16[128,512,1]{1,0,2:T(8,128)(2,1)} %reshape.162, bf16[4,512,512]{2,1,0:T(8,128)(2,1)S(1)} %bitcast.126), kind=kOutput, calls=%fused_computation.27 | convolution fusion | flops 268435456 | bytes 3276800 | tf_op jit(solution)/shard_map/dot_general | solution.py:166
  26.6 4.4 %all-to-all-start = ((f32[4,128,512]{2,1,0:T(8,128)}), f32[4,128,512]{2,1,0:T(8,128)S(1)}, u32[]{:S(2)}, u32[]{:S(2)}) async-start(f32[4,128,512]{2,1,0:T(8,128)} %convolution_bitcast_fusion), calls=%async_computation | async-start | bytes 2097152 | tf_op jit(solution)/shard_map/all_to_all | solution.py:97
  31.1 0.1 eq.97
  31.3 0.1 eq.93
  31.4 1.8 reduce-window.6
  33.2 0.3 slice_reduce_fusion
  33.5 12.6 %all-to-all-done = f32[4,128,512]{2,1,0:T(8,128)S(1)} async-done(((f32[4,128,512]{2,1,0:T(8,128)}), f32[4,128,512]{2,1,0:T(8,128)S(1)}, u32[]{:S(2)}, u32[]{:S(2)}) %all-to-all-start) | async-done | bytes 1048608 | tf_op jit(solution)/shard_map/all_to_all | solution.py:97
  46.2 0.9 add_convert_fusion.1
  47.3 0.9 broadcast_in_dim.79
  48.1 3.5 %all-to-all-start.1 = ((bf16[4,128,512]{1,2,0:T(8,128)(2,1)}), bf16[4,128,512]{1,2,0:T(8,128)(2,1)S(1)}, u32[]{:S(2)}, u32[]{:S(2)}) async-start(bf16[4,128,512]{1,2,0:T(8,128)(2,1)} %broadcast_in_dim.79), calls=%async_computation.1 | async-start | bytes 1048576 | tf_op jit(solution)/shard_map/all_to_all | solution.py:60
  51.6 0.1 fusion.78
  51.8 0.1 reduce_sum.71
  52.0 0.5 fusion.12
  52.5 7.7 %all-to-all-done.1 = bf16[4,128,512]{1,2,0:T(8,128)(2,1)S(1)} async-done(((bf16[4,128,512]{1,2,0:T(8,128)(2,1)}), bf16[4,128,512]{1,2,0:T(8,128)(2,1)S(1)}, u32[]{:S(2)}, u32[]{:S(2)}) %all-to-all-start.1) | async-done | bytes 524320 | tf_op jit(solution)/shard_map/all_to_all | solution.py:60
  60.2 0.3 multiply_reduce_fusion
  60.5 0.3 fusion.31
  60.8 0.8 copy-done.5
  61.6 1.4 convolution_convert_fusion
  63.0 11.8 %all-to-all-start.2 = ((bf16[64,16,512]{2,1,0:T(8,128)(2,1)}), bf16[64,16,512]{2,1,0:T(8,128)(2,1)S(1)}, u32[]{:S(2)}, u32[]{:S(2)}) async-start(bf16[64,16,512]{2,1,0:T(8,128)(2,1)} %bitcast.18), calls=%async_computation.2 | async-start | bytes 2097152 | tf_op jit(solution)/shard_map/all_to_all | solution.py:188
  74.9 0.8 concatenate.9
  75.6 27.1 %all-to-all-done.2 = bf16[64,16,512]{2,1,0:T(8,128)(2,1)S(1)} async-done(((bf16[64,16,512]{2,1,0:T(8,128)(2,1)}), bf16[64,16,512]{2,1,0:T(8,128)(2,1)S(1)}, u32[]{:S(2)}, u32[]{:S(2)}) %all-to-all-start.2) | async-done | bytes 1048608 | tf_op jit(solution)/shard_map/all_to_all | solution.py:188
  102.7 1.3 collective-permute-start
  104.0 0.8 collective-permute-start.2
  104.8 1.7 fusion.51
  106.5 0.6 fusion.57
  107.1 21.0 %collective-permute-done = bf16[1024,512]{1,0:T(8,128)(2,1)S(1)} collective-permute-done((bf16[1024,512]{1,0:T(8,128)(2,1)S(1)}, bf16[1024,512]{1,0:T(8,128)(2,1)S(1)}, u32[]{:S(2)}, u32[]{:S(2)}) %collective-permute-start) | collective-permute-done | bytes 1048608 | tf_op jit(solution)/shard_map/ppermute | solution.py:73
  128.2 2.5 %collective-permute-start.1 = (bf16[512,512]{1,0:T(8,128)(2,1)S(1)}, bf16[512,512]{1,0:T(8,128)(2,1)S(1)}, u32[]{:S(2)}, u32[]{:S(2)}) collective-permute-start(bf16[512,512]{1,0:T(8,128)(2,1)S(1)} %slice.56), channel_id=1, source_target_pairs={{0,3},{1,0},{2,1},{3,2},{4,7},{5,4},{6,5},{7,6},{8,11},{9,8},{10,9... | collective-permute-start | bytes 1572872 | tf_op jit(solution)/shard_map/ppermute | solution.py:74
  130.7 1.1 slice.57
  131.9 1.9 fusion.53
  133.8 0.6 convolution_add_fusion.1
  134.4 1.8 fusion.45
  136.2 0.6 convolution_add_fusion.3
  136.8 4.8 %collective-permute-done.1 = bf16[512,512]{1,0:T(8,128)(2,1)S(1)} collective-permute-done((bf16[512,512]{1,0:T(8,128)(2,1)S(1)}, bf16[512,512]{1,0:T(8,128)(2,1)S(1)}, u32[]{:S(2)}, u32[]{:S(2)}) %collective-permute-start.1) | collective-permute-done | bytes 524320 | tf_op jit(solution)/shard_map/ppermute | solution.py:74
  141.7 4.5 %collective-permute-done.3 = bf16[512,512]{1,0:T(8,128)(2,1)S(1)} collective-permute-done((bf16[512,512]{1,0:T(8,128)(2,1)S(1)}, bf16[512,512]{1,0:T(8,128)(2,1)S(1)}, u32[]{:S(2)}, u32[]{:S(2)}) %collective-permute-start.3) | collective-permute-done | bytes 524320 | tf_op jit(solution)/shard_map/ppermute | solution.py:75
  146.2 0.6 fusion.17
  146.8 1.7 multiply_convert_fusion
  148.5 2.0 collective-permute-start.6
  150.5 14.6 %collective-permute-done.4 = bf16[1024,352]{0,1:T(8,128)(2,1)S(1)} collective-permute-done((bf16[1024,352]{0,1:T(8,128)(2,1)}, bf16[1024,352]{0,1:T(8,128)(2,1)S(1)}, u32[]{:S(2)}, u32[]{:S(2)}) %collective-permute-start.4) | collective-permute-done | bytes 720928 | tf_op jit(solution)/shard_map/ppermute | solution.py:73
  165.1 1.6 collective-permute-start.5
  166.7 0.8 collective-permute-start.7
  167.5 1.9 fusion.43
  169.4 0.7 fusion.41
  170.1 2.9 %collective-permute-done.5 = bf16[512,352]{0,1:T(8,128)(2,1)S(1)} collective-permute-done((bf16[512,352]{0,1:T(8,128)(2,1)S(1)}, bf16[512,352]{0,1:T(8,128)(2,1)S(1)}, u32[]{:S(2)}, u32[]{:S(2)}) %collective-permute-start.5) | collective-permute-done | bytes 360480 | tf_op jit(solution)/shard_map/ppermute | solution.py:74
  173.0 3.0 %collective-permute-done.7 = bf16[512,352]{0,1:T(8,128)(2,1)S(1)} collective-permute-done((bf16[512,352]{0,1:T(8,128)(2,1)S(1)}, bf16[512,352]{0,1:T(8,128)(2,1)S(1)}, u32[]{:S(2)}, u32[]{:S(2)}) %collective-permute-start.7) | collective-permute-done | bytes 360480 | tf_op jit(solution)/shard_map/ppermute | solution.py:75
  176.0 0.7 fusion.32
  176.8 1.8 add_convert_fusion
  178.6 6.3 %all-to-all-start.3 = ((bf16[64,16,512]{2,1,0:T(8,128)(2,1)}), bf16[64,16,512]{2,1,0:T(8,128)(2,1)S(1)}, u32[]{:S(2)}, u32[]{:S(2)}) async-start(bf16[64,16,512]{2,1,0:T(8,128)(2,1)} %bitcast.32), calls=%async_computation.4 | async-start | bytes 2097152 | tf_op jit(solution)/shard_map/all_to_all | solution.py:107
  185.0 3.2 %fusion.10 = f32[128,704]{0,1:T(8,128)S(1)} fusion(bf16[128,2048]{0,1:T(8,128)(2,1)S(1)} %copy-done.6, bf16[2048,2112]{1,0:T(8,128)(2,1)} %all-gather.2.cloned.1.call-done), kind=kOutput, calls=%fused_computation.11 | convolution fusion | flops 369098752 | bytes 4030464 | tf_op jit(solution)/shard_map/dot_general | solution.py:115
  188.2 8.1 %fusion.13 = bf16[128,2048]{1,0:T(8,128)(2,1)} fusion(bf16[2048,2112]{1,0:T(8,128)(2,1)} %all-gather.2.cloned.1.call-done, bf16[128,2048]{0,1:T(8,128)(2,1)S(1)} %copy-done.6, f32[128,704]{0,1:T(8,128)S(1)} %fusion.10), kind=kOutput, calls=%fused_computation.17 | convolution fusion | flops 739000320 | bytes 7700480 | tf_op jit(solution)/shard_map/th,dh->td/dot_general | solution.py:122
  196.3 0.4 select_reduce_fusion
  196.7 16.1 %all-to-all-done.3 = bf16[64,16,512]{2,1,0:T(8,128)(2,1)S(1)} async-done(((bf16[64,16,512]{2,1,0:T(8,128)(2,1)}), bf16[64,16,512]{2,1,0:T(8,128)(2,1)S(1)}, u32[]{:S(2)}, u32[]{:S(2)}) %all-to-all-start.3) | async-done | bytes 1048608 | tf_op jit(solution)/shard_map/all_to_all | solution.py:107
  212.8 6.2 %reduce-scatter.2.cloned.1.call-done = bf16[128,512]{1,0:T(8,128)(2,1)} async-done(((bf16[128,2048]{1,0:T(8,128)(2,1)}), bf16[128,512]{1,0:T(8,128)(2,1)}) %reduce-scatter.2.cloned.1.call-update) | async-done | bytes 131088 | tf_op jit(solution)/shard_map/reduce_scatter | solution.py:128
  219.0 2.2 fusion.28
  (71 shorter events, 1.5 us)
Async XLA Ops:
  6.5 161.0 %copy-start = (bf16[1,1408,512]{2,1,0:T(8,128)(2,1)S(1)}, bf16[1,1408,512]{2,1,0:T(8,128)(2,1)}, u32[]{:S(2)}) copy-start(bf16[1,1408,512]{2,1,0:T(8,128)(2,1)} %param.30) | copy-start | bytes 4325380
  8.2 3.1 %copy-start.9 = (bf16[128,512]{1,0:T(8,128)(2,1)S(1)}, bf16[128,512]{1,0:T(8,128)(2,1)}, u32[]{:S(2)}) copy-start(bf16[128,512]{1,0:T(8,128)(2,1)} %param.17) | copy-start | bytes 393220
  8.2 3.2 %copy-start.10 = (s32[2,64,64]{2,1,0:T(8,128)S(1)}, s32[2,64,64]{2,1,0:T(8,128)}, u32[]{:S(2)}) copy-start(s32[2,64,64]{2,1,0:T(8,128)} %param.22) | copy-start | bytes 98308
  8.2 3.5 %copy-start.8 = (bf16[128,2,128]{2,1,0:T(2,128)(2,1)S(1)}, bf16[128,2,128]{2,1,0:T(2,128)(2,1)}, u32[]{:S(2)}) copy-start(bf16[128,2,128]{2,1,0:T(2,128)(2,1)} %param.18) | copy-start | bytes 196612
  14.0 3.0 %copy-start.2 = (bf16[40,1,128,128]{3,2,1,0:T(8,128)(2,1)S(1)}, bf16[40,1,128,128]{3,2,1,0:T(8,128)(2,1)}, u32[]{:S(2)}) copy-start(bf16[40,1,128,128]{3,2,1,0:T(8,128)(2,1)} %get-tuple-element.8) | copy-start | bytes 3932164
  26.6 4.4 %copy-start.14 = (s32[128,6]{0,1:T(8,128)S(1)}, s32[128,6]{0,1:T(8,128)}, u32[]{:S(2)}) copy-start(s32[128,6]{0,1:T(8,128)} %param.26) | copy-start | bytes 9220
  26.6 19.5 %all-to-all-start = ((f32[4,128,512]{2,1,0:T(8,128)}), f32[4,128,512]{2,1,0:T(8,128)S(1)}, u32[]{:S(2)}, u32[]{:S(2)}) async-start(f32[4,128,512]{2,1,0:T(8,128)} %convolution_bitcast_fusion), calls=%async_computation | async-start | bytes 2097152 | tf_op jit(solution)/shard_map/all_to_all | solution.py:97
  47.1 1.0 copy-start.3
  47.2 13.3 %copy-start.15 = (f32[2048]{0:T(1024)S(1)}, f32[2048]{0:T(1024)}, u32[]{:S(2)}) copy-start(f32[2048]{0:T(1024)} %param.25) | copy-start | bytes 24580
  48.1 12.0 %all-to-all-start.1 = ((bf16[4,128,512]{1,2,0:T(8,128)(2,1)}), bf16[4,128,512]{1,2,0:T(8,128)(2,1)S(1)}, u32[]{:S(2)}, u32[]{:S(2)}) async-start(bf16[4,128,512]{1,2,0:T(8,128)(2,1)} %broadcast_in_dim.79), calls=%async_computation.1 | async-start | bytes 1048576 | tf_op jit(solution)/shard_map/all_to_all | solution.py:60
  60.8 0.8 copy-start.5
  61.6 13.2 %copy-start.11 = (bf16[32,704]{1,0:T(8,128)(2,1)S(1)}, bf16[32,704]{1,0:T(8,128)(2,1)}, u32[]{:S(2)}) copy-start(bf16[32,704]{1,0:T(8,128)(2,1)} %param.31) | copy-start | bytes 135172
  61.6 13.3 %copy-start.12 = (bf16[32,704]{1,0:T(8,128)(2,1)S(1)}, bf16[32,704]{1,0:T(8,128)(2,1)}, u32[]{:S(2)}) copy-start(bf16[32,704]{1,0:T(8,128)(2,1)} %param.32) | copy-start | bytes 135172
  61.6 13.3 %copy-start.13 = (bf16[704,32]{0,1:T(8,128)(2,1)S(1)}, bf16[704,32]{0,1:T(8,128)(2,1)}, u32[]{:S(2)}) copy-start(bf16[704,32]{0,1:T(8,128)(2,1)} %param.33) | copy-start | bytes 135172
  63.0 39.7 %all-to-all-start.2 = ((bf16[64,16,512]{2,1,0:T(8,128)(2,1)}), bf16[64,16,512]{2,1,0:T(8,128)(2,1)S(1)}, u32[]{:S(2)}, u32[]{:S(2)}) async-start(bf16[64,16,512]{2,1,0:T(8,128)(2,1)} %bitcast.18), calls=%async_computation.2 | async-start | bytes 2097152 | tf_op jit(solution)/shard_map/all_to_all | solution.py:188
  74.8 110.2 %all-gather.2.cloned.1.call-start = ((), (), s32[]{:S(2)}) async-start(), calls=%async_computation.5 | async-start | bytes 9052160 | tf_op jit(solution)/shard_map/all_gather | solution.py:114
  102.7 25.4 %collective-permute-start = (bf16[1024,512]{1,0:T(8,128)(2,1)S(1)}, bf16[1024,512]{1,0:T(8,128)(2,1)S(1)}, u32[]{:S(2)}, u32[]{:S(2)}) collective-permute-start(bf16[1024,512]{1,0:T(8,128)(2,1)S(1)} %bitcast.122), channel_id=1, source_target_pairs={{0,3},{1,0},{2,1},{3,2},{4,7},{5,4},{6,5},{7,6},{8,11},{9,8},{10,9... | collective-permute-start | bytes 3145736 | tf_op jit(solution)/shard_map/ppermute | solution.py:73
  104.0 26.6 %collective-permute-start.2 = (bf16[1024,512]{1,0:T(8,128)(2,1)S(1)}, bf16[1024,512]{1,0:T(8,128)(2,1)}, u32[]{:S(2)}, u32[]{:S(2)}) collective-permute-start(bf16[1024,512]{1,0:T(8,128)(2,1)S(1)} %bitcast.123), channel_id=1, source_target_pairs={{0,1},{1,2},{2,3},{3,0},{4,5},{5,6},{6,7},{7,4},{8,9},{9,10},{10,1... | collective-permute-start | bytes 3145736 | tf_op jit(solution)/shard_map/ppermute | solution.py:72
  104.8 1.7 copy-start.1
  128.2 13.4 %collective-permute-start.1 = (bf16[512,512]{1,0:T(8,128)(2,1)S(1)}, bf16[512,512]{1,0:T(8,128)(2,1)S(1)}, u32[]{:S(2)}, u32[]{:S(2)}) collective-permute-start(bf16[512,512]{1,0:T(8,128)(2,1)S(1)} %slice.56), channel_id=1, source_target_pairs={{0,3},{1,0},{2,1},{3,2},{4,7},{5,4},{6,5},{7,6},{8,11},{9,8},{10,9... | collective-permute-start | bytes 1572872 | tf_op jit(solution)/shard_map/ppermute | solution.py:74
  131.8 2.0 copy-start.7
  131.8 14.4 %collective-permute-start.3 = (bf16[512,512]{1,0:T(8,128)(2,1)S(1)}, bf16[512,512]{1,0:T(8,128)(2,1)S(1)}, u32[]{:S(2)}, u32[]{:S(2)}) collective-permute-start(bf16[512,512]{1,0:T(8,128)(2,1)S(1)} %slice.57), channel_id=1, source_target_pairs={{0,1},{1,2},{2,3},{3,0},{4,5},{5,6},{6,7},{7,4},{8,9},{9,10},{10,1... | collective-permute-start | bytes 1572872 | tf_op jit(solution)/shard_map/ppermute | solution.py:75
  148.5 16.6 %collective-permute-start.4 = (bf16[1024,352]{0,1:T(8,128)(2,1)}, bf16[1024,352]{0,1:T(8,128)(2,1)S(1)}, u32[]{:S(2)}, u32[]{:S(2)}) collective-permute-start(bf16[1024,352]{0,1:T(8,128)(2,1)} %multiply_convert_fusion), channel_id=1, source_target_pairs={{0,3},{1,0},{2,1},{3,2},{4,7},{5,4},{6,5},{7,6},{8,11},{9,8},{10,9... | collective-permute-start | bytes 2162696 | tf_op jit(solution)/shard_map/ppermute | solution.py:73
  148.5 18.2 %collective-permute-start.6 = (bf16[1024,352]{0,1:T(8,128)(2,1)}, bf16[1024,352]{0,1:T(8,128)(2,1)S(1)}, u32[]{:S(2)}, u32[]{:S(2)}) collective-permute-start(bf16[1024,352]{0,1:T(8,128)(2,1)} %multiply_convert_fusion), channel_id=1, source_target_pairs={{0,1},{1,2},{2,3},{3,0},{4,5},{5,6},{6,7},{7,4},{8,9},{9,10},{10,1... | collective-permute-start | bytes 2162696 | tf_op jit(solution)/shard_map/ppermute | solution.py:72
  165.1 7.9 %collective-permute-start.5 = (bf16[512,352]{0,1:T(8,128)(2,1)S(1)}, bf16[512,352]{0,1:T(8,128)(2,1)S(1)}, u32[]{:S(2)}, u32[]{:S(2)}) collective-permute-start(bf16[512,352]{0,1:T(8,128)(2,1)S(1)} %slice.58), channel_id=1, source_target_pairs={{0,3},{1,0},{2,1},{3,2},{4,7},{5,4},{6,5},{7,6},{8,11},{9,8},{10,9... | collective-permute-start | bytes 1081352 | tf_op jit(solution)/shard_map/ppermute | solution.py:74
  166.7 9.3 %collective-permute-start.7 = (bf16[512,352]{0,1:T(8,128)(2,1)S(1)}, bf16[512,352]{0,1:T(8,128)(2,1)S(1)}, u32[]{:S(2)}, u32[]{:S(2)}) collective-permute-start(bf16[512,352]{0,1:T(8,128)(2,1)S(1)} %slice.59), channel_id=1, source_target_pairs={{0,1},{1,2},{2,3},{3,0},{4,5},{5,6},{6,7},{7,4},{8,9},{9,10},{10,1... | collective-permute-start | bytes 1081352 | tf_op jit(solution)/shard_map/ppermute | solution.py:75
  178.6 6.4 %copy-start.6 = (bf16[128,2048]{0,1:T(8,128)(2,1)S(1)}, bf16[128,2048]{0,1:T(8,128)(2,1)}, u32[]{:S(2)}) copy-start(bf16[128,2048]{0,1:T(8,128)(2,1)} %copy-done.5) | copy-start | bytes 1572868
  178.6 34.3 %all-to-all-start.3 = ((bf16[64,16,512]{2,1,0:T(8,128)(2,1)}), bf16[64,16,512]{2,1,0:T(8,128)(2,1)S(1)}, u32[]{:S(2)}, u32[]{:S(2)}) async-start(bf16[64,16,512]{2,1,0:T(8,128)(2,1)} %bitcast.32), calls=%async_computation.4 | async-start | bytes 2097152 | tf_op jit(solution)/shard_map/all_to_all | solution.py:107
  184.9 34.1 %reduce-scatter.2.cloned.1.call-start = ((), (), s32[]{:S(2)}) async-start(), calls=%async_computation.6 | async-start | bytes 655360 | tf_op jit(solution)/shard_map/reduce_scatter | solution.py:128
  188.2 8.1 %copy-start.16 = (f32[128,6]{0,1:T(8,128)S(1)}, f32[128,6]{0,1:T(8,128)}, u32[]{:S(2)}) copy-start(f32[128,6]{0,1:T(8,128)} %param.27) | copy-start | bytes 9220
  188.2 30.8 %copy-start.4 = (bf16[128,512]{1,0:T(8,128)(2,1)S(1)}, bf16[128,512]{1,0:T(8,128)(2,1)}, u32[]{:S(2)}) copy-start(bf16[128,512]{1,0:T(8,128)(2,1)} %copy-done.3) | copy-start | bytes 393220
Sparse Core Ops, SparseCore 0:
  102.9 79.5 all-gather.1
  196.4 22.5 reduce-scatter.1

commit v14 on v10

--- a/solution.py
+++ b/solution.py
@@ -73,21 +73,26 @@
     from_right = lax.ppermute(block, "mp", to_left)
     far_top = lax.ppermute(from_right[:half], "mp", to_left)
     far_bottom = lax.ppermute(from_left[half:], "mp", to_right)
-    far = jnp.concatenate([far_top, far_bottom], axis=0)
-    return [block, from_right, far, from_left]
+    return [
+        (block[:half], block[half:]),
+        (from_right[:half], from_right[half:]),
+        (far_top, far_bottom),
+        (from_left[:half], from_left[half:]),
+    ]
 
 
 def blockwise_dot(blocks, weights):
     parts = lax.axis_size("mp")
     mp_index = lax.axis_index("mp")
-    width = blocks[0].shape[1]
-    total = None
-    for step, piece in enumerate(blocks):
+    width = blocks[0][0].shape[1]
+    totals = [None, None]
+    for step, halves in enumerate(blocks):
         start = ((mp_index + step) % parts) * width
         rows = lax.dynamic_slice_in_dim(weights, start, width, 0)
-        term = jnp.dot(piece, rows, preferred_element_type=jnp.float32)
-        total = term if total is None else total + term
-    return total
+        for side, piece in enumerate(halves):
+            term = jnp.dot(piece, rows, preferred_element_type=jnp.float32)
+            totals[side] = term if totals[side] is None else totals[side] + term
+    return jnp.concatenate(totals, axis=0)
 
 
 def scatter_sum_mp(terms):

time: 228 us -> 228 us (level)
    dot_general x12 -> x24, matrix products: 14.4 us -> 11.8 us  [blockwise_dot(): term = jnp.dot(piece, rows, preferred_element_type=jnp.float32)]
where the time goes in v14:
time: 228 us; the launch traced here: 227 us
  waiting for transfers between devices  114 us (50%)
  starting transfers between devices  36.1 us (16%)
  matrix products  34.3 us (15%)
  local copies, waits for them, and re-layouts  16.1 us (7%)
  between operations  14.1 us (6%)
  other arithmetic  11.9 us (5%)
    ppermute x2, waiting for transfers between devices, ring_blocks_mp(): from_right = lax.ppermute(block, 'mp', to_left)  33.4 us
    all_to_all x1, waiting for transfers between devices, on_device(): lax.all_to_all(buffer, 'dp', split_axis=0, concat_axis=0, tiled=True)  27 us
    all_to_all x1, waiting for transfers between devices, run_experts(): lax.all_to_all(outputs, 'dp', split_axis=0, concat_axis=0, tiled=True)  15.4 us
    all_to_all x1, waiting for transfers between devices, scatter_sum_mp(): lax.all_to_all(blocks, 'mp', split_axis=0, concat_axis=0, tiled=True)  12.6 us
    all_to_all x1, starting transfers between devices, on_device(): lax.all_to_all(buffer, 'dp', split_axis=0, concat_axis=0, tiled=True)  12 us
    dot_general x24, matrix products, blockwise_dot(): term = jnp.dot(piece, rows, preferred_element_type=jnp.float32)  11.8 us
    dot_general x1, matrix products, shared_experts(): jnp.einsum('th,dh->td', shared_hidden, gathered[:, 2 * hidden_width:], pr...  8.16 us
    ppermute x2, waiting for transfers between devices, ring_blocks_mp(): far_top = lax.ppermute(from_right[:half], 'mp', to_left)  8.08 us
  transfers between devices with their start and end apart: 14, of which 11 were waited for; matrix products, arithmetic and copies ran while one was open for 16% of the time, Pallas kernels for 0%

profile of v14, /device:TPU:32, one launch (start us, length us, event | category | flops | bytes accessed | tf_op | source)
XLA Modules:
  0.0 226.6 jit_solution(228933496413665449)
XLA Ops:
  6.5 0.8 compare_select_fusion.1
  7.4 0.8 select_reduce_fusion
  8.2 3.1 %fusion.161 = (bf16[40,1,128,128]{3,2,1,0:T(8,128)(2,1)S(1)}, bf16[40,1,128,128]{3,2,1,0:T(8,128)(2,1)}) fusion(bf16[40,2,128,128]{3,2,1,0:T(8,128)(2,1)} %param.19), kind=kLoop, calls=%fused_computation.197 | loop fusion | bytes 5242880 | tf_op jit(solution)/shard_map/slice | solution.py:20
  12.0 1.8 fusion
  14.0 2.9 %fusion.1 = f32[2,256]{1,0:T(2,128)S(1)} fusion(f32[2,256,5120]{2,1,0:T(8,128)S(1)} %get-tuple-element.16, f32[2,256]{1,0:T(2,128)S(1)} %max.7, pred[2,5120]{1,0:T(4,128)(4,1)S(1)} %bitcast_compare_fusion), kind=kLoop, calls=%fused_computation.4 | loop fusion | flops 13106688 | bytes 10500096 | tf_op jit(solution)/shard_map/reduce_sum | solution.py:45
  17.0 3.0 %fusion.3 = f32[2,256,128]{2,1,0:T(8,128)S(1)} fusion(bf16[5120,128,1]{1,0,2:T(8,128)(2,1)S(1)} %bitcast.156, f32[2,256,5120]{2,1,0:T(8,128)S(1)} %get-tuple-element.16, f32[2,256]{1,0:T(2,128)S(1)} %max.7, pred[2,5120]{1,0:T(4,128)(4,1)S(1)} %bitcast_compare_fusion), kind=kOutput, calls=%fused_computation.6 | convolution fusion | flops 684195840 | bytes 12070912 | tf_op jit(solution)/shard_map/rqk,kd->rqd/dot_general | solution.py:46
  20.3 0.7 reshape.196
  21.0 2.9 %copy.48 = bf16[2048,512]{1,0:T(8,128)(2,1)S(1)} copy(bf16[2048,512]{0,1:T(8,128)(2,1)} %bitcast.155) | data formatting | bytes 4194304 | tf_op jit(solution)/shard_map/dot_general | solution.py:171
  23.9 2.7 %convolution_bitcast_fusion = f32[4,128,512]{2,1,0:T(8,128)} fusion(bf16[128,512,1]{1,0,2:T(8,128)(2,1)} %reshape.196, bf16[4,512,512]{2,1,0:T(8,128)(2,1)S(1)} %bitcast.149), kind=kOutput, calls=%fused_computation.27 | convolution fusion | flops 268435456 | bytes 3276800 | tf_op jit(solution)/shard_map/dot_general | solution.py:171
  26.6 4.4 %all-to-all-start = ((f32[4,128,512]{2,1,0:T(8,128)}), f32[4,128,512]{2,1,0:T(8,128)S(1)}, u32[]{:S(2)}, u32[]{:S(2)}) async-start(f32[4,128,512]{2,1,0:T(8,128)} %convolution_bitcast_fusion), calls=%async_computation | async-start | bytes 2097152 | tf_op jit(solution)/shard_map/all_to_all | solution.py:102
  31.4 1.8 reduce-window.6
  33.5 12.6 %all-to-all-done = f32[4,128,512]{2,1,0:T(8,128)S(1)} async-done(((f32[4,128,512]{2,1,0:T(8,128)}), f32[4,128,512]{2,1,0:T(8,128)S(1)}, u32[]{:S(2)}, u32[]{:S(2)}) %all-to-all-start) | async-done | bytes 1048608 | tf_op jit(solution)/shard_map/all_to_all | solution.py:102
  46.2 0.9 add_convert_fusion
  47.3 0.8 broadcast_in_dim.66
  48.1 3.5 %all-to-all-start.1 = ((bf16[4,128,512]{1,2,0:T(8,128)(2,1)}), bf16[4,128,512]{1,2,0:T(8,128)(2,1)S(1)}, u32[]{:S(2)}, u32[]{:S(2)}) async-start(bf16[4,128,512]{1,2,0:T(8,128)(2,1)} %broadcast_in_dim.66), calls=%async_computation.1 | async-start | bytes 1048576 | tf_op jit(solution)/shard_map/all_to_all | solution.py:60
  52.0 0.5 fusion.12
  52.5 7.7 %all-to-all-done.1 = bf16[4,128,512]{1,2,0:T(8,128)(2,1)S(1)} async-done(((bf16[4,128,512]{1,2,0:T(8,128)(2,1)}), bf16[4,128,512]{1,2,0:T(8,128)(2,1)S(1)}, u32[]{:S(2)}, u32[]{:S(2)}) %all-to-all-start.1) | async-done | bytes 524320 | tf_op jit(solution)/shard_map/all_to_all | solution.py:60
  60.8 1.4 convolution_convert_fusion
  62.3 12.0 %all-to-all-start.2 = ((bf16[64,16,512]{2,1,0:T(8,128)(2,1)}), bf16[64,16,512]{2,1,0:T(8,128)(2,1)}, u32[]{:S(2)}, u32[]{:S(2)}) async-start(bf16[64,16,512]{2,1,0:T(8,128)(2,1)} %bitcast.18), calls=%async_computation.2 | async-start | bytes 2097152 | tf_op jit(solution)/shard_map/all_to_all | solution.py:193
  74.3 0.8 concatenate.13
  75.1 27.0 %all-to-all-done.2 = bf16[64,16,512]{2,1,0:T(8,128)(2,1)} async-done(((bf16[64,16,512]{2,1,0:T(8,128)(2,1)}), bf16[64,16,512]{2,1,0:T(8,128)(2,1)}, u32[]{:S(2)}, u32[]{:S(2)}) %all-to-all-start.2) | async-done | bytes 1048608 | tf_op jit(solution)/shard_map/all_to_all | solution.py:193
  102.2 1.3 collective-permute-start
  103.4 0.8 collective-permute-start.2
  104.3 1.3 fusion.162
  105.6 0.4 fusion.80
  106.3 0.6 copy-done.2
  107.3 0.4 fusion.67
  107.7 20.1 %collective-permute-done = bf16[1024,512]{1,0:T(8,128)(2,1)S(1)} collective-permute-done((bf16[1024,512]{1,0:T(8,128)(2,1)}, bf16[1024,512]{1,0:T(8,128)(2,1)S(1)}, u32[]{:S(2)}, u32[]{:S(2)}) %collective-permute-start) | collective-permute-done | bytes 1048608 | tf_op jit(solution)/shard_map/ppermute | solution.py:73
  127.8 2.5 %collective-permute-start.1 = (bf16[512,512]{1,0:T(8,128)(2,1)S(1)}, bf16[512,512]{1,0:T(8,128)(2,1)S(1)}, u32[]{:S(2)}, u32[]{:S(2)}) collective-permute-start(bf16[512,512]{1,0:T(8,128)(2,1)S(1)} %slice.103), channel_id=1, source_target_pairs={{0,3},{1,0},{2,1},{3,2},{4,7},{5,4},{6,5},{7,6},{8,11},{9,8},{10,9... | collective-permute-start | bytes 1572872 | tf_op jit(solution)/shard_map/ppermute | solution.py:74
  131.6 0.4 convolution_add_fusion.11
  132.0 0.4 convolution_add_fusion.9
  132.4 0.4 convolution_add_fusion.7
  132.8 0.4 fusion.60
  133.2 0.4 convolution_add_fusion.5
  133.6 7.7 %collective-permute-done.1 = bf16[512,512]{1,0:T(8,128)(2,1)S(1)} collective-permute-done((bf16[512,512]{1,0:T(8,128)(2,1)S(1)}, bf16[512,512]{1,0:T(8,128)(2,1)S(1)}, u32[]{:S(2)}, u32[]{:S(2)}) %collective-permute-start.1) | collective-permute-done | bytes 524320 | tf_op jit(solution)/shard_map/ppermute | solution.py:74
  141.6 0.4 fusion.23
  142.0 2.6 %collective-permute-done.3 = bf16[512,512]{1,0:T(8,128)(2,1)S(1)} collective-permute-done((bf16[512,512]{1,0:T(8,128)(2,1)S(1)}, bf16[512,512]{1,0:T(8,128)(2,1)S(1)}, u32[]{:S(2)}, u32[]{:S(2)}) %collective-permute-start.3) | collective-permute-done | bytes 524320 | tf_op jit(solution)/shard_map/ppermute | solution.py:75
  144.7 0.4 fusion.22
  145.1 0.4 fusion.24
  145.5 0.4 fusion.16
  145.9 1.0 collective-permute-start.4
  146.9 1.1 collective-permute-start.6
  148.0 0.5 fusion.49
  148.4 0.5 fusion.45
  148.9 13.4 %collective-permute-done.4 = bf16[1024,352]{0,1:T(8,128)(2,1)S(1)} collective-permute-done((bf16[1024,352]{0,1:T(8,128)(2,1)S(1)}, bf16[1024,352]{0,1:T(8,128)(2,1)S(1)}, u32[]{:S(2)}, u32[]{:S(2)}) %collective-permute-start.4) | collective-permute-done | bytes 720928 | tf_op jit(solution)/shard_map/ppermute | solution.py:73
  162.3 2.5 %collective-permute-start.5 = (bf16[512,352]{0,1:T(8,128)(2,1)S(1)}, bf16[512,352]{0,1:T(8,128)(2,1)S(1)}, u32[]{:S(2)}, u32[]{:S(2)}) collective-permute-start(bf16[512,352]{0,1:T(8,128)(2,1)S(1)} %slice.109), channel_id=1, source_target_pairs={{0,3},{1,0},{2,1},{3,2},{4,7},{5,4},{6,5},{7,6},{8,11},{9,8},{10,9... | collective-permute-start | bytes 1081352 | tf_op jit(solution)/shard_map/ppermute | solution.py:74
  164.8 1.0 slice.113
  166.2 0.5 convolution_add_fusion.3
  166.6 0.5 convolution_add_fusion.1
  167.1 1.4 fusion.47
  168.6 1.5 fusion.51
  170.0 0.4 collective-permute-done.5
  170.4 0.5 fusion.19
  170.9 4.3 %collective-permute-done.7 = bf16[512,352]{0,1:T(8,128)(2,1)S(1)} collective-permute-done((bf16[512,352]{0,1:T(8,128)(2,1)S(1)}, bf16[512,352]{0,1:T(8,128)(2,1)S(1)}, u32[]{:S(2)}, u32[]{:S(2)}) %collective-permute-start.7) | collective-permute-done | bytes 360480 | tf_op jit(solution)/shard_map/ppermute | solution.py:75
  175.1 0.5 fusion.20
  175.6 1.1 pad_maximum_fusion.1
  176.7 6.5 %all-to-all-start.3 = ((bf16[64,16,512]{2,1,0:T(8,128)(2,1)}), bf16[64,16,512]{2,1,0:T(8,128)(2,1)S(1)}, u32[]{:S(2)}, u32[]{:S(2)}) async-start(bf16[64,16,512]{2,1,0:T(8,128)(2,1)} %bitcast.34), calls=%async_computation.4 | async-start | bytes 2097152 | tf_op jit(solution)/shard_map/all_to_all | solution.py:112
  183.3 4.0 %fusion.10 = f32[128,704]{0,1:T(8,128)} fusion(bf16[128,2048]{0,1:T(8,128)(2,1)S(1)} %copy-done.5, bf16[2048,2112]{1,0:T(8,128)(2,1)} %all-gather.2.cloned.1.call-done), kind=kOutput, calls=%fused_computation.12 | convolution fusion | flops 369098752 | bytes 4030464 | tf_op jit(solution)/shard_map/dot_general | solution.py:120
  187.3 8.2 %fusion.13 = bf16[128,2048]{1,0:T(8,128)(2,1)} fusion(bf16[2048,2112]{1,0:T(8,128)(2,1)} %all-gather.2.cloned.1.call-done, bf16[128,2048]{0,1:T(8,128)(2,1)S(1)} %copy-done.5, f32[128,704]{0,1:T(8,128)} %fusion.10), kind=kOutput, calls=%fused_computation.16 | convolution fusion | flops 739000320 | bytes 7700480 | tf_op jit(solution)/shard_map/th,dh->td/dot_general | solution.py:127
  195.8 15.4 %all-to-all-done.3 = bf16[64,16,512]{2,1,0:T(8,128)(2,1)S(1)} async-done(((bf16[64,16,512]{2,1,0:T(8,128)(2,1)}), bf16[64,16,512]{2,1,0:T(8,128)(2,1)S(1)}, u32[]{:S(2)}, u32[]{:S(2)}) %all-to-all-start.3) | async-done | bytes 1048608 | tf_op jit(solution)/shard_map/all_to_all | solution.py:112
  211.2 2.7 %gather_fusion = bf16[768,512]{1,0:T(8,128)(2,1)S(1)} fusion(bf16[1024,512]{1,0:T(8,128)(2,1)S(1)} %bitcast.148, s32[1024]{0:T(1024)S(1)} %pad_clamp_fusion), kind=kCustom, calls=%fused_computation | custom fusion | bytes 1575936 | tf_op jit(solution)/shard_map/gather | solution.py:205
  214.1 1.0 fusion.165
  215.1 3.1 %reduce-scatter.2.cloned.1.call-done = bf16[128,512]{1,0:T(8,128)(2,1)} async-done(((bf16[128,2048]{1,0:T(8,128)(2,1)}), bf16[128,512]{1,0:T(8,128)(2,1)}) %reduce-scatter.2.cloned.1.call-update) | async-done | bytes 131088 | tf_op jit(solution)/shard_map/reduce_scatter | solution.py:133
  218.2 1.6 fusion.111
  (86 shorter events, 6.6 us)
Async XLA Ops:
  6.5 141.4 %copy-start = (bf16[1,1408,512]{2,1,0:T(8,128)(2,1)S(1)}, bf16[1,1408,512]{2,1,0:T(8,128)(2,1)}, u32[]{:S(2)}) copy-start(bf16[1,1408,512]{2,1,0:T(8,128)(2,1)} %param.30) | copy-start | bytes 4325380
  8.2 3.1 %copy-start.7 = (bf16[128,512]{1,0:T(8,128)(2,1)S(1)}, bf16[128,512]{1,0:T(8,128)(2,1)}, u32[]{:S(2)}) copy-start(bf16[128,512]{1,0:T(8,128)(2,1)} %param.17) | copy-start | bytes 393220
  8.2 3.2 %copy-start.8 = (s32[2,64,64]{2,1,0:T(8,128)S(1)}, s32[2,64,64]{2,1,0:T(8,128)}, u32[]{:S(2)}) copy-start(s32[2,64,64]{2,1,0:T(8,128)} %param.22) | copy-start | bytes 98308
  8.2 3.5 %copy-start.6 = (bf16[128,2,128]{2,1,0:T(2,128)(2,1)S(1)}, bf16[128,2,128]{2,1,0:T(2,128)(2,1)}, u32[]{:S(2)}) copy-start(bf16[128,2,128]{2,1,0:T(2,128)(2,1)} %param.18) | copy-start | bytes 196612
  14.0 3.0 %copy-start.3 = (bf16[40,1,128,128]{3,2,1,0:T(8,128)(2,1)S(1)}, bf16[40,1,128,128]{3,2,1,0:T(8,128)(2,1)}, u32[]{:S(2)}) copy-start(bf16[40,1,128,128]{3,2,1,0:T(8,128)(2,1)} %get-tuple-element.8) | copy-start | bytes 3932164
  26.6 4.4 %copy-start.13 = (s32[128,6]{0,1:T(8,128)S(1)}, s32[128,6]{0,1:T(8,128)}, u32[]{:S(2)}) copy-start(s32[128,6]{0,1:T(8,128)} %param.26) | copy-start | bytes 9220
  26.6 19.5 %all-to-all-start = ((f32[4,128,512]{2,1,0:T(8,128)}), f32[4,128,512]{2,1,0:T(8,128)S(1)}, u32[]{:S(2)}, u32[]{:S(2)}) async-start(f32[4,128,512]{2,1,0:T(8,128)} %convolution_bitcast_fusion), calls=%async_computation | async-start | bytes 2097152 | tf_op jit(solution)/shard_map/all_to_all | solution.py:102
  47.3 13.2 %copy-start.12 = (f32[2048]{0:T(1024)S(1)}, f32[2048]{0:T(1024)}, u32[]{:S(2)}) copy-start(f32[2048]{0:T(1024)} %param.25) | copy-start | bytes 24580
  48.1 12.0 %all-to-all-start.1 = ((bf16[4,128,512]{1,2,0:T(8,128)(2,1)}), bf16[4,128,512]{1,2,0:T(8,128)(2,1)S(1)}, u32[]{:S(2)}, u32[]{:S(2)}) async-start(bf16[4,128,512]{1,2,0:T(8,128)(2,1)} %broadcast_in_dim.66), calls=%async_computation.1 | async-start | bytes 1048576 | tf_op jit(solution)/shard_map/all_to_all | solution.py:60
  60.8 1.5 copy-start.4
  60.8 13.5 %copy-start.9 = (bf16[32,704]{1,0:T(8,128)(2,1)S(1)}, bf16[32,704]{1,0:T(8,128)(2,1)}, u32[]{:S(2)}) copy-start(bf16[32,704]{1,0:T(8,128)(2,1)} %param.31) | copy-start | bytes 135172
  60.8 13.5 %copy-start.10 = (bf16[32,704]{1,0:T(8,128)(2,1)S(1)}, bf16[32,704]{1,0:T(8,128)(2,1)}, u32[]{:S(2)}) copy-start(bf16[32,704]{1,0:T(8,128)(2,1)} %param.32) | copy-start | bytes 135172
  60.8 13.5 %copy-start.11 = (bf16[704,32]{0,1:T(8,128)(2,1)S(1)}, bf16[704,32]{0,1:T(8,128)(2,1)}, u32[]{:S(2)}) copy-start(bf16[704,32]{0,1:T(8,128)(2,1)} %param.33) | copy-start | bytes 135172
  62.3 39.8 %all-to-all-start.2 = ((bf16[64,16,512]{2,1,0:T(8,128)(2,1)}), bf16[64,16,512]{2,1,0:T(8,128)(2,1)}, u32[]{:S(2)}, u32[]{:S(2)}) async-start(bf16[64,16,512]{2,1,0:T(8,128)(2,1)} %bitcast.18), calls=%async_computation.2 | async-start | bytes 2097152 | tf_op jit(solution)/shard_map/all_to_all | solution.py:193
  74.2 31.3 %copy-start.1 = (bf16[1,2048,352]{1,2,0:T(8,128)(2,1)S(1)}, bf16[1,2048,352]{1,2,0:T(8,128)(2,1)}, u32[]{:S(2)}) copy-start(bf16[1,2048,352]{1,2,0:T(8,128)(2,1)} %param.28) | copy-start | bytes 4325380
  74.2 109.1 %all-gather.2.cloned.1.call-start = ((), (), s32[]{:S(2)}) async-start(), calls=%async_computation.5 | async-start | bytes 9052160 | tf_op jit(solution)/shard_map/all_gather | solution.py:119
  102.2 25.6 %collective-permute-start = (bf16[1024,512]{1,0:T(8,128)(2,1)}, bf16[1024,512]{1,0:T(8,128)(2,1)S(1)}, u32[]{:S(2)}, u32[]{:S(2)}) collective-permute-start(bf16[1024,512]{1,0:T(8,128)(2,1)} %bitcast.21), channel_id=1, source_target_pairs={{0,3},{1,0},{2,1},{3,2},{4,7},{5,4},{6,5},{7,6},{8,11},{9,8},{10,9... | collective-permute-start | bytes 3145736 | tf_op jit(solution)/shard_map/ppermute | solution.py:73
  103.4 26.9 %collective-permute-start.2 = (bf16[1024,512]{1,0:T(8,128)(2,1)}, bf16[1024,512]{1,0:T(8,128)(2,1)S(1)}, u32[]{:S(2)}, u32[]{:S(2)}) collective-permute-start(bf16[1024,512]{1,0:T(8,128)(2,1)} %bitcast.21), channel_id=1, source_target_pairs={{0,1},{1,2},{2,3},{3,0},{4,5},{5,6},{6,7},{7,4},{8,9},{9,10},{10,1... | collective-permute-start | bytes 3145736 | tf_op jit(solution)/shard_map/ppermute | solution.py:72
  105.5 1.4 copy-start.2
  127.8 13.4 %collective-permute-start.1 = (bf16[512,512]{1,0:T(8,128)(2,1)S(1)}, bf16[512,512]{1,0:T(8,128)(2,1)S(1)}, u32[]{:S(2)}, u32[]{:S(2)}) collective-permute-start(bf16[512,512]{1,0:T(8,128)(2,1)S(1)} %slice.103), channel_id=1, source_target_pairs={{0,3},{1,0},{2,1},{3,2},{4,7},{5,4},{6,5},{7,6},{8,11},{9,8},{10,9... | collective-permute-start | bytes 1572872 | tf_op jit(solution)/shard_map/ppermute | solution.py:74
  130.3 14.3 %collective-permute-start.3 = (bf16[512,512]{1,0:T(8,128)(2,1)S(1)}, bf16[512,512]{1,0:T(8,128)(2,1)S(1)}, u32[]{:S(2)}, u32[]{:S(2)}) collective-permute-start(bf16[512,512]{1,0:T(8,128)(2,1)S(1)} %slice.107), channel_id=1, source_target_pairs={{0,1},{1,2},{2,3},{3,0},{4,5},{5,6},{6,7},{7,4},{8,9},{9,10},{10,1... | collective-permute-start | bytes 1572872 | tf_op jit(solution)/shard_map/ppermute | solution.py:75
  145.9 16.4 %collective-permute-start.4 = (bf16[1024,352]{0,1:T(8,128)(2,1)S(1)}, bf16[1024,352]{0,1:T(8,128)(2,1)S(1)}, u32[]{:S(2)}, u32[]{:S(2)}) collective-permute-start(bf16[1024,352]{0,1:T(8,128)(2,1)S(1)} %fusion.16), channel_id=1, source_target_pairs={{0,3},{1,0},{2,1},{3,2},{4,7},{5,4},{6,5},{7,6},{8,11},{9,8},{10,9... | collective-permute-start | bytes 2162696 | tf_op jit(solution)/shard_map/ppermute | solution.py:73
  146.9 17.9 %collective-permute-start.6 = (bf16[1024,352]{0,1:T(8,128)(2,1)S(1)}, bf16[1024,352]{0,1:T(8,128)(2,1)}, u32[]{:S(2)}, u32[]{:S(2)}) collective-permute-start(bf16[1024,352]{0,1:T(8,128)(2,1)S(1)} %fusion.16), channel_id=1, source_target_pairs={{0,1},{1,2},{2,3},{3,0},{4,5},{5,6},{6,7},{7,4},{8,9},{9,10},{10,1... | collective-permute-start | bytes 2162696 | tf_op jit(solution)/shard_map/ppermute | solution.py:72
  162.3 8.1 %collective-permute-start.5 = (bf16[512,352]{0,1:T(8,128)(2,1)S(1)}, bf16[512,352]{0,1:T(8,128)(2,1)S(1)}, u32[]{:S(2)}, u32[]{:S(2)}) collective-permute-start(bf16[512,352]{0,1:T(8,128)(2,1)S(1)} %slice.109), channel_id=1, source_target_pairs={{0,3},{1,0},{2,1},{3,2},{4,7},{5,4},{6,5},{7,6},{8,11},{9,8},{10,9... | collective-permute-start | bytes 1081352 | tf_op jit(solution)/shard_map/ppermute | solution.py:74
  165.9 9.3 %collective-permute-start.7 = (bf16[512,352]{0,1:T(8,128)(2,1)S(1)}, bf16[512,352]{0,1:T(8,128)(2,1)S(1)}, u32[]{:S(2)}, u32[]{:S(2)}) collective-permute-start(bf16[512,352]{0,1:T(8,128)(2,1)S(1)} %slice.113), channel_id=1, source_target_pairs={{0,1},{1,2},{2,3},{3,0},{4,5},{5,6},{6,7},{7,4},{8,9},{9,10},{10,1... | collective-permute-start | bytes 1081352 | tf_op jit(solution)/shard_map/ppermute | solution.py:75
  176.7 6.6 %copy-start.5 = (bf16[128,2048]{0,1:T(8,128)(2,1)S(1)}, bf16[128,2048]{0,1:T(8,128)(2,1)}, u32[]{:S(2)}) copy-start(bf16[128,2048]{0,1:T(8,128)(2,1)} %copy-done.4) | copy-start | bytes 1572868
  176.7 34.5 %all-to-all-start.3 = ((bf16[64,16,512]{2,1,0:T(8,128)(2,1)}), bf16[64,16,512]{2,1,0:T(8,128)(2,1)S(1)}, u32[]{:S(2)}, u32[]{:S(2)}) async-start(bf16[64,16,512]{2,1,0:T(8,128)(2,1)} %bitcast.34), calls=%async_computation.4 | async-start | bytes 2097152 | tf_op jit(solution)/shard_map/all_to_all | solution.py:112
  183.2 34.9 %reduce-scatter.2.cloned.1.call-start = ((), (), s32[]{:S(2)}) async-start(), calls=%async_computation.6 | async-start | bytes 655360 | tf_op jit(solution)/shard_map/reduce_scatter | solution.py:133
  187.3 8.3 %copy-start.14 = (f32[128,6]{0,1:T(8,128)S(1)}, f32[128,6]{0,1:T(8,128)}, u32[]{:S(2)}) copy-start(f32[128,6]{0,1:T(8,128)} %param.27) | copy-start | bytes 9220
Sparse Core Ops, SparseCore 0:
  102.2 79.5 all-gather.1
  195.6 22.5 reduce-scatter.1
